TPU v7x, 512 devices: a whole 4x8x8 slice. The times are simulated.
512 devices in a mesh: section: 2 (over core), tile: 256 (over z, y, x).
Axes of the slice: x: 4, y: 8, z: 8, core: 2. Of those that a mesh axis runs over, the one named last changes fastest.
Arguments:
- probe: bfloat16 [256, 2, 256], replicated, may hold values from -2.390625 to 2.390625
- kernel: bfloat16 [2, 256, 256], replicated, may hold values from -0.25 to 0.25
- object_slab: bfloat16 [4, 10240, 2, 256], P('section', 'tile'), as said below
- offsets: int32 [256], P('tile'), may hold values from 0 to 10239, as said below
- counts: int32 [256], P('tile'), may hold values from 1 to 1, as said below
- intensity: bfloat16 [256, 256, 256], P('tile'), may hold values from 0.5 to 3
Outputs:
- object_gradient: float32 [4, 10240, 2, 256], P('section', 'tile')
Inputs may be any that keep to these rules, and one draw needn't show every extreme that they name: `object_slab`: real parts lie in 0.7 to 1.2 and imaginary parts in -0.4 to 0.4. offsets[q] - (q) * 40 lies in 0 to 39; it is 0 at the first slot, 39 at the last slot, and 39 at the first slot of some tile index other than 0. `counts`: every entry is 1; each tile index holds exactly one live scan position.
All inputs are finite; a program needn't handle non-finite values.
Results may differ from a plain program's by a relative error of at most 0.015.
Values may be sent and summed in bfloat16 or wider, within the bound.
No kernel may reach another device: no remote copies, remote signals or barrier semaphores. Data moves between devices by JAX's collectives and lax.ppermute only.
A program may use at most 64 MiB of HBM per device.

v0:
```python
import jax
import jax.numpy as jnp
from jax import lax
from jax.sharding import PartitionSpec as P


def shifted(value, axis, steps):
    count = lax.axis_size(axis)
    pairs = [(source, (source + steps) % count) for source in range(count)]
    return lax.ppermute(value, axis, pairs)


def passed_along(shard, axis, by):
    length = lax.axis_size(axis)
    pairs = [(i, i + by) for i in range(length) if 0 <= i + by < length]
    return lax.ppermute(shard, axis, pairs)


def dft_matrix(length):
    points = jnp.arange(length, dtype=jnp.int32)
    product_mod = points[:, None] * points[None, :] % length
    angle = 2.0 * 3.141592653589793 / length * product_mod.astype(jnp.float32)
    scale_fac = 1.0 / jnp.sqrt(jnp.float32(length))
    return jnp.stack((jnp.cos(angle) * scale_fac, -jnp.sin(angle) * scale_fac)).astype(jnp.bfloat16)


def product(form, first, second):
    return jnp.einsum(form, first, second, preferred_element_type=jnp.float32)


def apply_left(matrix, field):
    first_part = product("ij,...jck->...ick", matrix[0], field)
    second_part = product("ij,...jck->...ick", matrix[1], field)
    return jnp.stack(
        (
            first_part[..., 0, :] - second_part[..., 1, :],
            first_part[..., 1, :] + second_part[..., 0, :],
        ),
        axis=-2,
    )


def apply_left_adj(matrix, field):
    first_part = product("ji,...jck->...ick", matrix[0], field)
    second_part = product("ji,...jck->...ick", matrix[1], field)
    return jnp.stack(
        (
            first_part[..., 0, :] + second_part[..., 1, :],
            first_part[..., 1, :] - second_part[..., 0, :],
        ),
        axis=-2,
    )


def apply_right(field, matrix):
    first_part = product("...ick,lk->...icl", field, matrix[0])
    second_part = product("...ick,lk->...icl", field, matrix[1])
    return jnp.stack(
        (
            first_part[..., 0, :] - second_part[..., 1, :],
            second_part[..., 0, :] + first_part[..., 1, :],
        ),
        axis=-2,
    )


def apply_right_conj(field, matrix):
    first_part = product("...ick,kl->...icl", field, matrix[0])
    second_part = product("...ick,kl->...icl", field, matrix[1])
    return jnp.stack(
        (
            first_part[..., 0, :] + second_part[..., 1, :],
            first_part[..., 1, :] - second_part[..., 0, :],
        ),
        axis=-2,
    )


def complex_mul(first, second):
    first = first.astype(jnp.float32)
    second = second.astype(jnp.float32)
    return jnp.stack(
        (
            first[..., 0, :] * second[..., 0, :] - first[..., 1, :] * second[..., 1, :],
            first[..., 0, :] * second[..., 1, :] + first[..., 1, :] * second[..., 0, :],
        ),
        axis=-2,
    )


def conj_mul(first, second):
    first = first.astype(jnp.float32)
    return jnp.stack(
        (
            first[..., 0, :] * second[..., 0, :] + first[..., 1, :] * second[..., 1, :],
            first[..., 0, :] * second[..., 1, :] - first[..., 1, :] * second[..., 0, :],
        ),
        axis=-2,
    )


def accumulate(gradients, starts, buffer_rows):
    slot_count, slice_count, width = (gradients.shape[0], gradients.shape[1], gradients.shape[-1])
    buffer_all = jnp.zeros((buffer_rows, slice_count, 2, width), jnp.float32)
    for slot_at in range(slot_count):
        start_row = starts[slot_at]
        current = lax.dynamic_slice_in_dim(buffer_all, start_row, width, 0)
        placed = jnp.transpose(gradients[slot_at], (1, 0, 2, 3))
        buffer_all = lax.dynamic_update_slice_in_dim(buffer_all, current + placed, start_row, 0)
    return buffer_all


def on_device(probe, kernel, object_slab, offsets, counts, intensity):
    width = probe.shape[0]
    slot_count = offsets.shape[0]
    local_rows = object_slab.shape[1]
    slice_count = object_slab.shape[0]
    sections = lax.axis_size("section")
    section_now = lax.axis_index("section")
    tile_now = lax.axis_index("tile")
    is_last = section_now == sections - 1
    dft_table = dft_matrix(width)
    reach = (local_rows + width - 2) // local_rows + 1
    blocks = [object_slab]
    for step_at in range(1, reach):
        blocks.append(shifted(object_slab, "tile", -step_at))
    window = jnp.concatenate(blocks, axis=1)
    relative = offsets - tile_now * local_rows
    patches = jax.vmap(lambda offset: lax.dynamic_slice_in_dim(window, offset, width, 1))(relative)
    live_slots = jnp.arange(slot_count, dtype=jnp.int32) < counts[0]

    def march(field_now, patches_here):
        incidents = []
        for slice_at in range(slice_count):
            incidents.append(field_now)
            phase = complex_mul(field_now, patches_here[..., slice_at, :, :, :]).astype(
                jnp.bfloat16
            )
            middle = apply_left(kernel, phase).astype(jnp.bfloat16)
            field_now = apply_right(middle, kernel).astype(jnp.bfloat16)
        return (field_now, jnp.stack(incidents, axis=-4))

    def far_adjoint(field_now, measured):
        half_far = apply_left(dft_table, field_now).astype(jnp.bfloat16)
        far = apply_right(half_far, dft_table)
        misfit = far[..., 0, :] ** 2 + far[..., 1, :] ** 2 - measured.astype(jnp.float32)
        grad_far = (far * misfit[..., None, :]).astype(jnp.bfloat16)
        half_back = apply_left_adj(dft_table, grad_far).astype(jnp.bfloat16)
        return apply_right_conj(half_back, dft_table).astype(jnp.bfloat16)

    def retreat(adjoint, patches_here, incidents):
        gradients = []
        for slice_at in reversed(range(slice_count)):
            middle = apply_left_adj(kernel, adjoint).astype(jnp.bfloat16)
            phibar = apply_right_conj(middle, kernel)
            gradients.append(conj_mul(incidents[..., slice_at, :, :, :], phibar))
            adjoint = conj_mul(patches_here[..., slice_at, :, :, :], phibar).astype(jnp.bfloat16)
        return (adjoint, jnp.stack(gradients[::-1], axis=-4))

    stored = jnp.zeros(patches.shape, jnp.bfloat16)
    gradients = jnp.zeros(patches.shape, jnp.float32)
    waves = jnp.broadcast_to(probe, (slot_count,) + probe.shape)
    for section_step in range(sections):
        if section_step > 0:
            waves = passed_along(waves, "section", 1)
        waves, stored = lax.cond(
            section_now == section_step,
            lambda field_in, kept: march(field_in, patches),
            lambda field_in, kept: (field_in, kept),
            waves,
            stored,
        )
    adjoints = lax.cond(
        is_last, lambda field_in: far_adjoint(field_in, intensity), lambda field_in: field_in, waves
    )
    for section_step in reversed(range(sections)):
        if section_step < sections - 1:
            adjoints = passed_along(adjoints, "section", -1)
        adjoints, gradients = lax.cond(
            section_now == section_step,
            lambda field_in, kept: retreat(field_in, patches, stored),
            lambda field_in, kept: (field_in, kept),
            adjoints,
            gradients,
        )
    gradients = gradients * live_slots.astype(jnp.float32)[:, None, None, None, None]
    nearby = accumulate(gradients, relative, reach * local_rows)
    own_rows = nearby[:local_rows]
    for step_at in range(1, reach):
        block_rows = nearby[step_at * local_rows : (step_at + 1) * local_rows]
        own_rows = own_rows + shifted(block_rows.astype(jnp.bfloat16), "tile", step_at).astype(
            block_rows.dtype
        )
    return jnp.transpose(own_rows, (1, 0, 2, 3))


def solution(mesh):
    return jax.shard_map(
        on_device,
        mesh=mesh,
        in_specs=(
            P(),
            P(),
            P("section", "tile", None, None),
            P("tile"),
            P("tile"),
            P("tile", None, None),
        ),
        out_specs=P("section", "tile", None, None),
        check_vma=False,
    )
```

profile of v0, /device:TPU:1, one launch (start us, length us, event | category | flops | bytes accessed | tf_op | source)
XLA Modules:
  0.0 105.9 jit_solution(14436167847313894640)
XLA Ops:
  0.0 16.7 %collective-permute-start = (bf16[2,40,2,256]{3,2,1,0:T(2,128)(2,1)}, bf16[2,40,2,256]{3,2,1,0:T(2,128)(2,1)S(1)}, u32[]{:S(2)}, u32[]{:S(2)}) collective-permute-start(bf16[2,40,2,256]{3,2,1,0:T(2,128)(2,1)} %param.18), channel_id=1, source_target_pairs={{0,255},{1,0},{2,1},{3,2},{4,3},{5,4},{6,5},{7,6},{8,7},{9,8},{10,... | collective-permute-start | bytes 245768 | tf_op jit(solution)/shard_map/ppermute | solution.py:10
  16.7 2.4 %collective-permute-start.1 = (bf16[2,40,2,256]{3,2,1,0:T(2,128)(2,1)}, bf16[2,40,2,256]{3,2,1,0:T(2,128)(2,1)S(1)}, u32[]{:S(2)}, u32[]{:S(2)}) collective-permute-start(bf16[2,40,2,256]{3,2,1,0:T(2,128)(2,1)} %param.18), channel_id=1, source_target_pairs={{0,254},{1,255},{2,0},{3,1},{4,2},{5,3},{6,4},{7,5},{8,6},{9,7},{1... | collective-permute-start | bytes 245768 | tf_op jit(solution)/shard_map/ppermute | solution.py:10
  19.2 3.3 %collective-permute-start.2 = (bf16[2,40,2,256]{3,2,1,0:T(2,128)(2,1)}, bf16[2,40,2,256]{3,2,1,0:T(2,128)(2,1)S(1)}, u32[]{:S(2)}, u32[]{:S(2)}) collective-permute-start(bf16[2,40,2,256]{3,2,1,0:T(2,128)(2,1)} %param.18), channel_id=1, source_target_pairs={{0,253},{1,254},{2,255},{3,0},{4,1},{5,2},{6,3},{7,4},{8,5},{9,6},... | collective-permute-start | bytes 245768 | tf_op jit(solution)/shard_map/ppermute | solution.py:10
  22.5 3.0 %collective-permute-start.3 = (bf16[2,40,2,256]{3,2,1,0:T(2,128)(2,1)}, bf16[2,40,2,256]{3,2,1,0:T(2,128)(2,1)S(1)}, u32[]{:S(2)}, u32[]{:S(2)}) collective-permute-start(bf16[2,40,2,256]{3,2,1,0:T(2,128)(2,1)} %param.18), channel_id=1, source_target_pairs={{0,252},{1,253},{2,254},{3,255},{4,0},{5,1},{6,2},{7,3},{8,4},{9,5... | collective-permute-start | bytes 245768 | tf_op jit(solution)/shard_map/ppermute | solution.py:10
  25.5 4.8 %collective-permute-start.4 = (bf16[2,40,2,256]{3,2,1,0:T(2,128)(2,1)}, bf16[2,40,2,256]{3,2,1,0:T(2,128)(2,1)S(1)}, u32[]{:S(2)}, u32[]{:S(2)}) collective-permute-start(bf16[2,40,2,256]{3,2,1,0:T(2,128)(2,1)} %param.18), channel_id=1, source_target_pairs={{0,251},{1,252},{2,253},{3,254},{4,255},{5,0},{6,1},{7,2},{8,3},{9... | collective-permute-start | bytes 245768 | tf_op jit(solution)/shard_map/ppermute | solution.py:10
  30.2 1.1 %copy.44 = bf16[256,2,256]{0,2,1:T(8,128)(2,1)S(1)} copy(bf16[256,2,256]{2,1,0:T(2,128)(2,1)} %param.16) | data formatting | bytes 524288 | tf_op args[0]
  31.4 1.0 copy.97
  33.0 0.9 constant_dynamic-update-slice_fusion.7
  34.0 2.9 %collective-permute-start.5 = (bf16[2,40,2,256]{3,2,1,0:T(2,128)(2,1)}, bf16[2,40,2,256]{3,2,1,0:T(2,128)(2,1)S(1)}, u32[]{:S(2)}, u32[]{:S(2)}) collective-permute-start(bf16[2,40,2,256]{3,2,1,0:T(2,128)(2,1)} %param.18), channel_id=1, source_target_pairs={{0,250},{1,251},{2,252},{3,253},{4,254},{5,255},{6,0},{7,1},{8,2},... | collective-permute-start | bytes 245768 | tf_op jit(solution)/shard_map/ppermute | solution.py:10
  37.0 1.9 %collective-permute-start.6 = (bf16[2,40,2,256]{3,2,1,0:T(2,128)(2,1)S(1)}, bf16[2,40,2,256]{3,2,1,0:T(2,128)(2,1)S(1)}, u32[]{:S(2)}, u32[]{:S(2)}) collective-permute-start(bf16[2,40,2,256]{3,2,1,0:T(2,128)(2,1)S(1)} %copy-done.3), channel_id=1, source_target_pairs={{0,249},{1,250},{2,251},{3,252},{4,253},{5,254},{6,255},{7,0},{8,1... | collective-permute-start | bytes 245768 | tf_op jit(solution)/shard_map/ppermute | solution.py:10
  39.3 2.5 %collective-permute-done.5 = bf16[2,40,2,256]{3,2,1,0:T(2,128)(2,1)S(1)} collective-permute-done((bf16[2,40,2,256]{3,2,1,0:T(2,128)(2,1)}, bf16[2,40,2,256]{3,2,1,0:T(2,128)(2,1)S(1)}, u32[]{:S(2)}, u32[]{:S(2)}) %collective-permute-start.5) | collective-permute-done | bytes 81952 | tf_op jit(solution)/shard_map/ppermute | solution.py:10
  41.8 2.8 %collective-permute-done.6 = bf16[2,40,2,256]{3,2,1,0:T(2,128)(2,1)S(1)} collective-permute-done((bf16[2,40,2,256]{3,2,1,0:T(2,128)(2,1)S(1)}, bf16[2,40,2,256]{3,2,1,0:T(2,128)(2,1)S(1)}, u32[]{:S(2)}, u32[]{:S(2)}) %collective-permute-start.6) | collective-permute-done | bytes 81952 | tf_op jit(solution)/shard_map/ppermute | solution.py:10
  44.7 0.4 constant_dynamic-slice_fusion
  45.4 1.3 %collective-permute-start.7 = (bf16[1,256,2,256]{1,3,2,0:T(8,128)(2,1)S(1)}, bf16[1,256,2,256]{1,3,2,0:T(8,128)(2,1)S(1)}, u32[]{:S(2)}, u32[]{:S(2)}) collective-permute-start(bf16[1,256,2,256]{1,3,2,0:T(8,128)(2,1)S(1)} %copy.49), channel_id=1, source_target_pairs={{0,256},{1,257},{2,258},{3,259},{4,260},{5,261},{6,262},{7,263},{8... | collective-permute-start | bytes 786440 | tf_op jit(solution)/shard_map/ppermute | solution.py:16
  46.7 1.1 %multiply_convert_fusion = (bf16[1,256,256]{2,1,0:T(8,128)(2,1)S(1)}, bf16[1,256,256]{2,1,0:T(8,128)(2,1)S(1)}) fusion(), kind=kLoop, calls=%fused_computation.346 | loop fusion | flops 1245184 | bytes 262144 | tf_op jit(solution)/shard_map/convert.104
  47.9 6.4 %collective-permute-done.7 = bf16[1,256,2,256]{1,3,2,0:T(8,128)(2,1)S(1)} collective-permute-done((bf16[1,256,2,256]{1,3,2,0:T(8,128)(2,1)S(1)}, bf16[1,256,2,256]{1,3,2,0:T(8,128)(2,1)S(1)}, u32[]{:S(2)}, u32[]{:S(2)}) %collective-permute-start.7) | collective-permute-done | bytes 262176 | tf_op jit(solution)/shard_map/ppermute | solution.py:16
  54.3 3.5 %conditional.6 = (bf16[1,256,2,256]{3,1,2,0:T(8,128)(2,1)S(1)}, bf16[1,2,256,2,256]{2,4,3,1,0:T(8,128)(2,1)S(1)}) conditional(s32[]{:T(128)} %convert_element_type.398, (bf16[1,256,2,256]{1,3,2,0:T(8,128)(2,1)S(1)}, bf16[1,2,256,2,256]{2,4,3,1,0:T(8,128)(2,1)S(1)}) %tuple.50, (bf16[1,256,2,256]{1,3,2,0:T(8,128)(2,1)S(1)}, ...), branch_computations={%region_2.3_spmd.clone, %region_3.4_spmd.clone} | conditional | flops 541327360 | bytes 22544400 | solution.py:166
  55.3 0.3 convolution_bitcast_fusion.37
  55.5 0.3 convolution_bitcast_fusion.36
  56.5 0.3 convolution_bitcast_fusion.35
  56.8 0.3 convolution_bitcast_fusion.34
  57.4 0.3 convolution_bitcast_fusion.32
  57.8 2.7 %conditional.7 = (bf16[1,256,2,256]{3,1,2,0:T(8,128)(2,1)S(1)}) conditional(s32[]{:T(128)} %convert_element_type.398, bf16[1,256,2,256]{3,1,2,0:T(8,128)(2,1)S(1)} %get-tuple-element.88, (bf16[1,256,2,256]{3,1,2,0:T(8,128)(2,1)S(1)}, bf16[2,256,256]{2,1,0:T(8,128)(2,1)S(1)}, bf16[1,256,256]{2,1,0:T(8,128)(2,1)S(1)}) %tuple.140), branch_computations={%region_4.5_spmd, %region_5.6_spmd} | conditional | flops 539688960 | bytes 15859720 | solution.py:173
  58.7 0.3 convolution_bitcast_fusion.12
  59.2 0.3 convolution_bitcast_fusion.11
  59.5 0.3 convolution_bitcast_fusion.10
  60.5 3.5 %conditional.8 = (bf16[1,256,2,256]{3,1,2,0:T(8,128)(2,1)S(1)}, f32[1,2,256,2,256]{4,2,3,1,0:T(8,128)S(1)}) conditional(s32[]{:T(128)} %convert_element_type.398, bf16[1,256,2,256]{3,1,2,0:T(8,128)(2,1)S(1)} %get-tuple-element.232, (bf16[1,2,256,2,256]{4,2,3,1,0:T(8,128)(2,1)S(1)}, bf16[1,256,2,256]{3,1,2,0:T(8,128)(2,1)S(1)}, ...), branch_computations={%region_6.7_spmd, %region_7.8_spmd} | conditional | flops 541458432 | bytes 27787280 | solution.py:179
  63.3 0.3 convolution_bitcast_fusion.16
  64.1 1.5 %collective-permute-start.8 = (bf16[1,256,2,256]{1,3,2,0:T(8,128)(2,1)S(1)}, bf16[1,256,2,256]{1,3,2,0:T(8,128)(2,1)S(1)}, u32[]{:S(2)}, u32[]{:S(2)}) collective-permute-start(bf16[1,256,2,256]{1,3,2,0:T(8,128)(2,1)S(1)} %copy.55), channel_id=1, source_target_pairs={{256,0},{257,1},{258,2},{259,3},{260,4},{261,5},{262,6},{263,7},{2... | collective-permute-start | bytes 786440 | tf_op jit(solution)/shard_map/ppermute | solution.py:16
  66.3 0.3 collective-permute-done.8
  66.6 1.8 %conditional.9 = (f32[1,2,256,2,256]{4,3,2,1,0:T(2,128)}) conditional(s32[]{:T(128)} %convert_element_type.397, f32[1,2,256,2,256]{4,2,3,1,0:T(8,128)S(1)} %get-tuple-element.91, (bf16[1,2,256,2,256]{2,4,3,1,0:T(8,128)(2,1)S(1)}, bf16[1,2,256,2,256]{4,2,3,1,0:T(8,128)(2,1)S(1)}, bf16[1,256,2,256]{1,3,2,0:T(8,128)(2,1)S(1)}, ...), branch_computations={%region_8.9_spmd, %region_9.10_spmd} | conditional | flops 540672000 | bytes 26214408 | solution.py:179
  66.6 1.8 %copy.90 = f32[1,2,256,2,256]{4,3,2,1,0:T(2,128)} copy(f32[1,2,256,2,256]{4,2,3,1,0:T(8,128)S(1)} %param.8) | data formatting | bytes 2097152 | tf_op jit(solution)/shard_map/cond | solution.py:179
  68.4 0.3 broadcast_in_dim.22
  68.8 1.7 %bitcast_dynamic-update-slice_fusion = f32[320,2,2,256]{3,2,0,1:T(2,128)S(1)} fusion(f32[320,2,2,256]{3,2,0,1:T(2,128)S(1)} %broadcast_in_dim.22, s32[]{:T(128)S(6)} %select_n.28, f32[1,2,256,2,256]{4,3,2,1,0:T(2,128)} %get-tuple-element.139, f32[]{:T(128)} %bitcast.141), kind=kLoop, calls=%fused_computation.336 | loop fusion | flops 262144 | bytes 2097160 | tf_op jit(solution)/shard_map/dynamic_update_slice | solution.py:109
  70.4 0.5 convert.201
  70.9 0.4 fusion.203
  71.3 3.4 %collective-permute-start.10 = (bf16[40,2,2,256]{3,2,0,1:T(2,128)(2,1)S(1)}, bf16[40,2,2,256]{3,2,0,1:T(2,128)(2,1)S(1)}, u32[]{:S(2)}, u32[]{:S(2)}) collective-permute-start(bf16[40,2,2,256]{3,2,0,1:T(2,128)(2,1)S(1)} %get-tuple-element.215), channel_id=1, source_target_pairs={{0,2},{1,3},{2,4},{3,5},{4,6},{5,7},{6,8},{7,9},{8,10},{9,11},{10,... | collective-permute-start | bytes 245768 | tf_op jit(solution)/shard_map/ppermute | solution.py:10
  74.7 4.5 %collective-permute-start.11 = (bf16[40,2,2,256]{3,2,0,1:T(2,128)(2,1)S(1)}, bf16[40,2,2,256]{3,2,0,1:T(2,128)(2,1)S(1)}, u32[]{:S(2)}, u32[]{:S(2)}) collective-permute-start(bf16[40,2,2,256]{3,2,0,1:T(2,128)(2,1)S(1)} %get-tuple-element.214), channel_id=1, source_target_pairs={{0,3},{1,4},{2,5},{3,6},{4,7},{5,8},{6,9},{7,10},{8,11},{9,12},{10... | collective-permute-start | bytes 245768 | tf_op jit(solution)/shard_map/ppermute | solution.py:10
  79.3 3.6 %collective-permute-start.12 = (bf16[40,2,2,256]{3,2,0,1:T(2,128)(2,1)S(1)}, bf16[40,2,2,256]{3,2,0,1:T(2,128)(2,1)S(1)}, u32[]{:S(2)}, u32[]{:S(2)}) collective-permute-start(bf16[40,2,2,256]{3,2,0,1:T(2,128)(2,1)S(1)} %get-tuple-element.213), channel_id=1, source_target_pairs={{0,4},{1,5},{2,6},{3,7},{4,8},{5,9},{6,10},{7,11},{8,12},{9,13},{1... | collective-permute-start | bytes 245768 | tf_op jit(solution)/shard_map/ppermute | solution.py:10
  82.8 2.7 %collective-permute-start.13 = (bf16[40,2,2,256]{3,2,0,1:T(2,128)(2,1)S(1)}, bf16[40,2,2,256]{3,2,0,1:T(2,128)(2,1)S(1)}, u32[]{:S(2)}, u32[]{:S(2)}) collective-permute-start(bf16[40,2,2,256]{3,2,0,1:T(2,128)(2,1)S(1)} %get-tuple-element.212), channel_id=1, source_target_pairs={{0,5},{1,6},{2,7},{3,8},{4,9},{5,10},{6,11},{7,12},{8,13},{9,14},{... | collective-permute-start | bytes 245768 | tf_op jit(solution)/shard_map/ppermute | solution.py:10
  85.6 3.6 %collective-permute-start.14 = (bf16[40,2,2,256]{3,2,0,1:T(2,128)(2,1)S(1)}, bf16[40,2,2,256]{3,2,0,1:T(2,128)(2,1)S(1)}, u32[]{:S(2)}, u32[]{:S(2)}) collective-permute-start(bf16[40,2,2,256]{3,2,0,1:T(2,128)(2,1)S(1)} %get-tuple-element.211), channel_id=1, source_target_pairs={{0,6},{1,7},{2,8},{3,9},{4,10},{5,11},{6,12},{7,13},{8,14},{9,15},... | collective-permute-start | bytes 245768 | tf_op jit(solution)/shard_map/ppermute | solution.py:10
  89.2 2.3 %collective-permute-start.15 = (bf16[40,2,2,256]{3,2,0,1:T(2,128)(2,1)S(1)}, bf16[40,2,2,256]{3,2,0,1:T(2,128)(2,1)S(1)}, u32[]{:S(2)}, u32[]{:S(2)}) collective-permute-start(bf16[40,2,2,256]{3,2,0,1:T(2,128)(2,1)S(1)} %get-tuple-element.210), channel_id=1, source_target_pairs={{0,7},{1,8},{2,9},{3,10},{4,11},{5,12},{6,13},{7,14},{8,15},{9,16}... | collective-permute-start | bytes 245768 | tf_op jit(solution)/shard_map/ppermute | solution.py:10
  91.5 1.9 %collective-permute-start.9 = (bf16[40,2,2,256]{3,2,0,1:T(2,128)(2,1)S(1)}, bf16[40,2,2,256]{3,2,0,1:T(2,128)(2,1)S(1)}, u32[]{:S(2)}, u32[]{:S(2)}) collective-permute-start(bf16[40,2,2,256]{3,2,0,1:T(2,128)(2,1)S(1)} %get-tuple-element.209), channel_id=1, source_target_pairs={{0,1},{1,2},{2,3},{3,4},{4,5},{5,6},{6,7},{7,8},{8,9},{9,10},{10,1... | collective-permute-start | bytes 245768 | tf_op jit(solution)/shard_map/ppermute | solution.py:10
  93.4 1.3 %collective-permute-done.13 = bf16[40,2,2,256]{3,2,0,1:T(2,128)(2,1)S(1)} collective-permute-done((bf16[40,2,2,256]{3,2,0,1:T(2,128)(2,1)S(1)}, bf16[40,2,2,256]{3,2,0,1:T(2,128)(2,1)S(1)}, u32[]{:S(2)}, u32[]{:S(2)}) %collective-permute-start.13) | collective-permute-done | bytes 81952 | tf_op jit(solution)/shard_map/ppermute | solution.py:10
  94.7 4.4 %collective-permute-done.14 = bf16[40,2,2,256]{3,2,0,1:T(2,128)(2,1)S(1)} collective-permute-done((bf16[40,2,2,256]{3,2,0,1:T(2,128)(2,1)S(1)}, bf16[40,2,2,256]{3,2,0,1:T(2,128)(2,1)S(1)}, u32[]{:S(2)}, u32[]{:S(2)}) %collective-permute-start.14) | collective-permute-done | bytes 81952 | tf_op jit(solution)/shard_map/ppermute | solution.py:10
  99.1 0.7 collective-permute-done.15
  99.8 5.1 %collective-permute-done.9 = bf16[40,2,2,256]{3,2,0,1:T(2,128)(2,1)S(1)} collective-permute-done((bf16[40,2,2,256]{3,2,0,1:T(2,128)(2,1)S(1)}, bf16[40,2,2,256]{3,2,0,1:T(2,128)(2,1)S(1)}, u32[]{:S(2)}, u32[]{:S(2)}) %collective-permute-start.9) | collective-permute-done | bytes 81952 | tf_op jit(solution)/shard_map/ppermute | solution.py:10
  104.9 1.0 add_bitcast_fusion
  (77 shorter events, 7.9 us)
Async XLA Ops:
  0.0 37.0 %copy-start.3 = (bf16[2,40,2,256]{3,2,1,0:T(2,128)(2,1)S(1)}, bf16[2,40,2,256]{3,2,1,0:T(2,128)(2,1)}, u32[]{:S(2)}) copy-start(bf16[2,40,2,256]{3,2,1,0:T(2,128)(2,1)} %param.18) | copy-start | bytes 245764
  0.0 33.9 %collective-permute-start = (bf16[2,40,2,256]{3,2,1,0:T(2,128)(2,1)}, bf16[2,40,2,256]{3,2,1,0:T(2,128)(2,1)S(1)}, u32[]{:S(2)}, u32[]{:S(2)}) collective-permute-start(bf16[2,40,2,256]{3,2,1,0:T(2,128)(2,1)} %param.18), channel_id=1, source_target_pairs={{0,255},{1,0},{2,1},{3,2},{4,3},{5,4},{6,5},{7,6},{8,7},{9,8},{10,... | collective-permute-start | bytes 245768 | tf_op jit(solution)/shard_map/ppermute | solution.py:10
  16.7 20.2 %collective-permute-start.1 = (bf16[2,40,2,256]{3,2,1,0:T(2,128)(2,1)}, bf16[2,40,2,256]{3,2,1,0:T(2,128)(2,1)S(1)}, u32[]{:S(2)}, u32[]{:S(2)}) collective-permute-start(bf16[2,40,2,256]{3,2,1,0:T(2,128)(2,1)} %param.18), channel_id=1, source_target_pairs={{0,254},{1,255},{2,0},{3,1},{4,2},{5,3},{6,4},{7,5},{8,6},{9,7},{1... | collective-permute-start | bytes 245768 | tf_op jit(solution)/shard_map/ppermute | solution.py:10
  19.2 19.8 %collective-permute-start.2 = (bf16[2,40,2,256]{3,2,1,0:T(2,128)(2,1)}, bf16[2,40,2,256]{3,2,1,0:T(2,128)(2,1)S(1)}, u32[]{:S(2)}, u32[]{:S(2)}) collective-permute-start(bf16[2,40,2,256]{3,2,1,0:T(2,128)(2,1)} %param.18), channel_id=1, source_target_pairs={{0,253},{1,254},{2,255},{3,0},{4,1},{5,2},{6,3},{7,4},{8,5},{9,6},... | collective-permute-start | bytes 245768 | tf_op jit(solution)/shard_map/ppermute | solution.py:10
  22.5 16.6 %collective-permute-start.3 = (bf16[2,40,2,256]{3,2,1,0:T(2,128)(2,1)}, bf16[2,40,2,256]{3,2,1,0:T(2,128)(2,1)S(1)}, u32[]{:S(2)}, u32[]{:S(2)}) collective-permute-start(bf16[2,40,2,256]{3,2,1,0:T(2,128)(2,1)} %param.18), channel_id=1, source_target_pairs={{0,252},{1,253},{2,254},{3,255},{4,0},{5,1},{6,2},{7,3},{8,4},{9,5... | collective-permute-start | bytes 245768 | tf_op jit(solution)/shard_map/ppermute | solution.py:10
  25.5 13.7 %collective-permute-start.4 = (bf16[2,40,2,256]{3,2,1,0:T(2,128)(2,1)}, bf16[2,40,2,256]{3,2,1,0:T(2,128)(2,1)S(1)}, u32[]{:S(2)}, u32[]{:S(2)}) collective-permute-start(bf16[2,40,2,256]{3,2,1,0:T(2,128)(2,1)} %param.18), channel_id=1, source_target_pairs={{0,251},{1,252},{2,253},{3,254},{4,255},{5,0},{6,1},{7,2},{8,3},{9... | collective-permute-start | bytes 245768 | tf_op jit(solution)/shard_map/ppermute | solution.py:10
  34.0 7.8 %collective-permute-start.5 = (bf16[2,40,2,256]{3,2,1,0:T(2,128)(2,1)}, bf16[2,40,2,256]{3,2,1,0:T(2,128)(2,1)S(1)}, u32[]{:S(2)}, u32[]{:S(2)}) collective-permute-start(bf16[2,40,2,256]{3,2,1,0:T(2,128)(2,1)} %param.18), channel_id=1, source_target_pairs={{0,250},{1,251},{2,252},{3,253},{4,254},{5,255},{6,0},{7,1},{8,2},... | collective-permute-start | bytes 245768 | tf_op jit(solution)/shard_map/ppermute | solution.py:10
  37.0 7.7 %collective-permute-start.6 = (bf16[2,40,2,256]{3,2,1,0:T(2,128)(2,1)S(1)}, bf16[2,40,2,256]{3,2,1,0:T(2,128)(2,1)S(1)}, u32[]{:S(2)}, u32[]{:S(2)}) collective-permute-start(bf16[2,40,2,256]{3,2,1,0:T(2,128)(2,1)S(1)} %copy-done.3), channel_id=1, source_target_pairs={{0,249},{1,250},{2,251},{3,252},{4,253},{5,254},{6,255},{7,0},{8,1... | collective-permute-start | bytes 245768 | tf_op jit(solution)/shard_map/ppermute | solution.py:10
  39.2 6.0 %copy-start = (bf16[2,256,256]{2,1,0:T(8,128)(2,1)S(1)}, bf16[2,256,256]{2,1,0:T(8,128)(2,1)}, u32[]{:S(2)}) copy-start(bf16[2,256,256]{2,1,0:T(8,128)(2,1)} %param.17) | copy-start | bytes 786436
  39.2 6.0 %copy-start.1 = (bf16[256,2,256]{2,1,0:T(2,128)(2,1)S(1)}, bf16[256,2,256]{2,1,0:T(2,128)(2,1)}, u32[]{:S(2)}) copy-start(bf16[256,2,256]{2,1,0:T(2,128)(2,1)} %param.16) | copy-start | bytes 786436
  45.4 8.8 %collective-permute-start.7 = (bf16[1,256,2,256]{1,3,2,0:T(8,128)(2,1)S(1)}, bf16[1,256,2,256]{1,3,2,0:T(8,128)(2,1)S(1)}, u32[]{:S(2)}, u32[]{:S(2)}) collective-permute-start(bf16[1,256,2,256]{1,3,2,0:T(8,128)(2,1)S(1)} %copy.49), channel_id=1, source_target_pairs={{0,256},{1,257},{2,258},{3,259},{4,260},{5,261},{6,262},{7,263},{8... | collective-permute-start | bytes 786440 | tf_op jit(solution)/shard_map/ppermute | solution.py:16
  54.2 3.6 %copy-start.2 = (bf16[1,256,256]{2,1,0:T(8,128)(2,1)S(1)}, bf16[1,256,256]{2,1,0:T(8,128)(2,1)}, u32[]{:S(2)}) copy-start(bf16[1,256,256]{2,1,0:T(8,128)(2,1)} %param.21) | copy-start | bytes 393220
  64.1 2.4 %collective-permute-start.8 = (bf16[1,256,2,256]{1,3,2,0:T(8,128)(2,1)S(1)}, bf16[1,256,2,256]{1,3,2,0:T(8,128)(2,1)S(1)}, u32[]{:S(2)}, u32[]{:S(2)}) collective-permute-start(bf16[1,256,2,256]{1,3,2,0:T(8,128)(2,1)S(1)} %copy.55), channel_id=1, source_target_pairs={{256,0},{257,1},{258,2},{259,3},{260,4},{261,5},{262,6},{263,7},{2... | collective-permute-start | bytes 786440 | tf_op jit(solution)/shard_map/ppermute | solution.py:16
  71.3 17.9 %collective-permute-start.10 = (bf16[40,2,2,256]{3,2,0,1:T(2,128)(2,1)S(1)}, bf16[40,2,2,256]{3,2,0,1:T(2,128)(2,1)S(1)}, u32[]{:S(2)}, u32[]{:S(2)}) collective-permute-start(bf16[40,2,2,256]{3,2,0,1:T(2,128)(2,1)S(1)} %get-tuple-element.215), channel_id=1, source_target_pairs={{0,2},{1,3},{2,4},{3,5},{4,6},{5,7},{6,8},{7,9},{8,10},{9,11},{10,... | collective-permute-start | bytes 245768 | tf_op jit(solution)/shard_map/ppermute | solution.py:10
  74.7 16.7 %collective-permute-start.11 = (bf16[40,2,2,256]{3,2,0,1:T(2,128)(2,1)S(1)}, bf16[40,2,2,256]{3,2,0,1:T(2,128)(2,1)S(1)}, u32[]{:S(2)}, u32[]{:S(2)}) collective-permute-start(bf16[40,2,2,256]{3,2,0,1:T(2,128)(2,1)S(1)} %get-tuple-element.214), channel_id=1, source_target_pairs={{0,3},{1,4},{2,5},{3,6},{4,7},{5,8},{6,9},{7,10},{8,11},{9,12},{10... | collective-permute-start | bytes 245768 | tf_op jit(solution)/shard_map/ppermute | solution.py:10
  79.3 14.1 %collective-permute-start.12 = (bf16[40,2,2,256]{3,2,0,1:T(2,128)(2,1)S(1)}, bf16[40,2,2,256]{3,2,0,1:T(2,128)(2,1)S(1)}, u32[]{:S(2)}, u32[]{:S(2)}) collective-permute-start(bf16[40,2,2,256]{3,2,0,1:T(2,128)(2,1)S(1)} %get-tuple-element.213), channel_id=1, source_target_pairs={{0,4},{1,5},{2,6},{3,7},{4,8},{5,9},{6,10},{7,11},{8,12},{9,13},{1... | collective-permute-start | bytes 245768 | tf_op jit(solution)/shard_map/ppermute | solution.py:10
  82.8 11.8 %collective-permute-start.13 = (bf16[40,2,2,256]{3,2,0,1:T(2,128)(2,1)S(1)}, bf16[40,2,2,256]{3,2,0,1:T(2,128)(2,1)S(1)}, u32[]{:S(2)}, u32[]{:S(2)}) collective-permute-start(bf16[40,2,2,256]{3,2,0,1:T(2,128)(2,1)S(1)} %get-tuple-element.212), channel_id=1, source_target_pairs={{0,5},{1,6},{2,7},{3,8},{4,9},{5,10},{6,11},{7,12},{8,13},{9,14},{... | collective-permute-start | bytes 245768 | tf_op jit(solution)/shard_map/ppermute | solution.py:10
  85.6 13.5 %collective-permute-start.14 = (bf16[40,2,2,256]{3,2,0,1:T(2,128)(2,1)S(1)}, bf16[40,2,2,256]{3,2,0,1:T(2,128)(2,1)S(1)}, u32[]{:S(2)}, u32[]{:S(2)}) collective-permute-start(bf16[40,2,2,256]{3,2,0,1:T(2,128)(2,1)S(1)} %get-tuple-element.211), channel_id=1, source_target_pairs={{0,6},{1,7},{2,8},{3,9},{4,10},{5,11},{6,12},{7,13},{8,14},{9,15},... | collective-permute-start | bytes 245768 | tf_op jit(solution)/shard_map/ppermute | solution.py:10
  89.2 10.6 %collective-permute-start.15 = (bf16[40,2,2,256]{3,2,0,1:T(2,128)(2,1)S(1)}, bf16[40,2,2,256]{3,2,0,1:T(2,128)(2,1)S(1)}, u32[]{:S(2)}, u32[]{:S(2)}) collective-permute-start(bf16[40,2,2,256]{3,2,0,1:T(2,128)(2,1)S(1)} %get-tuple-element.210), channel_id=1, source_target_pairs={{0,7},{1,8},{2,9},{3,10},{4,11},{5,12},{6,13},{7,14},{8,15},{9,16}... | collective-permute-start | bytes 245768 | tf_op jit(solution)/shard_map/ppermute | solution.py:10
  91.5 13.4 %collective-permute-start.9 = (bf16[40,2,2,256]{3,2,0,1:T(2,128)(2,1)S(1)}, bf16[40,2,2,256]{3,2,0,1:T(2,128)(2,1)S(1)}, u32[]{:S(2)}, u32[]{:S(2)}) collective-permute-start(bf16[40,2,2,256]{3,2,0,1:T(2,128)(2,1)S(1)} %get-tuple-element.209), channel_id=1, source_target_pairs={{0,1},{1,2},{2,3},{3,4},{4,5},{5,6},{6,7},{7,8},{8,9},{9,10},{10,1... | collective-permute-start | bytes 245768 | tf_op jit(solution)/shard_map/ppermute | solution.py:10
where the time goes:
time: 107 us; the launch traced here: 106 us
  starting transfers between devices  59.8 us (56%)
  waiting for transfers between devices  23.5 us (22%)
  local copies, waits for them, and re-layouts  7.6 us (7%)
  matrix products  6.43 us (6%)
  other arithmetic  6.41 us (6%)
  between operations  1.71 us (2%)
    ppermute x14, starting transfers between devices, shifted(): return lax.ppermute(value, axis, pairs)  57.1 us
    ppermute x14, waiting for transfers between devices, shifted(): return lax.ppermute(value, axis, pairs)  16.8 us
    ppermute x2, waiting for transfers between devices, passed_along(): return lax.ppermute(shard, axis, pairs)  6.66 us
    dot_general x24, matrix products, product(): return jnp.einsum(form, first, second, preferred_element_type=jnp.float32)  6.43 us
    ppermute x2, starting transfers between devices, passed_along(): return lax.ppermute(shard, axis, pairs)  2.78 us
    unnamed x16, local copies, waits for them, and re-layouts  2.49 us
  transfers between devices with their start and end apart: 16, of which 8 were waited for; matrix products, arithmetic and copies ran while one was open for 4% of the time, Pallas kernels for 0%

commit v1 on v0

--- a/solution.py
+++ b/solution.py
@@ -123,7 +123,7 @@
     reach = (local_rows + width - 2) // local_rows + 1
     blocks = [object_slab]
     for step_at in range(1, reach):
-        blocks.append(shifted(object_slab, "tile", -step_at))
+        blocks.append(shifted(blocks[-1], "tile", -1))
     window = jnp.concatenate(blocks, axis=1)
     relative = offsets - tile_now * local_rows
     patches = jax.vmap(lambda offset: lax.dynamic_slice_in_dim(window, offset, width, 1))(relative)
@@ -185,10 +185,10 @@
         )
     gradients = gradients * live_slots.astype(jnp.float32)[:, None, None, None, None]
     nearby = accumulate(gradients, relative, reach * local_rows)
-    own_rows = nearby[:local_rows]
-    for step_at in range(1, reach):
+    own_rows = nearby[(reach - 1) * local_rows : reach * local_rows]
+    for step_at in reversed(range(reach - 1)):
         block_rows = nearby[step_at * local_rows : (step_at + 1) * local_rows]
-        own_rows = own_rows + shifted(block_rows.astype(jnp.bfloat16), "tile", step_at).astype(
+        own_rows = block_rows + shifted(own_rows.astype(jnp.bfloat16), "tile", 1).astype(
             block_rows.dtype
         )
     return jnp.transpose(own_rows, (1, 0, 2, 3))

time: 107 us -> 194 us (1.81)
  the two profiles are of different devices: /device:TPU:1 before, /device:TPU:0 now
where the time goes in v1:
time: 194 us
  waiting for transfers between devices  90.3 us (47%)
  starting transfers between devices  83.7 us (43%)
  local copies, waits for them, and re-layouts  8.06 us (4%)
  other arithmetic  5.63 us (3%)
  matrix products  4.19 us (2%)
    ppermute x14, waiting for transfers between devices, shifted(): return lax.ppermute(value, axis, pairs)  81 us
    ppermute x14, starting transfers between devices, shifted(): return lax.ppermute(value, axis, pairs)  80.9 us
    ppermute x2, waiting for transfers between devices, passed_along(): return lax.ppermute(shard, axis, pairs)  9.26 us
    dot_general x16, matrix products, product(): return jnp.einsum(form, first, second, preferred_element_type=jnp.float32)  4.19 us
  transfers between devices with their start and end apart: 16, of which 14 were waited for; matrix products, arithmetic and copies ran while one was open for 2% of the time, Pallas kernels for 0%

profile of v1, /device:TPU:0, one launch (start us, length us, event | category | flops | bytes accessed | tf_op | source)
XLA Modules:
  0.0 193.7 jit_solution(4185315060230927449)
XLA Ops:
  0.0 10.7 %collective-permute-start = (bf16[2,40,2,256]{3,2,1,0:T(2,128)(2,1)}, bf16[2,40,2,256]{3,2,1,0:T(2,128)(2,1)S(1)}, u32[]{:S(2)}, u32[]{:S(2)}) collective-permute-start(bf16[2,40,2,256]{3,2,1,0:T(2,128)(2,1)} %param.18), channel_id=1, source_target_pairs={{0,255},{1,0},{2,1},{3,2},{4,3},{5,4},{6,5},{7,6},{8,7},{9,8},{10,... | collective-permute-start | bytes 245768 | tf_op jit(solution)/shard_map/ppermute | solution.py:10
  10.7 1.1 copy.44
  11.8 1.0 copy.97
  13.4 0.9 constant_dynamic-update-slice_fusion.7
  14.4 8.2 %collective-permute-start.1 = (bf16[2,40,2,256]{3,2,1,0:T(2,128)(2,1)S(1)}, bf16[2,40,2,256]{3,2,1,0:T(2,128)(2,1)S(1)}, u32[]{:S(2)}, u32[]{:S(2)}) collective-permute-start(bf16[2,40,2,256]{3,2,1,0:T(2,128)(2,1)S(1)} %collective-permute-done), channel_id=1, source_target_pairs={{0,255},{1,0},{2,1},{3,2},{4,3},{5,4},{6,5},{7,6},{8,7},{9,8},{10,... | collective-permute-start | bytes 245768 | tf_op jit(solution)/shard_map/ppermute | solution.py:10
  22.7 2.0 %collective-permute-done.1 = bf16[2,40,2,256]{3,2,1,0:T(2,128)(2,1)S(1)} collective-permute-done((bf16[2,40,2,256]{3,2,1,0:T(2,128)(2,1)S(1)}, bf16[2,40,2,256]{3,2,1,0:T(2,128)(2,1)S(1)}, u32[]{:S(2)}, u32[]{:S(2)}) %collective-permute-start.1) | collective-permute-done | bytes 81952 | tf_op jit(solution)/shard_map/ppermute | solution.py:10
  24.7 9.7 %collective-permute-start.2 = (bf16[2,40,2,256]{3,2,1,0:T(2,128)(2,1)S(1)}, bf16[2,40,2,256]{3,2,1,0:T(2,128)(2,1)S(1)}, u32[]{:S(2)}, u32[]{:S(2)}) collective-permute-start(bf16[2,40,2,256]{3,2,1,0:T(2,128)(2,1)S(1)} %collective-permute-done.1), channel_id=1, source_target_pairs={{0,255},{1,0},{2,1},{3,2},{4,3},{5,4},{6,5},{7,6},{8,7},{9,8},{10,... | collective-permute-start | bytes 245768 | tf_op jit(solution)/shard_map/ppermute | solution.py:10
  34.5 2.0 %collective-permute-done.2 = bf16[2,40,2,256]{3,2,1,0:T(2,128)(2,1)S(1)} collective-permute-done((bf16[2,40,2,256]{3,2,1,0:T(2,128)(2,1)S(1)}, bf16[2,40,2,256]{3,2,1,0:T(2,128)(2,1)S(1)}, u32[]{:S(2)}, u32[]{:S(2)}) %collective-permute-start.2) | collective-permute-done | bytes 81952 | tf_op jit(solution)/shard_map/ppermute | solution.py:10
  36.4 9.7 %collective-permute-start.3 = (bf16[2,40,2,256]{3,2,1,0:T(2,128)(2,1)S(1)}, bf16[2,40,2,256]{3,2,1,0:T(2,128)(2,1)S(1)}, u32[]{:S(2)}, u32[]{:S(2)}) collective-permute-start(bf16[2,40,2,256]{3,2,1,0:T(2,128)(2,1)S(1)} %collective-permute-done.2), channel_id=1, source_target_pairs={{0,255},{1,0},{2,1},{3,2},{4,3},{5,4},{6,5},{7,6},{8,7},{9,8},{10,... | collective-permute-start | bytes 245768 | tf_op jit(solution)/shard_map/ppermute | solution.py:10
  46.2 2.0 %collective-permute-done.3 = bf16[2,40,2,256]{3,2,1,0:T(2,128)(2,1)S(1)} collective-permute-done((bf16[2,40,2,256]{3,2,1,0:T(2,128)(2,1)S(1)}, bf16[2,40,2,256]{3,2,1,0:T(2,128)(2,1)S(1)}, u32[]{:S(2)}, u32[]{:S(2)}) %collective-permute-start.3) | collective-permute-done | bytes 81952 | tf_op jit(solution)/shard_map/ppermute | solution.py:10
  48.2 9.7 %collective-permute-start.4 = (bf16[2,40,2,256]{3,2,1,0:T(2,128)(2,1)S(1)}, bf16[2,40,2,256]{3,2,1,0:T(2,128)(2,1)S(1)}, u32[]{:S(2)}, u32[]{:S(2)}) collective-permute-start(bf16[2,40,2,256]{3,2,1,0:T(2,128)(2,1)S(1)} %collective-permute-done.3), channel_id=1, source_target_pairs={{0,255},{1,0},{2,1},{3,2},{4,3},{5,4},{6,5},{7,6},{8,7},{9,8},{10,... | collective-permute-start | bytes 245768 | tf_op jit(solution)/shard_map/ppermute | solution.py:10
  58.0 1.9 %collective-permute-done.4 = bf16[2,40,2,256]{3,2,1,0:T(2,128)(2,1)S(1)} collective-permute-done((bf16[2,40,2,256]{3,2,1,0:T(2,128)(2,1)S(1)}, bf16[2,40,2,256]{3,2,1,0:T(2,128)(2,1)S(1)}, u32[]{:S(2)}, u32[]{:S(2)}) %collective-permute-start.4) | collective-permute-done | bytes 81952 | tf_op jit(solution)/shard_map/ppermute | solution.py:10
  59.9 9.7 %collective-permute-start.5 = (bf16[2,40,2,256]{3,2,1,0:T(2,128)(2,1)S(1)}, bf16[2,40,2,256]{3,2,1,0:T(2,128)(2,1)S(1)}, u32[]{:S(2)}, u32[]{:S(2)}) collective-permute-start(bf16[2,40,2,256]{3,2,1,0:T(2,128)(2,1)S(1)} %collective-permute-done.4), channel_id=1, source_target_pairs={{0,255},{1,0},{2,1},{3,2},{4,3},{5,4},{6,5},{7,6},{8,7},{9,8},{10,... | collective-permute-start | bytes 245768 | tf_op jit(solution)/shard_map/ppermute | solution.py:10
  69.7 2.0 %collective-permute-done.5 = bf16[2,40,2,256]{3,2,1,0:T(2,128)(2,1)S(1)} collective-permute-done((bf16[2,40,2,256]{3,2,1,0:T(2,128)(2,1)S(1)}, bf16[2,40,2,256]{3,2,1,0:T(2,128)(2,1)S(1)}, u32[]{:S(2)}, u32[]{:S(2)}) %collective-permute-start.5) | collective-permute-done | bytes 81952 | tf_op jit(solution)/shard_map/ppermute | solution.py:10
  71.7 9.7 %collective-permute-start.6 = (bf16[2,40,2,256]{3,2,1,0:T(2,128)(2,1)S(1)}, bf16[2,40,2,256]{3,2,1,0:T(2,128)(2,1)S(1)}, u32[]{:S(2)}, u32[]{:S(2)}) collective-permute-start(bf16[2,40,2,256]{3,2,1,0:T(2,128)(2,1)S(1)} %collective-permute-done.5), channel_id=1, source_target_pairs={{0,255},{1,0},{2,1},{3,2},{4,3},{5,4},{6,5},{7,6},{8,7},{9,8},{10,... | collective-permute-start | bytes 245768 | tf_op jit(solution)/shard_map/ppermute | solution.py:10
  81.5 2.0 %collective-permute-done.6 = bf16[2,40,2,256]{3,2,1,0:T(2,128)(2,1)S(1)} collective-permute-done((bf16[2,40,2,256]{3,2,1,0:T(2,128)(2,1)S(1)}, bf16[2,40,2,256]{3,2,1,0:T(2,128)(2,1)S(1)}, u32[]{:S(2)}, u32[]{:S(2)}) %collective-permute-start.6) | collective-permute-done | bytes 81952 | tf_op jit(solution)/shard_map/ppermute | solution.py:10
  83.5 0.4 constant_dynamic-slice_fusion
  84.0 3.5 %conditional.5 = (bf16[1,256,2,256]{3,1,2,0:T(8,128)(2,1)S(1)}, bf16[1,2,256,2,256]{2,4,3,1,0:T(8,128)(2,1)S(1)}) conditional(s32[]{:T(128)} %convert_element_type.409, bf16[1,256,2,256]{3,1,2,0:T(8,128)(2,1)S(1)} %bitcast.400, (bf16[1,256,2,256]{1,3,2,0:T(8,128)(2,1)S(1)}, bf16[1,2,256,2,256]{4,2,3,1,0:T(8,128)(2,1)S(1)}, ...), branch_computations={%region_0.1_spmd, %region_1.2_spmd} | conditional | flops 541327360 | bytes 22544400 | solution.py:166
  85.0 0.3 convolution_bitcast_fusion.5
  85.3 0.3 convolution_bitcast_fusion.4
  86.1 0.3 convolution_bitcast_fusion.3
  86.4 0.3 convolution_bitcast_fusion.2
  87.1 0.3 convolution_bitcast_fusion
  87.6 1.3 collective-permute-start.7
  88.9 1.1 multiply_convert_fusion
  90.3 0.7 copy-done.2
  91.2 1.5 collective-permute-start.8
  93.4 9.3 %collective-permute-done.8 = bf16[1,256,2,256]{1,3,2,0:T(8,128)(2,1)S(1)} collective-permute-done((bf16[1,256,2,256]{1,3,2,0:T(8,128)(2,1)S(1)}, bf16[1,256,2,256]{1,3,2,0:T(8,128)(2,1)S(1)}, u32[]{:S(2)}, u32[]{:S(2)}) %collective-permute-start.8) | collective-permute-done | bytes 262176 | tf_op jit(solution)/shard_map/ppermute | solution.py:16
  102.6 5.0 %conditional.9 = (f32[1,2,256,2,256]{4,3,2,1,0:T(2,128)}) conditional(s32[]{:T(128)} %convert_element_type.409, f32[1,2,256,2,256]{4,2,3,1,0:T(8,128)S(1)} %get-tuple-element.91, (bf16[1,2,256,2,256]{2,4,3,1,0:T(8,128)(2,1)S(1)}, bf16[1,2,256,2,256]{4,2,3,1,0:T(8,128)(2,1)S(1)}, bf16[1,256,2,256]{1,3,2,0:T(8,128)(2,1)S(1)}, ...), branch_computations={%region_8.9_spmd, %region_9.10_spmd} | conditional | flops 540672000 | bytes 26214408 | solution.py:179
  103.4 0.3 convolution_bitcast_fusion.29
  105.8 1.8 copy.91
  107.6 0.3 broadcast_in_dim.22
  107.9 1.7 bitcast_dynamic-update-slice_fusion
  109.7 1.9 collective-permute-start.9
  111.6 10.2 %collective-permute-done.9 = bf16[40,2,2,256]{3,2,0,1:T(2,128)(2,1)S(1)} collective-permute-done((bf16[40,2,2,256]{3,2,0,1:T(2,128)(2,1)S(1)}, bf16[40,2,2,256]{3,2,0,1:T(2,128)(2,1)S(1)}, u32[]{:S(2)}, u32[]{:S(2)}) %collective-permute-start.9) | collective-permute-done | bytes 81952 | tf_op jit(solution)/shard_map/ppermute | solution.py:10
  121.9 1.9 collective-permute-start.10
  123.8 9.8 %collective-permute-done.10 = bf16[40,2,2,256]{3,2,0,1:T(2,128)(2,1)S(1)} collective-permute-done((bf16[40,2,2,256]{3,2,0,1:T(2,128)(2,1)S(1)}, bf16[40,2,2,256]{3,2,0,1:T(2,128)(2,1)S(1)}, u32[]{:S(2)}, u32[]{:S(2)}) %collective-permute-start.10) | collective-permute-done | bytes 81952 | tf_op jit(solution)/shard_map/ppermute | solution.py:10
  133.8 1.9 collective-permute-start.11
  135.7 9.8 %collective-permute-done.11 = bf16[40,2,2,256]{3,2,0,1:T(2,128)(2,1)S(1)} collective-permute-done((bf16[40,2,2,256]{3,2,0,1:T(2,128)(2,1)S(1)}, bf16[40,2,2,256]{3,2,0,1:T(2,128)(2,1)S(1)}, u32[]{:S(2)}, u32[]{:S(2)}) %collective-permute-start.11) | collective-permute-done | bytes 81952 | tf_op jit(solution)/shard_map/ppermute | solution.py:10
  145.6 1.9 collective-permute-start.12
  147.6 9.8 %collective-permute-done.12 = bf16[40,2,2,256]{3,2,0,1:T(2,128)(2,1)S(1)} collective-permute-done((bf16[40,2,2,256]{3,2,0,1:T(2,128)(2,1)S(1)}, bf16[40,2,2,256]{3,2,0,1:T(2,128)(2,1)S(1)}, u32[]{:S(2)}, u32[]{:S(2)}) %collective-permute-start.12) | collective-permute-done | bytes 81952 | tf_op jit(solution)/shard_map/ppermute | solution.py:10
  157.5 1.9 collective-permute-start.13
  159.4 9.8 %collective-permute-done.13 = bf16[40,2,2,256]{3,2,0,1:T(2,128)(2,1)S(1)} collective-permute-done((bf16[40,2,2,256]{3,2,0,1:T(2,128)(2,1)S(1)}, bf16[40,2,2,256]{3,2,0,1:T(2,128)(2,1)S(1)}, u32[]{:S(2)}, u32[]{:S(2)}) %collective-permute-start.13) | collective-permute-done | bytes 81952 | tf_op jit(solution)/shard_map/ppermute | solution.py:10
  169.3 1.9 collective-permute-start.14
  171.3 9.8 %collective-permute-done.14 = bf16[40,2,2,256]{3,2,0,1:T(2,128)(2,1)S(1)} collective-permute-done((bf16[40,2,2,256]{3,2,0,1:T(2,128)(2,1)S(1)}, bf16[40,2,2,256]{3,2,0,1:T(2,128)(2,1)S(1)}, u32[]{:S(2)}, u32[]{:S(2)}) %collective-permute-start.14) | collective-permute-done | bytes 81952 | tf_op jit(solution)/shard_map/ppermute | solution.py:10
  181.2 1.9 collective-permute-start.15
  183.1 9.8 %collective-permute-done.15 = bf16[40,2,2,256]{3,2,0,1:T(2,128)(2,1)S(1)} collective-permute-done((bf16[40,2,2,256]{3,2,0,1:T(2,128)(2,1)S(1)}, bf16[40,2,2,256]{3,2,0,1:T(2,128)(2,1)S(1)}, u32[]{:S(2)}, u32[]{:S(2)}) %collective-permute-start.15) | collective-permute-done | bytes 81952 | tf_op jit(solution)/shard_map/ppermute | solution.py:10
  193.0 0.8 fusion.204
  (65 shorter events, 6.7 us)
Async XLA Ops:
  0.0 14.4 %collective-permute-start = (bf16[2,40,2,256]{3,2,1,0:T(2,128)(2,1)}, bf16[2,40,2,256]{3,2,1,0:T(2,128)(2,1)S(1)}, u32[]{:S(2)}, u32[]{:S(2)}) collective-permute-start(bf16[2,40,2,256]{3,2,1,0:T(2,128)(2,1)} %param.18), channel_id=1, source_target_pairs={{0,255},{1,0},{2,1},{3,2},{4,3},{5,4},{6,5},{7,6},{8,7},{9,8},{10,... | collective-permute-start | bytes 245768 | tf_op jit(solution)/shard_map/ppermute | solution.py:10
  14.4 10.3 %collective-permute-start.1 = (bf16[2,40,2,256]{3,2,1,0:T(2,128)(2,1)S(1)}, bf16[2,40,2,256]{3,2,1,0:T(2,128)(2,1)S(1)}, u32[]{:S(2)}, u32[]{:S(2)}) collective-permute-start(bf16[2,40,2,256]{3,2,1,0:T(2,128)(2,1)S(1)} %collective-permute-done), channel_id=1, source_target_pairs={{0,255},{1,0},{2,1},{3,2},{4,3},{5,4},{6,5},{7,6},{8,7},{9,8},{10,... | collective-permute-start | bytes 245768 | tf_op jit(solution)/shard_map/ppermute | solution.py:10
  24.7 11.8 %collective-permute-start.2 = (bf16[2,40,2,256]{3,2,1,0:T(2,128)(2,1)S(1)}, bf16[2,40,2,256]{3,2,1,0:T(2,128)(2,1)S(1)}, u32[]{:S(2)}, u32[]{:S(2)}) collective-permute-start(bf16[2,40,2,256]{3,2,1,0:T(2,128)(2,1)S(1)} %collective-permute-done.1), channel_id=1, source_target_pairs={{0,255},{1,0},{2,1},{3,2},{4,3},{5,4},{6,5},{7,6},{8,7},{9,8},{10,... | collective-permute-start | bytes 245768 | tf_op jit(solution)/shard_map/ppermute | solution.py:10
  36.4 11.8 %collective-permute-start.3 = (bf16[2,40,2,256]{3,2,1,0:T(2,128)(2,1)S(1)}, bf16[2,40,2,256]{3,2,1,0:T(2,128)(2,1)S(1)}, u32[]{:S(2)}, u32[]{:S(2)}) collective-permute-start(bf16[2,40,2,256]{3,2,1,0:T(2,128)(2,1)S(1)} %collective-permute-done.2), channel_id=1, source_target_pairs={{0,255},{1,0},{2,1},{3,2},{4,3},{5,4},{6,5},{7,6},{8,7},{9,8},{10,... | collective-permute-start | bytes 245768 | tf_op jit(solution)/shard_map/ppermute | solution.py:10
  48.2 11.8 %collective-permute-start.4 = (bf16[2,40,2,256]{3,2,1,0:T(2,128)(2,1)S(1)}, bf16[2,40,2,256]{3,2,1,0:T(2,128)(2,1)S(1)}, u32[]{:S(2)}, u32[]{:S(2)}) collective-permute-start(bf16[2,40,2,256]{3,2,1,0:T(2,128)(2,1)S(1)} %collective-permute-done.3), channel_id=1, source_target_pairs={{0,255},{1,0},{2,1},{3,2},{4,3},{5,4},{6,5},{7,6},{8,7},{9,8},{10,... | collective-permute-start | bytes 245768 | tf_op jit(solution)/shard_map/ppermute | solution.py:10
  58.0 26.0 %copy-start = (bf16[2,256,256]{2,1,0:T(8,128)(2,1)S(1)}, bf16[2,256,256]{2,1,0:T(8,128)(2,1)}, u32[]{:S(2)}) copy-start(bf16[2,256,256]{2,1,0:T(8,128)(2,1)} %param.17) | copy-start | bytes 786436
  58.0 26.0 %copy-start.1 = (bf16[256,2,256]{2,1,0:T(2,128)(2,1)S(1)}, bf16[256,2,256]{2,1,0:T(2,128)(2,1)}, u32[]{:S(2)}) copy-start(bf16[256,2,256]{2,1,0:T(2,128)(2,1)} %param.16) | copy-start | bytes 786436
  59.9 11.8 %collective-permute-start.5 = (bf16[2,40,2,256]{3,2,1,0:T(2,128)(2,1)S(1)}, bf16[2,40,2,256]{3,2,1,0:T(2,128)(2,1)S(1)}, u32[]{:S(2)}, u32[]{:S(2)}) collective-permute-start(bf16[2,40,2,256]{3,2,1,0:T(2,128)(2,1)S(1)} %collective-permute-done.4), channel_id=1, source_target_pairs={{0,255},{1,0},{2,1},{3,2},{4,3},{5,4},{6,5},{7,6},{8,7},{9,8},{10,... | collective-permute-start | bytes 245768 | tf_op jit(solution)/shard_map/ppermute | solution.py:10
  71.7 11.8 %collective-permute-start.6 = (bf16[2,40,2,256]{3,2,1,0:T(2,128)(2,1)S(1)}, bf16[2,40,2,256]{3,2,1,0:T(2,128)(2,1)S(1)}, u32[]{:S(2)}, u32[]{:S(2)}) collective-permute-start(bf16[2,40,2,256]{3,2,1,0:T(2,128)(2,1)S(1)} %collective-permute-done.5), channel_id=1, source_target_pairs={{0,255},{1,0},{2,1},{3,2},{4,3},{5,4},{6,5},{7,6},{8,7},{9,8},{10,... | collective-permute-start | bytes 245768 | tf_op jit(solution)/shard_map/ppermute | solution.py:10
  87.6 2.5 %collective-permute-start.7 = (bf16[1,256,2,256]{1,3,2,0:T(8,128)(2,1)S(1)}, bf16[1,256,2,256]{1,3,2,0:T(8,128)(2,1)S(1)}, u32[]{:S(2)}, u32[]{:S(2)}) collective-permute-start(bf16[1,256,2,256]{1,3,2,0:T(8,128)(2,1)S(1)} %copy.49), channel_id=1, source_target_pairs={{0,256},{1,257},{2,258},{3,259},{4,260},{5,261},{6,262},{7,263},{8... | collective-permute-start | bytes 786440 | tf_op jit(solution)/shard_map/ppermute | solution.py:16
  90.1 0.9 copy-start.2
  91.2 11.4 %collective-permute-start.8 = (bf16[1,256,2,256]{1,3,2,0:T(8,128)(2,1)S(1)}, bf16[1,256,2,256]{1,3,2,0:T(8,128)(2,1)S(1)}, u32[]{:S(2)}, u32[]{:S(2)}) collective-permute-start(bf16[1,256,2,256]{1,3,2,0:T(8,128)(2,1)S(1)} %copy.55), channel_id=1, source_target_pairs={{256,0},{257,1},{258,2},{259,3},{260,4},{261,5},{262,6},{263,7},{2... | collective-permute-start | bytes 786440 | tf_op jit(solution)/shard_map/ppermute | solution.py:16
  109.7 12.1 %collective-permute-start.9 = (bf16[40,2,2,256]{3,2,0,1:T(2,128)(2,1)S(1)}, bf16[40,2,2,256]{3,2,0,1:T(2,128)(2,1)S(1)}, u32[]{:S(2)}, u32[]{:S(2)}) collective-permute-start(bf16[40,2,2,256]{3,2,0,1:T(2,128)(2,1)S(1)} %slice.1255), channel_id=1, source_target_pairs={{0,1},{1,2},{2,3},{3,4},{4,5},{5,6},{6,7},{7,8},{8,9},{9,10},{10,1... | collective-permute-start | bytes 245768 | tf_op jit(solution)/shard_map/ppermute | solution.py:10
  121.9 11.8 %collective-permute-start.10 = (bf16[40,2,2,256]{3,2,0,1:T(2,128)(2,1)S(1)}, bf16[40,2,2,256]{3,2,0,1:T(2,128)(2,1)S(1)}, u32[]{:S(2)}, u32[]{:S(2)}) collective-permute-start(bf16[40,2,2,256]{3,2,0,1:T(2,128)(2,1)S(1)} %fusion.198), channel_id=1, source_target_pairs={{0,1},{1,2},{2,3},{3,4},{4,5},{5,6},{6,7},{7,8},{8,9},{9,10},{10,1... | collective-permute-start | bytes 245768 | tf_op jit(solution)/shard_map/ppermute | solution.py:10
  133.8 11.8 %collective-permute-start.11 = (bf16[40,2,2,256]{3,2,0,1:T(2,128)(2,1)S(1)}, bf16[40,2,2,256]{3,2,0,1:T(2,128)(2,1)S(1)}, u32[]{:S(2)}, u32[]{:S(2)}) collective-permute-start(bf16[40,2,2,256]{3,2,0,1:T(2,128)(2,1)S(1)} %fusion.199), channel_id=1, source_target_pairs={{0,1},{1,2},{2,3},{3,4},{4,5},{5,6},{6,7},{7,8},{8,9},{9,10},{10,1... | collective-permute-start | bytes 245768 | tf_op jit(solution)/shard_map/ppermute | solution.py:10
  145.6 11.8 %collective-permute-start.12 = (bf16[40,2,2,256]{3,2,0,1:T(2,128)(2,1)S(1)}, bf16[40,2,2,256]{3,2,0,1:T(2,128)(2,1)S(1)}, u32[]{:S(2)}, u32[]{:S(2)}) collective-permute-start(bf16[40,2,2,256]{3,2,0,1:T(2,128)(2,1)S(1)} %fusion.200), channel_id=1, source_target_pairs={{0,1},{1,2},{2,3},{3,4},{4,5},{5,6},{6,7},{7,8},{8,9},{9,10},{10,1... | collective-permute-start | bytes 245768 | tf_op jit(solution)/shard_map/ppermute | solution.py:10
  157.5 11.8 %collective-permute-start.13 = (bf16[40,2,2,256]{3,2,0,1:T(2,128)(2,1)S(1)}, bf16[40,2,2,256]{3,2,0,1:T(2,128)(2,1)S(1)}, u32[]{:S(2)}, u32[]{:S(2)}) collective-permute-start(bf16[40,2,2,256]{3,2,0,1:T(2,128)(2,1)S(1)} %fusion.201), channel_id=1, source_target_pairs={{0,1},{1,2},{2,3},{3,4},{4,5},{5,6},{6,7},{7,8},{8,9},{9,10},{10,1... | collective-permute-start | bytes 245768 | tf_op jit(solution)/shard_map/ppermute | solution.py:10
  169.3 11.8 %collective-permute-start.14 = (bf16[40,2,2,256]{3,2,0,1:T(2,128)(2,1)S(1)}, bf16[40,2,2,256]{3,2,0,1:T(2,128)(2,1)S(1)}, u32[]{:S(2)}, u32[]{:S(2)}) collective-permute-start(bf16[40,2,2,256]{3,2,0,1:T(2,128)(2,1)S(1)} %fusion.202), channel_id=1, source_target_pairs={{0,1},{1,2},{2,3},{3,4},{4,5},{5,6},{6,7},{7,8},{8,9},{9,10},{10,1... | collective-permute-start | bytes 245768 | tf_op jit(solution)/shard_map/ppermute | solution.py:10
  181.2 11.8 %collective-permute-start.15 = (bf16[40,2,2,256]{3,2,0,1:T(2,128)(2,1)S(1)}, bf16[40,2,2,256]{3,2,0,1:T(2,128)(2,1)S(1)}, u32[]{:S(2)}, u32[]{:S(2)}) collective-permute-start(bf16[40,2,2,256]{3,2,0,1:T(2,128)(2,1)S(1)} %fusion.203), channel_id=1, source_target_pairs={{0,1},{1,2},{2,3},{3,4},{4,5},{5,6},{6,7},{7,8},{8,9},{9,10},{10,1... | collective-permute-start | bytes 245768 | tf_op jit(solution)/shard_map/ppermute | solution.py:10

commit v2 on v1

--- a/solution.py
+++ b/solution.py
@@ -1,3 +1,5 @@
+import functools
+
 import jax
 import jax.numpy as jnp
 from jax import lax
@@ -110,21 +112,37 @@
     return buffer_all
 
 
-def on_device(probe, kernel, object_slab, offsets, counts, intensity):
+def on_device(row_axis, tile_axes, probe, kernel, object_slab, offsets, counts, intensity):
     width = probe.shape[0]
     slot_count = offsets.shape[0]
     local_rows = object_slab.shape[1]
     slice_count = object_slab.shape[0]
     sections = lax.axis_size("section")
     section_now = lax.axis_index("section")
-    tile_now = lax.axis_index("tile")
+    row_size = lax.axis_size(row_axis)
+    tile_count = lax.axis_size(tile_axes)
+    tile_now = lax.axis_index(tile_axes)
+    place = lax.axis_index(row_axis)
     is_last = section_now == sections - 1
     dft_table = dft_matrix(width)
-    reach = (local_rows + width - 2) // local_rows + 1
-    blocks = [object_slab]
-    for step_at in range(1, reach):
-        blocks.append(shifted(blocks[-1], "tile", -1))
-    window = jnp.concatenate(blocks, axis=1)
+    chunk_ids = jnp.arange(row_size, dtype=jnp.int32)
+    later = [object_slab] + [
+        lax.ppermute(
+            object_slab,
+            tile_axes,
+            [(s, (s - ahead * row_size) % tile_count) for s in range(tile_count)],
+        )
+        for ahead in (1, 2)
+    ]
+    own_row = (chunk_ids <= place)[:, None, None, None, None, None]
+    sent = jnp.where(
+        own_row, jnp.stack(later[:2])[None], jnp.stack(later[1:])[None]
+    )
+    got = lax.all_to_all(sent, row_axis, 0, 0)
+    got = lax.dynamic_slice_in_dim(jnp.concatenate((got, got), axis=0), place, row_size, 0)
+    window = jnp.concatenate(
+        [got[at % row_size, at // row_size] for at in range(2 * row_size)], axis=1
+    )
     relative = offsets - tile_now * local_rows
     patches = jax.vmap(lambda offset: lax.dynamic_slice_in_dim(window, offset, width, 1))(relative)
     live_slots = jnp.arange(slot_count, dtype=jnp.int32) < counts[0]
@@ -184,28 +202,53 @@
             gradients,
         )
     gradients = gradients * live_slots.astype(jnp.float32)[:, None, None, None, None]
-    nearby = accumulate(gradients, relative, reach * local_rows)
-    own_rows = nearby[(reach - 1) * local_rows : reach * local_rows]
-    for step_at in reversed(range(reach - 1)):
-        block_rows = nearby[step_at * local_rows : (step_at + 1) * local_rows]
-        own_rows = block_rows + shifted(own_rows.astype(jnp.bfloat16), "tile", 1).astype(
-            block_rows.dtype
-        )
+    nearby = accumulate(gradients, offsets - tile_now * local_rows, 2 * row_size * local_rows)
+    tiles = jnp.stack(
+        [nearby[at * local_rows : (at + 1) * local_rows] for at in range(2 * row_size)], axis=0
+    ).astype(jnp.bfloat16)
+    tiles = tiles.reshape((2, row_size) + tiles.shape[1:]).swapaxes(0, 1)
+    tiles = jnp.concatenate((tiles, tiles), axis=0)
+    outgoing = lax.dynamic_slice_in_dim(tiles, row_size - place, row_size, 0)
+    incoming = lax.all_to_all(outgoing, row_axis, 0, 0).astype(jnp.float32)
+    same = (chunk_ids <= place)[:, None, None, None, None]
+    first = incoming[:, 0]
+    second = incoming[:, 1]
+    own_rows = jnp.sum(jnp.where(same, first, 0.0), axis=0)
+    spills = [
+        jnp.sum(jnp.where(same, second, first), axis=0),
+        jnp.sum(jnp.where(same, 0.0, second), axis=0),
+    ]
+    for ahead, spill in zip((1, 2), spills):
+        own_rows = own_rows + lax.ppermute(
+            spill.astype(jnp.bfloat16),
+            tile_axes,
+            [(s, (s + ahead * row_size) % tile_count) for s in range(tile_count)],
+        ).astype(jnp.float32)
     return jnp.transpose(own_rows, (1, 0, 2, 3))
 
 
+def row_length(devices):
+    places = sorted({device.coords[0] for device in devices})
+    return len(places)
+
+
 def solution(mesh):
+    sections, tiles = mesh.devices.shape
+    row_size = row_length(list(mesh.devices[0]))
+    grid = mesh.devices.reshape(sections, tiles // row_size, row_size)
+    grid_mesh = jax.sharding.Mesh(grid, ("section", "lines", "x"))
+    tile_axes = ("lines", "x")
     return jax.shard_map(
-        on_device,
-        mesh=mesh,
+        functools.partial(on_device, "x", tile_axes),
+        mesh=grid_mesh,
         in_specs=(
             P(),
             P(),
-            P("section", "tile", None, None),
-            P("tile"),
-            P("tile"),
-            P("tile", None, None),
-        ),
-        out_specs=P("section", "tile", None, None),
+            P("section", tile_axes, None, None),
+            P(tile_axes),
+            P(tile_axes),
+            P(tile_axes, None, None),
+        ),
+        out_specs=P("section", tile_axes, None, None),
         check_vma=False,
     )

time: 194 us -> 90.8 us (0.47)
  the two profiles are of different devices: /device:TPU:0 before, /device:TPU:2 now
where the time goes in v2:
time: 90.8 us; the launch traced here: 90.3 us
  starting transfers between devices  30.8 us (34%)
  waiting for transfers between devices  29.1 us (32%)
  blocking collectives  11.2 us (12%)
  local copies, waits for them, and re-layouts  7.17 us (8%)
  other arithmetic  5.84 us (6%)
  matrix products  4.2 us (5%)
  between operations  1.72 us (2%)
    ppermute x2, starting transfers between devices, on_device(): lax.ppermute(object_slab, tile_axes, [(s, (s - ahead * row_size) % tile_c...  17.9 us
    all_to_all x1, blocking collectives, on_device(): incoming = lax.all_to_all(outgoing, row_axis, 0, 0).astype(jnp.float32)  11.2 us
    ppermute x2, waiting for transfers between devices, passed_along(): return lax.ppermute(shard, axis, pairs)  9.44 us
    ppermute x2, waiting for transfers between devices, on_device(): lax.ppermute(spill.astype(jnp.bfloat16), tile_axes, [(s, (s + ahead * row...  9.12 us
    all_to_all x1, waiting for transfers between devices, on_device(): got = lax.all_to_all(sent, row_axis, 0, 0)  7.2 us
    ppermute x2, starting transfers between devices, on_device(): lax.ppermute(spill.astype(jnp.bfloat16), tile_axes, [(s, (s + ahead * row...  5.47 us
    all_to_all x1, starting transfers between devices, on_device(): got = lax.all_to_all(sent, row_axis, 0, 0)  4.82 us
    dot_general x16, matrix products, product(): return jnp.einsum(form, first, second, preferred_element_type=jnp.float32)  4.2 us
  transfers between devices with their start and end apart: 7, of which 5 were waited for; matrix products, arithmetic and copies ran while one was open for 1% of the time, Pallas kernels for 0%

profile of v2, /device:TPU:2, one launch (start us, length us, event | category | flops | bytes accessed | tf_op | source)
XLA Modules:
  0.0 90.3 jit_solution(7155720681381344707)
XLA Ops:
  0.0 13.8 %collective-permute-start = (bf16[2,40,2,256]{3,2,1,0:T(2,128)(2,1)}, bf16[2,40,2,256]{3,2,1,0:T(2,128)(2,1)S(1)}, u32[]{:S(2)}, u32[]{:S(2)}) collective-permute-start(bf16[2,40,2,256]{3,2,1,0:T(2,128)(2,1)} %param.18), channel_id=1, source_target_pairs={{0,252},{1,253},{2,254},{3,255},{4,0},{5,1},{6,2},{7,3},{8,4},{9,5... | collective-permute-start | bytes 245768 | tf_op jit(solution)/shard_map/ppermute | solution.py:130
  13.9 4.1 %collective-permute-start.1 = (bf16[2,40,2,256]{3,2,1,0:T(2,128)(2,1)}, bf16[2,40,2,256]{3,2,1,0:T(2,128)(2,1)S(1)}, u32[]{:S(2)}, u32[]{:S(2)}) collective-permute-start(bf16[2,40,2,256]{3,2,1,0:T(2,128)(2,1)} %param.18), channel_id=1, source_target_pairs={{0,248},{1,249},{2,250},{3,251},{4,252},{5,253},{6,254},{7,255},{8... | collective-permute-start | bytes 245768 | tf_op jit(solution)/shard_map/ppermute | solution.py:130
  17.9 3.4 %collective-permute-done.1 = bf16[2,40,2,256]{3,2,1,0:T(2,128)(2,1)S(1)} collective-permute-done((bf16[2,40,2,256]{3,2,1,0:T(2,128)(2,1)}, bf16[2,40,2,256]{3,2,1,0:T(2,128)(2,1)S(1)}, u32[]{:S(2)}, u32[]{:S(2)}) %collective-permute-start.1) | collective-permute-done | bytes 81952 | tf_op jit(solution)/shard_map/ppermute | solution.py:130
  21.3 1.2 %pad_maximum_fusion.55 = (bf16[2,2,40,2,256]{4,3,2,1,0:T(2,128)(2,1)S(1)}, bf16[2,2,40,2,256]{4,3,2,1,0:T(2,128)(2,1)S(1)}) fusion(bf16[1,2,40,2,256]{4,3,2,1,0:T(2,128)(2,1)S(1)} %bitcast.484, bf16[1,2,40,2,256]{4,3,2,1,0:T(2,128)(2,1)} %bitcast.483, bf16[1,2,40,2,256]{4,3,2,1,0:T(2,128)(2,1)S(1)} %bitcast.485), kind=kLoop, calls=%fused_computation.363 | loop fusion | flops 163840 | bytes 573440 | tf_op jit(solution)/shard_map/stack | solution.py:139
  22.6 0.9 %broadcast_select_fusion = bf16[4,2,2,40,2,256]{5,3,4,2,1,0:T(8,128)(2,1)} fusion(pred[4]{0:T(512)(128)(4,1)S(1)} %iota_compare_fusion, bf16[2,2,40,2,256]{4,2,3,1,0:T(8,128)(2,1)S(1)} %copy.148, bf16[2,2,40,2,256]{4,2,3,1,0:T(8,128)(2,1)S(1)} %copy.147), kind=kLoop, calls=%fused_computation.348 | loop fusion | flops 327680 | bytes 983044 | tf_op jit(solution)/shard_map/jit(_where)/select_n | solution.py:138
  23.6 4.8 %all-to-all-start = ((bf16[4,2,2,40,2,256]{5,3,4,2,1,0:T(8,128)(2,1)}), bf16[4,2,2,40,2,256]{5,3,4,2,1,0:T(8,128)(2,1)S(1)}, u32[]{:S(2)}, u32[]{:S(2)}) async-start(bf16[4,2,2,40,2,256]{5,3,4,2,1,0:T(8,128)(2,1)} %broadcast_select_fusion), calls=%async_computation | async-start | bytes 1310720 | tf_op jit(solution)/shard_map/all_to_all | solution.py:141
  28.4 0.2 copy.146
  29.3 7.2 %all-to-all-done = bf16[4,2,2,40,2,256]{5,3,4,2,1,0:T(8,128)(2,1)S(1)} async-done(((bf16[4,2,2,40,2,256]{5,3,4,2,1,0:T(8,128)(2,1)}), bf16[4,2,2,40,2,256]{5,3,4,2,1,0:T(8,128)(2,1)S(1)}, u32[]{:S(2)}, u32[]{:S(2)}) %all-to-all-start) | async-done | bytes 655392 | tf_op jit(solution)/shard_map/all_to_all | solution.py:141
  36.5 0.2 fusion.193
  37.0 0.7 copy-done
  37.7 3.5 %conditional.5 = (bf16[1,256,2,256]{3,1,2,0:T(8,128)(2,1)S(1)}, bf16[1,2,256,2,256]{2,4,3,1,0:T(8,128)(2,1)S(1)}) conditional(s32[]{:T(128)} %convert_element_type.389, bf16[1,256,2,256]{3,1,2,0:T(8,128)(2,1)S(1)} %bitcast.479, (bf16[1,256,2,256]{1,3,2,0:T(8,128)(2,1)S(1)}, bf16[1,2,256,2,256]{4,2,3,1,0:T(8,128)(2,1)S(1)}, ...), branch_computations={%region_0.1_spmd, %region_1.2_spmd} | conditional | flops 541327360 | bytes 22544400 | solution.py:184
  37.7 0.2 copy.150
  38.1 0.3 convolution_bitcast_fusion.7
  38.3 0.3 convolution_bitcast_fusion.6
  38.7 0.3 convolution_bitcast_fusion.5
  39.0 0.3 convolution_bitcast_fusion.4
  39.4 0.2 copy.118
  39.8 0.3 convolution_bitcast_fusion.3
  40.1 0.3 convolution_bitcast_fusion.2
  40.5 0.3 convolution_bitcast_fusion.1
  40.7 0.3 convolution_bitcast_fusion
  41.3 1.3 %collective-permute-start.2 = (bf16[1,256,2,256]{1,3,2,0:T(8,128)(2,1)S(1)}, bf16[1,256,2,256]{1,3,2,0:T(8,128)(2,1)S(1)}, u32[]{:S(2)}, u32[]{:S(2)}) collective-permute-start(bf16[1,256,2,256]{1,3,2,0:T(8,128)(2,1)S(1)} %copy.152), channel_id=1, source_target_pairs={{0,256},{1,257},{2,258},{3,259},{4,260},{5,261},{6,262},{7,263},{8... | collective-permute-start | bytes 786440 | tf_op jit(solution)/shard_map/ppermute | solution.py:18
  42.6 1.1 %multiply_convert_fusion = (bf16[1,256,256]{2,1,0:T(8,128)(2,1)S(1)}, bf16[1,256,256]{2,1,0:T(8,128)(2,1)S(1)}) fusion(), kind=kLoop, calls=%fused_computation.358 | loop fusion | flops 1245184 | bytes 262144 | tf_op jit(solution)/shard_map/convert.121
  43.8 0.2 conditional.6
  43.9 0.7 copy-done.2
  44.9 1.3 %collective-permute-start.3 = (bf16[1,256,2,256]{1,3,2,0:T(8,128)(2,1)S(1)}, bf16[1,256,2,256]{1,3,2,0:T(8,128)(2,1)S(1)}, u32[]{:S(2)}, u32[]{:S(2)}) collective-permute-start(bf16[1,256,2,256]{1,3,2,0:T(8,128)(2,1)S(1)} %copy.158), channel_id=1, source_target_pairs={{256,0},{257,1},{258,2},{259,3},{260,4},{261,5},{262,6},{263,7},{2... | collective-permute-start | bytes 786440 | tf_op jit(solution)/shard_map/ppermute | solution.py:18
  46.9 9.4 %collective-permute-done.3 = bf16[1,256,2,256]{1,3,2,0:T(8,128)(2,1)S(1)} collective-permute-done((bf16[1,256,2,256]{1,3,2,0:T(8,128)(2,1)S(1)}, bf16[1,256,2,256]{1,3,2,0:T(8,128)(2,1)S(1)}, u32[]{:S(2)}, u32[]{:S(2)}) %collective-permute-start.3) | collective-permute-done | bytes 262176 | tf_op jit(solution)/shard_map/ppermute | solution.py:18
  56.3 3.1 %conditional.9 = (f32[1,2,256,2,256]{4,2,3,1,0:T(8,128)S(1)}) conditional(s32[]{:T(128)} %convert_element_type.389, f32[1,2,256,2,256]{4,2,3,1,0:T(8,128)S(1)} %get-tuple-element.91, (bf16[1,2,256,2,256]{2,4,3,1,0:T(8,128)(2,1)S(1)}, bf16[1,2,256,2,256]{4,2,3,1,0:T(8,128)(2,1)S(1)}, bf16[1,256,2,256]{1,3,2,0:T(8,128)(2,1)S(1)}, ...), branch_computations={%region_8.9_spmd, %region_9.10_spmd} | conditional | flops 540672000 | bytes 24117256 | solution.py:197
  56.3 0.2 convolution_bitcast_fusion.30
  56.5 0.2 convolution_bitcast_fusion.31
  56.8 0.3 convolution_bitcast_fusion.28
  57.1 0.3 convolution_bitcast_fusion.29
  57.4 0.2 copy.159
  57.6 0.1 fusion.120
  58.0 0.3 convolution_bitcast_fusion.27
  58.2 0.3 convolution_bitcast_fusion.26
  58.6 0.3 convolution_bitcast_fusion.25
  58.9 0.3 convolution_bitcast_fusion.24
  59.6 3.3 %dynamic_update_slice.3 = bf16[320,2,2,256]{3,0,2,1:T(8,128)(2,1)S(1)} dynamic-update-slice(bf16[320,2,2,256]{3,0,2,1:T(8,128)(2,1)S(1)} %broadcast_in_dim.77, bf16[256,2,2,256]{3,0,2,1:T(8,128)(2,1)S(1)} %multiply_bitcast_fusion, s32[]{:T(128)S(6)} %select_n.52, s32[]{:T(128)} %constant.28.clone.1, s32[]{:T(128)} %constant.28.clone.1, s32[]{:T(128)} %constant.28.clone.1) | dynamic-update-slice | bytes 1048580 | tf_op jit(solution)/shard_map/dynamic_update_slice | solution.py:111
  63.0 0.3 fusion.192
  63.3 11.2 %all_to_all.10 = bf16[4,2,40,2,2,256]{5,2,4,3,1,0:T(8,128)(2,1)S(1)} all-to-all(bf16[4,2,40,2,2,256]{5,2,4,3,1,0:T(8,128)(2,1)S(1)} %copy.160), channel_id=1, replica_groups=mesh['section'=2,'lines'=64,'x'=4] {'x'}, dimensions={0} | all-to-all | bytes 1310720 | tf_op jit(solution)/shard_map/all_to_all | solution.py:212
  74.6 0.2 convert_element_type.393
  74.7 0.2 select_reduce_fusion.1
  75.0 3.5 %collective-permute-start.4 = (bf16[40,2,2,256]{3,0,2,1:T(8,128)(2,1)S(1)}, bf16[40,2,2,256]{3,0,2,1:T(8,128)(2,1)S(1)}, u32[]{:S(2)}, u32[]{:S(2)}) collective-permute-start(bf16[40,2,2,256]{3,0,2,1:T(8,128)(2,1)S(1)} %get-tuple-element.187), channel_id=1, source_target_pairs={{0,4},{1,5},{2,6},{3,7},{4,8},{5,9},{6,10},{7,11},{8,12},{9,13},{1... | collective-permute-start | bytes 245768 | tf_op jit(solution)/shard_map/ppermute | solution.py:222
  78.5 1.9 %collective-permute-start.5 = (bf16[40,2,2,256]{3,0,2,1:T(8,128)(2,1)S(1)}, bf16[40,2,2,256]{3,0,2,1:T(8,128)(2,1)S(1)}, u32[]{:S(2)}, u32[]{:S(2)}) collective-permute-start(bf16[40,2,2,256]{3,0,2,1:T(8,128)(2,1)S(1)} %get-tuple-element.188), channel_id=1, source_target_pairs={{0,8},{1,9},{2,10},{3,11},{4,12},{5,13},{6,14},{7,15},{8,16},{9,17... | collective-permute-start | bytes 245768 | tf_op jit(solution)/shard_map/ppermute | solution.py:222
  80.4 5.7 %collective-permute-done.4 = bf16[40,2,2,256]{3,0,2,1:T(8,128)(2,1)S(1)} collective-permute-done((bf16[40,2,2,256]{3,0,2,1:T(8,128)(2,1)S(1)}, bf16[40,2,2,256]{3,0,2,1:T(8,128)(2,1)S(1)}, u32[]{:S(2)}, u32[]{:S(2)}) %collective-permute-start.4) | collective-permute-done | bytes 81952 | tf_op jit(solution)/shard_map/ppermute | solution.py:222
  86.2 3.4 %collective-permute-done.5 = bf16[40,2,2,256]{3,0,2,1:T(8,128)(2,1)S(1)} collective-permute-done((bf16[40,2,2,256]{3,0,2,1:T(8,128)(2,1)S(1)}, bf16[40,2,2,256]{3,0,2,1:T(8,128)(2,1)S(1)}, u32[]{:S(2)}, u32[]{:S(2)}) %collective-permute-start.5) | collective-permute-done | bytes 81952 | tf_op jit(solution)/shard_map/ppermute | solution.py:222
  89.6 0.8 copy.162
  (59 shorter events, 2.6 us)
Async XLA Ops:
  0.0 17.9 %collective-permute-start = (bf16[2,40,2,256]{3,2,1,0:T(2,128)(2,1)}, bf16[2,40,2,256]{3,2,1,0:T(2,128)(2,1)S(1)}, u32[]{:S(2)}, u32[]{:S(2)}) collective-permute-start(bf16[2,40,2,256]{3,2,1,0:T(2,128)(2,1)} %param.18), channel_id=1, source_target_pairs={{0,252},{1,253},{2,254},{3,255},{4,0},{5,1},{6,2},{7,3},{8,4},{9,5... | collective-permute-start | bytes 245768 | tf_op jit(solution)/shard_map/ppermute | solution.py:130
  13.9 7.5 %collective-permute-start.1 = (bf16[2,40,2,256]{3,2,1,0:T(2,128)(2,1)}, bf16[2,40,2,256]{3,2,1,0:T(2,128)(2,1)S(1)}, u32[]{:S(2)}, u32[]{:S(2)}) collective-permute-start(bf16[2,40,2,256]{3,2,1,0:T(2,128)(2,1)} %param.18), channel_id=1, source_target_pairs={{0,248},{1,249},{2,250},{3,251},{4,252},{5,253},{6,254},{7,255},{8... | collective-permute-start | bytes 245768 | tf_op jit(solution)/shard_map/ppermute | solution.py:130
  22.6 5.8 %copy-start.1 = (bf16[256,2,256]{2,1,0:T(2,128)(2,1)S(1)}, bf16[256,2,256]{2,1,0:T(2,128)(2,1)}, u32[]{:S(2)}) copy-start(bf16[256,2,256]{2,1,0:T(2,128)(2,1)} %param.16) | copy-start | bytes 786436
  23.6 12.9 %all-to-all-start = ((bf16[4,2,2,40,2,256]{5,3,4,2,1,0:T(8,128)(2,1)}), bf16[4,2,2,40,2,256]{5,3,4,2,1,0:T(8,128)(2,1)S(1)}, u32[]{:S(2)}, u32[]{:S(2)}) async-start(bf16[4,2,2,40,2,256]{5,3,4,2,1,0:T(8,128)(2,1)} %broadcast_select_fusion), calls=%async_computation | async-start | bytes 1310720 | tf_op jit(solution)/shard_map/all_to_all | solution.py:141
  36.7 1.0 %copy-start = (bf16[2,256,256]{2,1,0:T(8,128)(2,1)S(1)}, bf16[2,256,256]{2,1,0:T(8,128)(2,1)}, u32[]{:S(2)}) copy-start(bf16[2,256,256]{2,1,0:T(8,128)(2,1)} %param.17) | copy-start | bytes 786436
  41.3 2.5 %collective-permute-start.2 = (bf16[1,256,2,256]{1,3,2,0:T(8,128)(2,1)S(1)}, bf16[1,256,2,256]{1,3,2,0:T(8,128)(2,1)S(1)}, u32[]{:S(2)}, u32[]{:S(2)}) collective-permute-start(bf16[1,256,2,256]{1,3,2,0:T(8,128)(2,1)S(1)} %copy.152), channel_id=1, source_target_pairs={{0,256},{1,257},{2,258},{3,259},{4,260},{5,261},{6,262},{7,263},{8... | collective-permute-start | bytes 786440 | tf_op jit(solution)/shard_map/ppermute | solution.py:18
  43.8 0.9 %copy-start.2 = (bf16[1,256,256]{2,1,0:T(8,128)(2,1)S(1)}, bf16[1,256,256]{2,1,0:T(8,128)(2,1)}, u32[]{:S(2)}) copy-start(bf16[1,256,256]{2,1,0:T(8,128)(2,1)} %param.21) | copy-start | bytes 393220
  44.9 11.4 %collective-permute-start.3 = (bf16[1,256,2,256]{1,3,2,0:T(8,128)(2,1)S(1)}, bf16[1,256,2,256]{1,3,2,0:T(8,128)(2,1)S(1)}, u32[]{:S(2)}, u32[]{:S(2)}) collective-permute-start(bf16[1,256,2,256]{1,3,2,0:T(8,128)(2,1)S(1)} %copy.158), channel_id=1, source_target_pairs={{256,0},{257,1},{258,2},{259,3},{260,4},{261,5},{262,6},{263,7},{2... | collective-permute-start | bytes 786440 | tf_op jit(solution)/shard_map/ppermute | solution.py:18
  75.0 11.2 %collective-permute-start.4 = (bf16[40,2,2,256]{3,0,2,1:T(8,128)(2,1)S(1)}, bf16[40,2,2,256]{3,0,2,1:T(8,128)(2,1)S(1)}, u32[]{:S(2)}, u32[]{:S(2)}) collective-permute-start(bf16[40,2,2,256]{3,0,2,1:T(8,128)(2,1)S(1)} %get-tuple-element.187), channel_id=1, source_target_pairs={{0,4},{1,5},{2,6},{3,7},{4,8},{5,9},{6,10},{7,11},{8,12},{9,13},{1... | collective-permute-start | bytes 245768 | tf_op jit(solution)/shard_map/ppermute | solution.py:222
  78.5 11.0 %collective-permute-start.5 = (bf16[40,2,2,256]{3,0,2,1:T(8,128)(2,1)S(1)}, bf16[40,2,2,256]{3,0,2,1:T(8,128)(2,1)S(1)}, u32[]{:S(2)}, u32[]{:S(2)}) collective-permute-start(bf16[40,2,2,256]{3,0,2,1:T(8,128)(2,1)S(1)} %get-tuple-element.188), channel_id=1, source_target_pairs={{0,8},{1,9},{2,10},{3,11},{4,12},{5,13},{6,14},{7,15},{8,16},{9,17... | collective-permute-start | bytes 245768 | tf_op jit(solution)/shard_map/ppermute | solution.py:222

commit v3 on v2

--- a/solution.py
+++ b/solution.py
@@ -30,52 +30,42 @@
     return jnp.einsum(form, first, second, preferred_element_type=jnp.float32)
 
 
-def apply_left(matrix, field):
-    first_part = product("ij,...jck->...ick", matrix[0], field)
-    second_part = product("ij,...jck->...ick", matrix[1], field)
-    return jnp.stack(
-        (
-            first_part[..., 0, :] - second_part[..., 1, :],
-            first_part[..., 1, :] + second_part[..., 0, :],
-        ),
-        axis=-2,
-    )
-
-
-def apply_left_adj(matrix, field):
-    first_part = product("ji,...jck->...ick", matrix[0], field)
-    second_part = product("ji,...jck->...ick", matrix[1], field)
-    return jnp.stack(
-        (
-            first_part[..., 0, :] + second_part[..., 1, :],
-            first_part[..., 1, :] - second_part[..., 0, :],
-        ),
-        axis=-2,
-    )
-
-
-def apply_right(field, matrix):
-    first_part = product("...ick,lk->...icl", field, matrix[0])
-    second_part = product("...ick,lk->...icl", field, matrix[1])
-    return jnp.stack(
-        (
-            first_part[..., 0, :] - second_part[..., 1, :],
-            second_part[..., 0, :] + first_part[..., 1, :],
-        ),
-        axis=-2,
-    )
-
-
-def apply_right_conj(field, matrix):
-    first_part = product("...ick,kl->...icl", field, matrix[0])
-    second_part = product("...ick,kl->...icl", field, matrix[1])
-    return jnp.stack(
-        (
-            first_part[..., 0, :] + second_part[..., 1, :],
-            first_part[..., 1, :] - second_part[..., 0, :],
-        ),
-        axis=-2,
-    )
+def left_block(real, imag):
+    top = jnp.stack((real, -imag), axis=-1)
+    bottom = jnp.stack((imag, real), axis=-1)
+    side = real.shape[0]
+    return jnp.stack((top, bottom), axis=1).reshape(2 * side, 2 * side)
+
+
+def right_block(real, imag):
+    upper = jnp.stack((real, imag), axis=1)
+    lower = jnp.stack((-imag, real), axis=1)
+    side = real.shape[0]
+    return jnp.stack((upper, lower), axis=0).reshape(2 * side, 2 * side)
+
+
+def blocks_of(matrix):
+    real, imag = matrix[0], matrix[1]
+    return {
+        "left": left_block(real, imag),
+        "left_adj": left_block(real.T, -imag.T),
+        "right": right_block(real.T, imag.T),
+        "right_conj": right_block(real, -imag),
+    }
+
+
+def apply_left(block, field):
+    lead = field.shape[:-3]
+    rows, parts, width = field.shape[-3:]
+    flat = field.reshape(lead + (rows * parts, width))
+    return product("ab,...bk->...ak", block, flat).reshape(field.shape)
+
+
+def apply_right(field, block):
+    lead = field.shape[:-3]
+    rows, parts, width = field.shape[-3:]
+    flat = field.reshape(lead + (rows, parts * width))
+    return product("...ia,ab->...ib", flat, block).reshape(field.shape)
 
 
 def complex_mul(first, second):
@@ -102,14 +92,11 @@
 
 
 def accumulate(gradients, starts, buffer_rows):
-    slot_count, slice_count, width = (gradients.shape[0], gradients.shape[1], gradients.shape[-1])
-    buffer_all = jnp.zeros((buffer_rows, slice_count, 2, width), jnp.float32)
-    for slot_at in range(slot_count):
-        start_row = starts[slot_at]
-        current = lax.dynamic_slice_in_dim(buffer_all, start_row, width, 0)
-        placed = jnp.transpose(gradients[slot_at], (1, 0, 2, 3))
-        buffer_all = lax.dynamic_update_slice_in_dim(buffer_all, current + placed, start_row, 0)
-    return buffer_all
+    width = gradients.shape[-1]
+    margin = buffer_rows - width
+    placed = jnp.transpose(gradients[0], (1, 0, 2, 3))
+    padded = jnp.pad(placed, ((margin, margin), (0, 0), (0, 0), (0, 0)))
+    return lax.dynamic_slice_in_dim(padded, margin - starts[0], buffer_rows, 0)
 
 
 def on_device(row_axis, tile_axes, probe, kernel, object_slab, offsets, counts, intensity):
@@ -124,7 +111,8 @@
     tile_now = lax.axis_index(tile_axes)
     place = lax.axis_index(row_axis)
     is_last = section_now == sections - 1
-    dft_table = dft_matrix(width)
+    dft_table = blocks_of(dft_matrix(width))
+    kernel = blocks_of(kernel)
     chunk_ids = jnp.arange(row_size, dtype=jnp.int32)
     later = [object_slab] + [
         lax.ppermute(
@@ -154,23 +142,23 @@
             phase = complex_mul(field_now, patches_here[..., slice_at, :, :, :]).astype(
                 jnp.bfloat16
             )
-            middle = apply_left(kernel, phase).astype(jnp.bfloat16)
-            field_now = apply_right(middle, kernel).astype(jnp.bfloat16)
+            middle = apply_left(kernel["left"], phase).astype(jnp.bfloat16)
+            field_now = apply_right(middle, kernel["right"]).astype(jnp.bfloat16)
         return (field_now, jnp.stack(incidents, axis=-4))
 
     def far_adjoint(field_now, measured):
-        half_far = apply_left(dft_table, field_now).astype(jnp.bfloat16)
-        far = apply_right(half_far, dft_table)
+        half_far = apply_left(dft_table["left"], field_now).astype(jnp.bfloat16)
+        far = apply_right(half_far, dft_table["right"])
         misfit = far[..., 0, :] ** 2 + far[..., 1, :] ** 2 - measured.astype(jnp.float32)
         grad_far = (far * misfit[..., None, :]).astype(jnp.bfloat16)
-        half_back = apply_left_adj(dft_table, grad_far).astype(jnp.bfloat16)
-        return apply_right_conj(half_back, dft_table).astype(jnp.bfloat16)
+        half_back = apply_left(dft_table["left_adj"], grad_far).astype(jnp.bfloat16)
+        return apply_right(half_back, dft_table["right_conj"]).astype(jnp.bfloat16)
 
     def retreat(adjoint, patches_here, incidents):
         gradients = []
         for slice_at in reversed(range(slice_count)):
-            middle = apply_left_adj(kernel, adjoint).astype(jnp.bfloat16)
-            phibar = apply_right_conj(middle, kernel)
+            middle = apply_left(kernel["left_adj"], adjoint).astype(jnp.bfloat16)
+            phibar = apply_right(middle, kernel["right_conj"])
             gradients.append(conj_mul(incidents[..., slice_at, :, :, :], phibar))
             adjoint = conj_mul(patches_here[..., slice_at, :, :, :], phibar).astype(jnp.bfloat16)
         return (adjoint, jnp.stack(gradients[::-1], axis=-4))

time: 90.8 us -> 419 us (4.61)
  waiting for transfers between devices: 29.1 us -> 184 us
  local copies, waits for them, and re-layouts: 7.17 us -> 159 us
  other arithmetic: 5.84 us -> 27.3 us
    ppermute x2, waiting for transfers between devices: 9.44 us -> 176 us  [passed_along(): return lax.ppermute(shard, axis, pairs)]
    reshape x0 -> x2, local copies, waits for them, and re-layouts: none -> 97.9 us  [left_block(): return jnp.stack((top, bottom), axis=1).reshape(2 * side, 2 * side)]
    another operation x5 -> x12, local copies, waits for them, and re-layouts: 0.78 us -> 50.2 us  [the longest x2 47.2 us: left_block(): return jnp.stack((top, bottom), axis=1).reshape(2 * side, 2 * side)]
    another operation x9 -> x24, other arithmetic: 1.68 us -> 11.6 us  [the longest x8 3.79 us: right_block(): return jnp.stack((upper, lower), axis=0).reshape(2 * side, 2 * side)]
    all_to_all x1, waiting for transfers between devices: 7.2 us -> 0.01 us  [on_device(): got = lax.all_to_all(sent, row_axis, 0, 0)]
    neg x0 -> x4, other arithmetic: none -> 4.23 us  [left_block(): top = jnp.stack((real, -imag), axis=-1)]
  transfers between devices with their start and end apart: 7 -> 7, of which waited for: 5 -> 3; matrix products, arithmetic and copies ran while one was open for 1% -> 40% of each run, Pallas kernels for 0% -> 0%
where the time goes in v3:
time: 419 us; the launch traced here: 417 us
  waiting for transfers between devices  184 us (44%)
  local copies, waits for them, and re-layouts  159 us (38%)
  starting transfers between devices  30.1 us (7%)
  other arithmetic  27.3 us (7%)
  blocking collectives  11.9 us (3%)
    ppermute x2, waiting for transfers between devices, passed_along(): return lax.ppermute(shard, axis, pairs)  176 us
    reshape x2, local copies, waits for them, and re-layouts, left_block(): return jnp.stack((top, bottom), axis=1).reshape(2 * side, 2 * side)  97.9 us
    another operation x2, local copies, waits for them, and re-layouts, left_block(): return jnp.stack((top, bottom), axis=1).reshape(2 * side, 2 * side)  47.2 us
    ppermute x2, starting transfers between devices, on_device(): lax.ppermute(object_slab, tile_axes, [(s, (s - ahead * row_size) % tile_c...  18 us
    all_to_all x1, blocking collectives, on_device(): incoming = lax.all_to_all(outgoing, row_axis, 0, 0).astype(jnp.float32)  11.9 us
  transfers between devices with their start and end apart: 7, of which 3 were waited for; matrix products, arithmetic and copies ran while one was open for 40% of the time, Pallas kernels for 0%

profile of v3, /device:TPU:2, one launch (start us, length us, event | category | flops | bytes accessed | tf_op | source)
XLA Modules:
  0.0 417.3 jit_solution(8492155427917605434)
XLA Ops:
  0.0 14.0 %collective-permute-start = (bf16[2,40,2,256]{3,2,1,0:T(2,128)(2,1)}, bf16[2,40,2,256]{3,2,1,0:T(2,128)(2,1)}, u32[]{:S(2)}, u32[]{:S(2)}) collective-permute-start(bf16[2,40,2,256]{3,2,1,0:T(2,128)(2,1)} %param.18), channel_id=1, source_target_pairs={{0,252},{1,253},{2,254},{3,255},{4,0},{5,1},{6,2},{7,3},{8,4},{9,5... | collective-permute-start | bytes 245768 | tf_op jit(solution)/shard_map/ppermute | solution.py:118
  14.0 4.0 collective-permute-start.1
  18.0 0.9 fusion.53
  19.0 1.0 slice_bitcast_fusion.24
  20.1 1.7 fusion.51
  21.7 1.8 fusion.26
  23.5 1.8 fusion.24
  25.2 1.6 fusion.32
  26.9 1.1 fusion.23
  28.0 1.0 fusion.31
  30.1 0.8 pad_maximum_fusion.13
  31.0 0.9 pad_maximum_fusion.14
  31.9 0.8 pad_maximum_fusion.15
  32.9 1.4 pad_maximum_fusion.19
  34.4 1.0 broadcast_select_fusion
  35.4 4.8 %all-to-all-start = ((bf16[4,2,2,40,2,256]{5,3,4,2,1,0:T(8,128)(2,1)}), bf16[4,2,2,40,2,256]{5,3,4,2,1,0:T(8,128)(2,1)S(1)}, u32[]{:S(2)}, u32[]{:S(2)}) async-start(bf16[4,2,2,40,2,256]{5,3,4,2,1,0:T(8,128)(2,1)} %broadcast_select_fusion), calls=%async_computation | async-start | bytes 1310720 | tf_op jit(solution)/shard_map/all_to_all | solution.py:129
  40.2 1.7 fusion.25
  42.6 0.7 copy.147
  43.4 23.0 %copy.117 = bf16[256,2,256,2]{3,2,1,0:T(8,128)(2,1)} copy(bf16[256,2,256,2]{2,0,3,1:T(8,128)(2,1)S(1)} %pad_maximum_fusion.11) | data formatting | bytes 1048576 | tf_op jit(solution)/shard_map/stack | solution.py:37
  66.3 48.9 %reshape.916 = bf16[512,512]{1,0:T(8,128)(2,1)S(1)} reshape(bf16[256,2,256,2]{3,2,1,0:T(8,128)(2,1)} %copy.117) | data formatting | bytes 1048576 | tf_op jit(solution)/shard_map/reshape | solution.py:37
  116.0 0.9 pad_maximum_fusion.18
  118.0 5.1 %conditional.5 = (bf16[1,256,2,256]{3,1,2,0:T(8,128)(2,1)S(1)}, bf16[1,2,256,2,256]{4,2,3,1,0:T(8,128)(2,1)S(1)}) conditional(s32[]{:T(128)} %convert_element_type.481, bf16[1,256,2,256]{3,1,2,0:T(8,128)(2,1)S(1)} %bitcast.422, (bf16[1,256,2,256]{3,1,2,0:T(8,128)(2,1)S(1)}, bf16[1,2,256,2,256]{4,2,3,1,0:T(8,128)(2,1)S(1)}, ...), branch_computations={%region_0.1_spmd, %region_1.2_spmd} | conditional | flops 539492352 | bytes 17563692 | solution.py:172
  119.2 1.1 bitcast_convert_fusion.1
  122.2 1.0 pad_maximum_fusion
  123.2 0.7 copy-done.9
  123.9 1.3 collective-permute-start.2
  125.2 1.7 fusion.52
  126.8 24.2 %copy.126 = bf16[256,2,256,2]{3,2,1,0:T(8,128)(2,1)} copy(bf16[256,2,256,2]{0,2,3,1:T(8,128)(2,1)S(1)} %pad_maximum_fusion.17) | data formatting | bytes 1048576 | tf_op jit(solution)/shard_map/stack | solution.py:37
  151.1 49.0 %reshape.922 = bf16[512,512]{1,0:T(8,128)(2,1)S(1)} reshape(bf16[256,2,256,2]{3,2,1,0:T(8,128)(2,1)} %copy.126) | data formatting | bytes 1048576 | tf_op jit(solution)/shard_map/reshape | solution.py:37
  200.0 1.1 copy.127
  201.2 1.1 copy.138
  202.3 1.1 maximum_bitcast_fusion.14
  203.4 0.8 pad_maximum_fusion.16
  204.2 0.9 copy-done.20
  205.1 1.1 conditional.8
  205.1 1.1 broadcast_in_dim.52
  206.5 1.3 collective-permute-start.3
  208.5 176.2 %collective-permute-done.3 = bf16[1,256,2,256]{3,2,1,0:T(2,128)(2,1)S(1)} collective-permute-done((bf16[1,256,2,256]{3,2,1,0:T(2,128)(2,1)S(1)}, bf16[1,256,2,256]{3,2,1,0:T(2,128)(2,1)S(1)}, u32[]{:S(2)}, u32[]{:S(2)}) %collective-permute-start.3) | collective-permute-done | bytes 262176 | tf_op jit(solution)/shard_map/ppermute | solution.py:18
  384.7 5.2 %conditional.9 = (f32[1,2,256,2,256]{4,2,3,1,0:T(8,128)}) conditional(s32[]{:T(128)} %convert_element_type.481, f32[1,2,256,2,256]{4,2,3,1,0:T(8,128)} %get-tuple-element.112, (bf16[1,2,256,2,256]{4,2,3,1,0:T(8,128)(2,1)S(1)}, bf16[1,2,256,2,256]{4,2,3,1,0:T(8,128)(2,1)S(1)}, bf16[1,256,2,256]{3,2,1,0:T(2,128)(2,1)S(1)}, ...), branch_computations={%region_8.9_spmd, %region_9.10_spmd} | conditional | flops 539492352 | bytes 21495844 | solution.py:185
  384.7 0.9 bitcast_convert_fusion.8
  388.8 1.1 pad_maximum_fusion.6
  389.9 1.3 multiply_bitcast_fusion
  391.9 11.9 %all_to_all.10 = bf16[4,2,40,2,2,256]{5,2,4,3,1,0:T(8,128)(2,1)S(1)} all-to-all(bf16[4,2,40,2,2,256]{5,2,4,3,1,0:T(8,128)(2,1)S(1)} %copy.130), channel_id=1, replica_groups=mesh['section'=2,'lines'=64,'x'=4] {'x'}, dimensions={0} | all-to-all | bytes 1310720 | tf_op jit(solution)/shard_map/all_to_all | solution.py:200
  404.2 2.7 collective-permute-start.5
  406.9 1.9 collective-permute-start.4
  408.8 6.0 %collective-permute-done.5 = bf16[40,2,2,256]{3,0,2,1:T(8,128)(2,1)S(1)} collective-permute-done((bf16[40,2,2,256]{3,0,2,1:T(8,128)(2,1)S(1)}, bf16[40,2,2,256]{3,0,2,1:T(8,128)(2,1)S(1)}, u32[]{:S(2)}, u32[]{:S(2)}) %collective-permute-start.5) | collective-permute-done | bytes 81952 | tf_op jit(solution)/shard_map/ppermute | solution.py:210
  414.8 1.7 collective-permute-done.4
  416.6 0.8 copy.132
  (110 shorter events, 10.3 us)
Async XLA Ops:
  0.0 20.0 %copy-start.7 = (bf16[2,256,256]{2,1,0:T(8,128)(2,1)S(1)}, bf16[2,256,256]{2,1,0:T(8,128)(2,1)}, u32[]{:S(2)}) copy-start(bf16[2,256,256]{2,1,0:T(8,128)(2,1)} %param.17) | copy-start | bytes 786436
  0.0 32.9 %collective-permute-start = (bf16[2,40,2,256]{3,2,1,0:T(2,128)(2,1)}, bf16[2,40,2,256]{3,2,1,0:T(2,128)(2,1)}, u32[]{:S(2)}, u32[]{:S(2)}) collective-permute-start(bf16[2,40,2,256]{3,2,1,0:T(2,128)(2,1)} %param.18), channel_id=1, source_target_pairs={{0,252},{1,253},{2,254},{3,255},{4,0},{5,1},{6,2},{7,3},{8,4},{9,5... | collective-permute-start | bytes 245768 | tf_op jit(solution)/shard_map/ppermute | solution.py:118
  14.0 18.9 %collective-permute-start.1 = (bf16[2,40,2,256]{3,2,1,0:T(2,128)(2,1)}, bf16[2,40,2,256]{3,2,1,0:T(2,128)(2,1)}, u32[]{:S(2)}, u32[]{:S(2)}) collective-permute-start(bf16[2,40,2,256]{3,2,1,0:T(2,128)(2,1)} %param.18), channel_id=1, source_target_pairs={{0,248},{1,249},{2,250},{3,251},{4,252},{5,253},{6,254},{7,255},{8... | collective-permute-start | bytes 245768 | tf_op jit(solution)/shard_map/ppermute | solution.py:118
  29.0 0.9 copy-start.17
  29.0 1.0 copy-start.18
  29.1 1.0 copy-start.19
  29.2 1.8 copy-start.14
  29.2 1.8 copy-start.15
  29.2 1.8 copy-start.16
  31.9 1.0 copy-start.21
  34.4 8.2 %copy-start.10 = (bf16[256,2,256]{2,1,0:T(2,128)(2,1)S(1)}, bf16[256,2,256]{2,1,0:T(2,128)(2,1)}, u32[]{:S(2)}) copy-start(bf16[256,2,256]{2,1,0:T(2,128)(2,1)} %param.16) | copy-start | bytes 786436
  35.4 81.4 %all-to-all-start = ((bf16[4,2,2,40,2,256]{5,3,4,2,1,0:T(8,128)(2,1)}), bf16[4,2,2,40,2,256]{5,3,4,2,1,0:T(8,128)(2,1)S(1)}, u32[]{:S(2)}, u32[]{:S(2)}) async-start(bf16[4,2,2,40,2,256]{5,3,4,2,1,0:T(8,128)(2,1)} %broadcast_select_fusion), calls=%async_computation | async-start | bytes 1310720 | tf_op jit(solution)/shard_map/all_to_all | solution.py:129
  117.1 1.0 copy-start.8
  121.2 1.0 copy-start.11
  123.2 0.7 copy-start.9
  123.9 80.4 %collective-permute-start.2 = (bf16[1,256,2,256]{3,1,2,0:T(8,128)(2,1)}, bf16[1,256,2,256]{3,1,2,0:T(8,128)(2,1)S(1)}, u32[]{:S(2)}, u32[]{:S(2)}) collective-permute-start(bf16[1,256,2,256]{3,1,2,0:T(8,128)(2,1)} %copy-done.9), channel_id=1, source_target_pairs={{0,256},{1,257},{2,258},{3,259},{4,260},{5,261},{6,262},{7,263},{8... | collective-permute-start | bytes 786440 | tf_op jit(solution)/shard_map/ppermute | solution.py:18
  151.1 49.0 %copy-start.5 = (bf16[2,256,2,256]{3,1,2,0:T(8,128)(2,1)S(1)}, bf16[2,256,2,256]{3,1,2,0:T(8,128)(2,1)}, u32[]{:S(2)}) copy-start(bf16[2,256,2,256]{3,1,2,0:T(8,128)(2,1)} %pad_maximum_fusion.18) | copy-start | bytes 1572868
  204.2 0.9 copy-start.20
  206.5 178.2 %collective-permute-start.3 = (bf16[1,256,2,256]{3,2,1,0:T(2,128)(2,1)S(1)}, bf16[1,256,2,256]{3,2,1,0:T(2,128)(2,1)S(1)}, u32[]{:S(2)}, u32[]{:S(2)}) collective-permute-start(bf16[1,256,2,256]{3,2,1,0:T(2,128)(2,1)S(1)} %copy.129), channel_id=1, source_target_pairs={{256,0},{257,1},{258,2},{259,3},{260,4},{261,5},{262,6},{263,7},{2... | collective-permute-start | bytes 786440 | tf_op jit(solution)/shard_map/ppermute | solution.py:18
  386.1 1.0 copy-start.6
  404.2 10.6 %collective-permute-start.5 = (bf16[40,2,2,256]{3,0,2,1:T(8,128)(2,1)S(1)}, bf16[40,2,2,256]{3,0,2,1:T(8,128)(2,1)S(1)}, u32[]{:S(2)}, u32[]{:S(2)}) collective-permute-start(bf16[40,2,2,256]{3,0,2,1:T(8,128)(2,1)S(1)} %get-tuple-element.206), channel_id=1, source_target_pairs={{0,8},{1,9},{2,10},{3,11},{4,12},{5,13},{6,14},{7,15},{8,16},{9,17... | collective-permute-start | bytes 245768 | tf_op jit(solution)/shard_map/ppermute | solution.py:210
  406.9 9.7 %collective-permute-start.4 = (bf16[40,2,2,256]{3,0,2,1:T(8,128)(2,1)S(1)}, bf16[40,2,2,256]{3,0,2,1:T(8,128)(2,1)S(1)}, u32[]{:S(2)}, u32[]{:S(2)}) collective-permute-start(bf16[40,2,2,256]{3,0,2,1:T(8,128)(2,1)S(1)} %get-tuple-element.205), channel_id=1, source_target_pairs={{0,4},{1,5},{2,6},{3,7},{4,8},{5,9},{6,10},{7,11},{8,12},{9,13},{1... | collective-permute-start | bytes 245768 | tf_op jit(solution)/shard_map/ppermute | solution.py:210

commit v4 on v2

--- a/solution.py
+++ b/solution.py
@@ -1,6 +1,7 @@
 import functools
 
 import jax
+from jax.experimental import pallas as pl
 import jax.numpy as jnp
 from jax import lax
 from jax.sharding import PartitionSpec as P
@@ -102,14 +103,115 @@
 
 
 def accumulate(gradients, starts, buffer_rows):
-    slot_count, slice_count, width = (gradients.shape[0], gradients.shape[1], gradients.shape[-1])
-    buffer_all = jnp.zeros((buffer_rows, slice_count, 2, width), jnp.float32)
-    for slot_at in range(slot_count):
-        start_row = starts[slot_at]
-        current = lax.dynamic_slice_in_dim(buffer_all, start_row, width, 0)
-        placed = jnp.transpose(gradients[slot_at], (1, 0, 2, 3))
-        buffer_all = lax.dynamic_update_slice_in_dim(buffer_all, current + placed, start_row, 0)
-    return buffer_all
+    width = gradients.shape[-1]
+    margin = buffer_rows - width
+    placed = jnp.transpose(gradients[0], (1, 0, 2, 3))
+    padded = jnp.pad(placed, ((margin, margin), (0, 0), (0, 0), (0, 0)))
+    return lax.dynamic_slice_in_dim(padded, margin - starts[0], buffer_rows, 0)
+
+
+def real_dot(first, second):
+    return jnp.dot(first, second, preferred_element_type=jnp.float32)
+
+
+def times_left(real, imag, field_real, field_imag):
+    return (
+        real_dot(real, field_real) - real_dot(imag, field_imag),
+        real_dot(real, field_imag) + real_dot(imag, field_real),
+    )
+
+
+def times_left_adj(real_t, imag_t, field_real, field_imag):
+    return (
+        real_dot(real_t, field_real) + real_dot(imag_t, field_imag),
+        real_dot(real_t, field_imag) - real_dot(imag_t, field_real),
+    )
+
+
+def times_right(field_real, field_imag, real_t, imag_t):
+    return (
+        real_dot(field_real, real_t) - real_dot(field_imag, imag_t),
+        real_dot(field_real, imag_t) + real_dot(field_imag, real_t),
+    )
+
+
+def times_right_conj(field_real, field_imag, real, imag):
+    return (
+        real_dot(field_real, real) + real_dot(field_imag, imag),
+        real_dot(field_imag, real) - real_dot(field_real, imag),
+    )
+
+
+def rounded(pair):
+    return (pair[0].astype(jnp.bfloat16), pair[1].astype(jnp.bfloat16))
+
+
+def march_kernel(field_ref, patch_ref, mat_ref, out_ref, incident_ref):
+    real, imag, real_t, imag_t = mat_ref[0], mat_ref[1], mat_ref[2], mat_ref[3]
+    field_real, field_imag = field_ref[0], field_ref[1]
+    for slice_at in range(patch_ref.shape[0]):
+        incident_ref[slice_at, 0] = field_real
+        incident_ref[slice_at, 1] = field_imag
+        first_real = field_real.astype(jnp.float32)
+        first_imag = field_imag.astype(jnp.float32)
+        second_real = patch_ref[slice_at, 0].astype(jnp.float32)
+        second_imag = patch_ref[slice_at, 1].astype(jnp.float32)
+        phase = rounded(
+            (
+                first_real * second_real - first_imag * second_imag,
+                first_real * second_imag + first_imag * second_real,
+            )
+        )
+        middle = rounded(times_left(real, imag, *phase))
+        field_real, field_imag = rounded(times_right(*middle, real_t, imag_t))
+    out_ref[0] = field_real
+    out_ref[1] = field_imag
+
+
+def far_kernel(field_ref, measured_ref, mat_ref, out_ref):
+    real, imag, real_t, imag_t = mat_ref[0], mat_ref[1], mat_ref[2], mat_ref[3]
+    half_far = rounded(times_left(real, imag, field_ref[0], field_ref[1]))
+    far_real, far_imag = times_right(*half_far, real_t, imag_t)
+    misfit = far_real * far_real + far_imag * far_imag - measured_ref[...].astype(jnp.float32)
+    grad_far = rounded((far_real * misfit, far_imag * misfit))
+    half_back = rounded(times_left_adj(real_t, imag_t, *grad_far))
+    back_real, back_imag = rounded(times_right_conj(*half_back, real, imag))
+    out_ref[0] = back_real
+    out_ref[1] = back_imag
+
+
+def retreat_kernel(back_ref, patch_ref, incident_ref, mat_ref, out_ref, grad_ref):
+    real, imag, real_t, imag_t = mat_ref[0], mat_ref[1], mat_ref[2], mat_ref[3]
+    back = (back_ref[0], back_ref[1])
+    for slice_at in reversed(range(patch_ref.shape[0])):
+        middle = rounded(times_left_adj(real_t, imag_t, *back))
+        bar_real, bar_imag = times_right_conj(*middle, real, imag)
+        inc_real = incident_ref[slice_at, 0].astype(jnp.float32)
+        inc_imag = incident_ref[slice_at, 1].astype(jnp.float32)
+        grad_ref[slice_at, 0] = inc_real * bar_real + inc_imag * bar_imag
+        grad_ref[slice_at, 1] = inc_real * bar_imag - inc_imag * bar_real
+        pat_real = patch_ref[slice_at, 0].astype(jnp.float32)
+        pat_imag = patch_ref[slice_at, 1].astype(jnp.float32)
+        back = rounded(
+            (pat_real * bar_real + pat_imag * bar_imag, pat_real * bar_imag - pat_imag * bar_real)
+        )
+    out_ref[0] = back[0]
+    out_ref[1] = back[1]
+
+
+def planes_of(matrix):
+    return jnp.stack((matrix[0], matrix[1], matrix[0].T, matrix[1].T))
+
+
+def run_kernel(body, outs, flops, *args):
+    moved = sum(arg.size * arg.dtype.itemsize for arg in args)
+    listed = outs if isinstance(outs, tuple) else (outs,)
+    moved += sum(out.size * jnp.dtype(out.dtype).itemsize for out in listed)
+    return pl.pallas_call(
+        body,
+        out_shape=outs,
+        cost_estimate=pl.CostEstimate(flops=flops, transcendentals=0, bytes_accessed=moved),
+    )(*args)
 
 
 def on_device(row_axis, tile_axes, probe, kernel, object_slab, offsets, counts, intensity):
@@ -147,60 +249,54 @@
     patches = jax.vmap(lambda offset: lax.dynamic_slice_in_dim(window, offset, width, 1))(relative)
     live_slots = jnp.arange(slot_count, dtype=jnp.int32) < counts[0]
 
-    def march(field_now, patches_here):
-        incidents = []
-        for slice_at in range(slice_count):
-            incidents.append(field_now)
-            phase = complex_mul(field_now, patches_here[..., slice_at, :, :, :]).astype(
-                jnp.bfloat16
-            )
-            middle = apply_left(kernel, phase).astype(jnp.bfloat16)
-            field_now = apply_right(middle, kernel).astype(jnp.bfloat16)
-        return (field_now, jnp.stack(incidents, axis=-4))
-
-    def far_adjoint(field_now, measured):
-        half_far = apply_left(dft_table, field_now).astype(jnp.bfloat16)
-        far = apply_right(half_far, dft_table)
-        misfit = far[..., 0, :] ** 2 + far[..., 1, :] ** 2 - measured.astype(jnp.float32)
-        grad_far = (far * misfit[..., None, :]).astype(jnp.bfloat16)
-        half_back = apply_left_adj(dft_table, grad_far).astype(jnp.bfloat16)
-        return apply_right_conj(half_back, dft_table).astype(jnp.bfloat16)
-
-    def retreat(adjoint, patches_here, incidents):
-        gradients = []
-        for slice_at in reversed(range(slice_count)):
-            middle = apply_left_adj(kernel, adjoint).astype(jnp.bfloat16)
-            phibar = apply_right_conj(middle, kernel)
-            gradients.append(conj_mul(incidents[..., slice_at, :, :, :], phibar))
-            adjoint = conj_mul(patches_here[..., slice_at, :, :, :], phibar).astype(jnp.bfloat16)
-        return (adjoint, jnp.stack(gradients[::-1], axis=-4))
-
-    stored = jnp.zeros(patches.shape, jnp.bfloat16)
-    gradients = jnp.zeros(patches.shape, jnp.float32)
-    waves = jnp.broadcast_to(probe, (slot_count,) + probe.shape)
+    planes = jnp.transpose(patches[0], (0, 2, 1, 3))
+    kernel_planes = planes_of(kernel)
+    dft_planes = planes_of(dft_matrix(width))
+    field_shape = jax.ShapeDtypeStruct((2, width, width), jnp.bfloat16)
+    dot_flops = 2 * width**3
+
+    def march(field_in):
+        outs = (field_shape, jax.ShapeDtypeStruct(planes.shape, jnp.bfloat16))
+        flops = slice_count * 8 * dot_flops
+        return tuple(run_kernel(march_kernel, outs, flops, field_in, planes, kernel_planes))
+
+    def far_adjoint(field_in):
+        return run_kernel(far_kernel, field_shape, 16 * dot_flops, field_in, intensity[0], dft_planes)
+
+    def retreat(back_in, incidents):
+        outs = (field_shape, jax.ShapeDtypeStruct(planes.shape, jnp.float32))
+        flops = slice_count * 8 * dot_flops
+        return tuple(
+            run_kernel(retreat_kernel, outs, flops, back_in, planes, incidents, kernel_planes)
+        )
+
+    stored = jnp.zeros(planes.shape, jnp.bfloat16)
+    gradients = jnp.zeros(planes.shape, jnp.float32)
+    waves = jnp.transpose(probe, (1, 0, 2))
     for section_step in range(sections):
         if section_step > 0:
             waves = passed_along(waves, "section", 1)
         waves, stored = lax.cond(
             section_now == section_step,
-            lambda field_in, kept: march(field_in, patches),
+            lambda field_in, kept: march(field_in),
             lambda field_in, kept: (field_in, kept),
             waves,
             stored,
         )
     adjoints = lax.cond(
-        is_last, lambda field_in: far_adjoint(field_in, intensity), lambda field_in: field_in, waves
+        is_last, lambda field_in: far_adjoint(field_in), lambda field_in: field_in, waves
     )
     for section_step in reversed(range(sections)):
         if section_step < sections - 1:
             adjoints = passed_along(adjoints, "section", -1)
         adjoints, gradients = lax.cond(
             section_now == section_step,
-            lambda field_in, kept: retreat(field_in, patches, stored),
+            lambda field_in, kept: retreat(field_in, stored),
             lambda field_in, kept: (field_in, kept),
             adjoints,
             gradients,
         )
+    gradients = jnp.transpose(gradients, (0, 2, 1, 3))[None]
     gradients = gradients * live_slots.astype(jnp.float32)[:, None, None, None, None]
     nearby = accumulate(gradients, offsets - tile_now * local_rows, 2 * row_size * local_rows)
     tiles = jnp.stack(

time: 90.8 us -> 82.7 us (0.911)
  local copies, waits for them, and re-layouts: 7.17 us -> 2.71 us
  matrix products: 4.2 us -> 0 us
  waiting for transfers between devices: 29.1 us -> 25.5 us
  Pallas kernels: 0 us -> 3.02 us
    dot_general x16 -> x0, matrix products: 4.2 us -> none  [product(): return jnp.einsum(form, first, second, preferred_element_type=jnp.float32)]
    dynamic_update_slice x1 -> x0, local copies, waits for them, and re-layouts: 3.28 us -> none  [accumulate(): lax.dynamic_update_slice_in_dim(buffer_all, current + placed, start_row, 0)]
    pallas_call x0 -> x2, Pallas kernels: none -> 3.02 us  [run_kernel(): pl.pallas_call(body, out_shape=outs, cost_estimate=pl.CostEstimate(flops=...]
    ppermute x2, waiting for transfers between devices: 9.44 us -> 6.91 us  [passed_along(): return lax.ppermute(shard, axis, pairs)]
    slice x0 -> x2, other arithmetic: none -> 1.97 us  [planes_of(): return jnp.stack((matrix[0], matrix[1], matrix[0].T, matrix[1].T))]
    all_to_all x1, waiting for transfers between devices: 7.2 us -> 6.07 us  [on_device(): got = lax.all_to_all(sent, row_axis, 0, 0)]
    another operation x16 -> x3, other arithmetic: 2.16 us -> 1.24 us  [planes_of(): return jnp.stack((matrix[0], matrix[1], matrix[0].T, matrix[1].T))]
  transfers between devices with their start and end apart: 7 -> 7, of which waited for: 5 -> 5; matrix products, arithmetic and copies ran while one was open for 1% -> 4% of each run, Pallas kernels for 0% -> 0%
where the time goes in v4:
time: 82.7 us; the launch traced here: 82.3 us
  starting transfers between devices  30.9 us (37%)
  waiting for transfers between devices  25.5 us (31%)
  blocking collectives  12 us (15%)
  other arithmetic  6.41 us (8%)
  Pallas kernels  3.02 us (4%)
  local copies, waits for them, and re-layouts  2.71 us (3%)
  between operations  1.74 us (2%)
    ppermute x2, starting transfers between devices, on_device(): lax.ppermute(object_slab, tile_axes, [(s, (s - ahead * row_size) % tile_c...  17.9 us
    all_to_all x1, blocking collectives, on_device(): incoming = lax.all_to_all(outgoing, row_axis, 0, 0).astype(jnp.float32)  12 us
    ppermute x2, waiting for transfers between devices, on_device(): lax.ppermute(spill.astype(jnp.bfloat16), tile_axes, [(s, (s + ahead * row...  9.14 us
    ppermute x2, waiting for transfers between devices, passed_along(): return lax.ppermute(shard, axis, pairs)  6.91 us
    all_to_all x1, waiting for transfers between devices, on_device(): got = lax.all_to_all(sent, row_axis, 0, 0)  6.07 us
    ppermute x2, starting transfers between devices, on_device(): lax.ppermute(spill.astype(jnp.bfloat16), tile_axes, [(s, (s + ahead * row...  5.47 us
    all_to_all x1, starting transfers between devices, on_device(): got = lax.all_to_all(sent, row_axis, 0, 0)  4.96 us
    ppermute x2, waiting for transfers between devices, on_device(): lax.ppermute(object_slab, tile_axes, [(s, (s - ahead * row_size) % tile_c...  3.37 us
  transfers between devices with their start and end apart: 7, of which 5 were waited for; matrix products, arithmetic and copies ran while one was open for 4% of the time, Pallas kernels for 0%

profile of v4, /device:TPU:2, one launch (start us, length us, event | category | flops | bytes accessed | tf_op | source)
XLA Modules:
  0.0 82.3 jit_solution(5504576661478065207)
XLA Ops:
  0.0 13.8 %collective-permute-start = (bf16[2,40,2,256]{3,2,1,0:T(2,128)(2,1)}, bf16[2,40,2,256]{3,2,1,0:T(2,128)(2,1)S(1)}, u32[]{:S(2)}, u32[]{:S(2)}) collective-permute-start(bf16[2,40,2,256]{3,2,1,0:T(2,128)(2,1)} %param.18), channel_id=1, source_target_pairs={{0,252},{1,253},{2,254},{3,255},{4,0},{5,1},{6,2},{7,3},{8,4},{9,5... | collective-permute-start | bytes 245768 | tf_op jit(solution)/shard_map/ppermute | solution.py:232
  13.9 4.1 %collective-permute-start.1 = (bf16[2,40,2,256]{3,2,1,0:T(2,128)(2,1)}, bf16[2,40,2,256]{3,2,1,0:T(2,128)(2,1)S(1)}, u32[]{:S(2)}, u32[]{:S(2)}) collective-permute-start(bf16[2,40,2,256]{3,2,1,0:T(2,128)(2,1)} %param.18), channel_id=1, source_target_pairs={{0,248},{1,249},{2,250},{3,251},{4,252},{5,253},{6,254},{7,255},{8... | collective-permute-start | bytes 245768 | tf_op jit(solution)/shard_map/ppermute | solution.py:232
  17.9 0.0 collective-permute-done
  17.9 3.4 %collective-permute-done.1 = bf16[2,40,2,256]{3,2,1,0:T(2,128)(2,1)S(1)} collective-permute-done((bf16[2,40,2,256]{3,2,1,0:T(2,128)(2,1)}, bf16[2,40,2,256]{3,2,1,0:T(2,128)(2,1)S(1)}, u32[]{:S(2)}, u32[]{:S(2)}) %collective-permute-start.1) | collective-permute-done | bytes 81952 | tf_op jit(solution)/shard_map/ppermute | solution.py:232
  21.3 1.2 %pad_maximum_fusion.2 = (bf16[2,2,40,2,256]{4,3,2,1,0:T(2,128)(2,1)S(1)}, bf16[2,2,40,2,256]{4,3,2,1,0:T(2,128)(2,1)S(1)}) fusion(bf16[1,2,40,2,256]{4,3,2,1,0:T(2,128)(2,1)S(1)} %bitcast.127, bf16[1,2,40,2,256]{4,3,2,1,0:T(2,128)(2,1)} %bitcast.126, bf16[1,2,40,2,256]{4,3,2,1,0:T(2,128)(2,1)S(1)} %bitcast.128), kind=kLoop, calls=%fused_computation.30 | loop fusion | flops 163840 | bytes 573440 | tf_op jit(solution)/shard_map/stack | solution.py:241
  22.6 0.0 copy-start
  22.6 1.0 %broadcast_select_fusion = bf16[4,2,2,40,2,256]{5,3,4,2,1,0:T(8,128)(2,1)} fusion(pred[4]{0:T(512)(128)(4,1)S(1)} %iota_compare_fusion, bf16[2,2,40,2,256]{4,2,3,1,0:T(8,128)(2,1)S(1)} %copy.26, bf16[2,2,40,2,256]{4,2,3,1,0:T(8,128)(2,1)S(1)} %copy.25), kind=kLoop, calls=%fused_computation.14 | loop fusion | flops 327680 | bytes 983044 | tf_op jit(solution)/shard_map/jit(_where)/select_n | solution.py:240
  23.6 0.0 copy-start.1
  23.6 5.0 %all-to-all-start = ((bf16[4,2,2,40,2,256]{5,3,4,2,1,0:T(8,128)(2,1)}), bf16[4,2,2,40,2,256]{5,3,4,2,1,0:T(8,128)(2,1)S(1)}, u32[]{:S(2)}, u32[]{:S(2)}) async-start(bf16[4,2,2,40,2,256]{5,3,4,2,1,0:T(8,128)(2,1)} %broadcast_select_fusion), calls=%async_computation | async-start | bytes 1310720 | tf_op jit(solution)/shard_map/all_to_all | solution.py:243
  29.2 0.0 copy-done
  29.2 0.1 copy.34
  29.3 0.1 copy.35
  29.4 0.0 copy-done.1
  29.5 1.0 %multiply_convert_fusion.1 = bf16[1,256,256]{1,2,0:T(8,128)(2,1)S(1)} fusion(), kind=kLoop, calls=%fused_computation.26 | loop fusion | flops 1048576 | bytes 131072 | tf_op jit(solution)/shard_map/slice | solution.py:203
  30.5 0.1 pad_maximum_fusion
  30.6 6.1 %all-to-all-done = bf16[4,2,2,40,2,256]{5,3,4,2,1,0:T(8,128)(2,1)S(1)} async-done(((bf16[4,2,2,40,2,256]{5,3,4,2,1,0:T(8,128)(2,1)}), bf16[4,2,2,40,2,256]{5,3,4,2,1,0:T(8,128)(2,1)S(1)}, u32[]{:S(2)}, u32[]{:S(2)}) %all-to-all-start) | async-done | bytes 655392 | tf_op jit(solution)/shard_map/all_to_all | solution.py:243
  36.6 0.2 fusion.2
  37.0 0.1 dynamic-slice_bitcast_fusion
  37.1 1.1 %conditional.5 = ((bf16[2,256,256]{2,1,0:T(8,128)(2,1)S(1)}, bf16[2,2,256,256]{3,2,1,0:T(8,128)(2,1)S(1)})) conditional(s32[]{:T(128)} %convert_element_type.53, bf16[2,256,256]{2,1,0:T(8,128)(2,1)S(1)} %bitcast.121, (bf16[2,256,256]{2,1,0:T(8,128)(2,1)S(1)}, bf16[2,2,256,256]{3,2,1,0:T(8,128)(2,1)S(1)}, bf16[4,256,256]{2,1,0:T(8,128)(2,1)S(1)}) %tuple.83), branch_computations={%region_0.1_spmd, %region_1.2_spmd} | conditional | flops 536870912 | bytes 2097160 | solution.py:279
  37.2 1.1 %branch_1_fun.5 = (bf16[2,256,256]{2,1,0:T(8,128)(2,1)S(1)}, bf16[2,2,256,256]{3,2,1,0:T(8,128)(2,1)S(1)}) custom-call(bf16[2,256,256]{2,1,0:T(8,128)(2,1)S(1)} %get-tuple-element.61.field_ref, bf16[2,2,256,256]{3,2,1,0:T(8,128)(2,1)S(1)} %get-tuple-element.62.patch_ref, bf16[4,256,256]{2,1,0:T(8,128)(2,1)S(1)} %get-tuple-element.63.mat_ref), custom_call_target="tpu_custom_call" | custom-call | flops 536870912 | bytes 2097152 | tf_op jit(solution)/shard_map/cond/branch_1_fun/pallas_call | solution.py:210
  38.3 1.3 %collective-permute-start.2 = (bf16[2,256,256]{2,1,0:T(8,128)(2,1)S(1)}, bf16[2,256,256]{2,1,0:T(8,128)(2,1)S(1)}, u32[]{:S(2)}, u32[]{:S(2)}) collective-permute-start(bf16[2,256,256]{2,1,0:T(8,128)(2,1)S(1)} %get-tuple-element.90), channel_id=1, source_target_pairs={{0,256},{1,257},{2,258},{3,259},{4,260},{5,261},{6,262},{7,263},{8... | collective-permute-start | bytes 786440 | tf_op jit(solution)/shard_map/ppermute | solution.py:19
  39.6 1.0 %multiply_convert_fusion = bf16[1,256,256]{1,2,0:T(8,128)(2,1)S(1)} fusion(), kind=kLoop, calls=%fused_computation.25 | loop fusion | flops 1114112 | bytes 131072 | tf_op jit(solution)/shard_map/slice | solution.py:203
  40.6 0.1 copy.29
  40.7 0.1 copy.30
  40.8 1.1 %fusion.25 = (bf16[1,256,256]{2,1,0:T(8,128)(2,1)S(1)}, bf16[1,256,256]{2,1,0:T(8,128)(2,1)S(1)}) fusion(), kind=kLoop, calls=%fused_computation.65 | loop fusion | flops 1245184 | bytes 262144 | tf_op jit(solution)/shard_map/stack | solution.py:203
  41.9 0.1 pad_maximum_fusion.1
  42.0 0.0 copy-start.2
  42.0 0.0 collective-permute-done.2
  42.1 0.9 %copy-done.2 = bf16[1,256,256]{2,1,0:T(8,128)(2,1)S(1)} copy-done((bf16[1,256,256]{2,1,0:T(8,128)(2,1)S(1)}, bf16[1,256,256]{2,1,0:T(8,128)(2,1)}, u32[]{:S(2)}) %copy-start.2) | copy-done | bytes 131096
  42.9 0.1 conditional.8
  42.9 0.1 broadcast_in_dim.47
  43.0 1.3 %collective-permute-start.3 = (bf16[2,256,256]{2,1,0:T(8,128)(2,1)S(1)}, bf16[2,256,256]{2,1,0:T(8,128)(2,1)S(1)}, u32[]{:S(2)}, u32[]{:S(2)}) collective-permute-start(bf16[2,256,256]{2,1,0:T(8,128)(2,1)S(1)} %get-tuple-element.96), channel_id=1, source_target_pairs={{256,0},{257,1},{258,2},{259,3},{260,4},{261,5},{262,6},{263,7},{2... | collective-permute-start | bytes 786440 | tf_op jit(solution)/shard_map/ppermute | solution.py:19
  45.0 6.9 %collective-permute-done.3 = bf16[2,256,256]{2,1,0:T(8,128)(2,1)S(1)} collective-permute-done((bf16[2,256,256]{2,1,0:T(8,128)(2,1)S(1)}, bf16[2,256,256]{2,1,0:T(8,128)(2,1)S(1)}, u32[]{:S(2)}, u32[]{:S(2)}) %collective-permute-start.3) | collective-permute-done | bytes 262176 | tf_op jit(solution)/shard_map/ppermute | solution.py:19
  51.9 1.9 %conditional.9 = (f32[2,2,256,256]{3,2,1,0:T(8,128)S(1)}) conditional(s32[]{:T(128)} %convert_element_type.53, f32[2,2,256,256]{3,2,1,0:T(8,128)S(1)} %get-tuple-element.95, (bf16[2,256,256]{2,1,0:T(8,128)(2,1)S(1)}, bf16[2,2,256,256]{3,2,1,0:T(8,128)(2,1)S(1)}, bf16[2,2,256,256]{3,2,1,0:T(8,128)(2,1)S(1)}, bf16[4,256,256]{2,1,0:T(8,128)(2,1)S(1)}) %tuple.52), branch_computations={%region_8.9_spmd, %region_9.10_spmd} | conditional | flops 536870912 | bytes 3145736 | solution.py:292
  51.9 1.9 %branch_1_fun.8 = (bf16[2,256,256]{2,1,0:T(8,128)(2,1)}, f32[2,2,256,256]{3,2,1,0:T(8,128)S(1)}) custom-call(bf16[2,256,256]{2,1,0:T(8,128)(2,1)S(1)} %get-tuple-element.78.back_ref, bf16[2,2,256,256]{3,2,1,0:T(8,128)(2,1)S(1)} %get-tuple-element.79.patch_ref, bf16[2,2,256,256]{3,2,1,0:T(8,128)(2,1)S(1)} %get-tuple-element.80.incident_ref, ...), custom_call_target="tpu_custom_call" | custom-call | flops 536870912 | bytes 3145728 | tf_op jit(solution)/shard_map/cond/branch_1_fun/pallas_call | solution.py:210
  53.8 0.1 multiply_bitcast_fusion
  53.9 0.2 fusion
  54.2 0.3 fusion.1
  54.5 12.0 %all_to_all.10 = bf16[4,2,40,2,2,256]{5,2,4,3,1,0:T(8,128)(2,1)S(1)} all-to-all(bf16[4,2,40,2,2,256]{5,2,4,3,1,0:T(8,128)(2,1)S(1)} %copy.31), channel_id=1, replica_groups=mesh['section'=2,'lines'=64,'x'=4] {'x'}, dimensions={0} | all-to-all | bytes 1310720 | tf_op jit(solution)/shard_map/all_to_all | solution.py:308
  66.5 0.2 convert_element_type.57
  66.7 0.2 select_reduce_fusion.1
  66.9 3.5 %collective-permute-start.4 = (bf16[40,2,2,256]{3,0,2,1:T(8,128)(2,1)S(1)}, bf16[40,2,2,256]{3,0,2,1:T(8,128)(2,1)S(1)}, u32[]{:S(2)}, u32[]{:S(2)}) collective-permute-start(bf16[40,2,2,256]{3,0,2,1:T(8,128)(2,1)S(1)} %get-tuple-element.121), channel_id=1, source_target_pairs={{0,4},{1,5},{2,6},{3,7},{4,8},{5,9},{6,10},{7,11},{8,12},{9,13},{1... | collective-permute-start | bytes 245768 | tf_op jit(solution)/shard_map/ppermute | solution.py:318
  70.4 1.9 %collective-permute-start.5 = (bf16[40,2,2,256]{3,0,2,1:T(8,128)(2,1)S(1)}, bf16[40,2,2,256]{3,0,2,1:T(8,128)(2,1)S(1)}, u32[]{:S(2)}, u32[]{:S(2)}) collective-permute-start(bf16[40,2,2,256]{3,0,2,1:T(8,128)(2,1)S(1)} %get-tuple-element.122), channel_id=1, source_target_pairs={{0,8},{1,9},{2,10},{3,11},{4,12},{5,13},{6,14},{7,15},{8,16},{9,17... | collective-permute-start | bytes 245768 | tf_op jit(solution)/shard_map/ppermute | solution.py:318
  72.4 6.3 %collective-permute-done.4 = bf16[40,2,2,256]{3,0,2,1:T(8,128)(2,1)S(1)} collective-permute-done((bf16[40,2,2,256]{3,0,2,1:T(8,128)(2,1)S(1)}, bf16[40,2,2,256]{3,0,2,1:T(8,128)(2,1)S(1)}, u32[]{:S(2)}, u32[]{:S(2)}) %collective-permute-start.4) | collective-permute-done | bytes 81952 | tf_op jit(solution)/shard_map/ppermute | solution.py:318
  78.7 2.8 %collective-permute-done.5 = bf16[40,2,2,256]{3,0,2,1:T(8,128)(2,1)S(1)} collective-permute-done((bf16[40,2,2,256]{3,0,2,1:T(8,128)(2,1)S(1)}, bf16[40,2,2,256]{3,0,2,1:T(8,128)(2,1)S(1)}, u32[]{:S(2)}, u32[]{:S(2)}) %collective-permute-start.5) | collective-permute-done | bytes 81952 | tf_op jit(solution)/shard_map/ppermute | solution.py:318
  81.5 0.8 copy.33
  (25 shorter events, 0.3 us)
Async XLA Ops:
  0.0 17.9 %collective-permute-start = (bf16[2,40,2,256]{3,2,1,0:T(2,128)(2,1)}, bf16[2,40,2,256]{3,2,1,0:T(2,128)(2,1)S(1)}, u32[]{:S(2)}, u32[]{:S(2)}) collective-permute-start(bf16[2,40,2,256]{3,2,1,0:T(2,128)(2,1)} %param.18), channel_id=1, source_target_pairs={{0,252},{1,253},{2,254},{3,255},{4,0},{5,1},{6,2},{7,3},{8,4},{9,5... | collective-permute-start | bytes 245768 | tf_op jit(solution)/shard_map/ppermute | solution.py:232
  13.9 7.5 %collective-permute-start.1 = (bf16[2,40,2,256]{3,2,1,0:T(2,128)(2,1)}, bf16[2,40,2,256]{3,2,1,0:T(2,128)(2,1)S(1)}, u32[]{:S(2)}, u32[]{:S(2)}) collective-permute-start(bf16[2,40,2,256]{3,2,1,0:T(2,128)(2,1)} %param.18), channel_id=1, source_target_pairs={{0,248},{1,249},{2,250},{3,251},{4,252},{5,253},{6,254},{7,255},{8... | collective-permute-start | bytes 245768 | tf_op jit(solution)/shard_map/ppermute | solution.py:232
  22.6 6.6 %copy-start = (bf16[2,256,256]{2,1,0:T(8,128)(2,1)S(1)}, bf16[2,256,256]{2,1,0:T(8,128)(2,1)}, u32[]{:S(2)}) copy-start(bf16[2,256,256]{2,1,0:T(8,128)(2,1)} %param.17) | copy-start | bytes 786436
  23.6 5.9 %copy-start.1 = (bf16[256,2,256]{2,1,0:T(2,128)(2,1)S(1)}, bf16[256,2,256]{2,1,0:T(2,128)(2,1)}, u32[]{:S(2)}) copy-start(bf16[256,2,256]{2,1,0:T(2,128)(2,1)} %param.16) | copy-start | bytes 786436
  23.6 13.0 %all-to-all-start = ((bf16[4,2,2,40,2,256]{5,3,4,2,1,0:T(8,128)(2,1)}), bf16[4,2,2,40,2,256]{5,3,4,2,1,0:T(8,128)(2,1)S(1)}, u32[]{:S(2)}, u32[]{:S(2)}) async-start(bf16[4,2,2,40,2,256]{5,3,4,2,1,0:T(8,128)(2,1)} %broadcast_select_fusion), calls=%async_computation | async-start | bytes 1310720 | tf_op jit(solution)/shard_map/all_to_all | solution.py:243
  38.3 3.7 %collective-permute-start.2 = (bf16[2,256,256]{2,1,0:T(8,128)(2,1)S(1)}, bf16[2,256,256]{2,1,0:T(8,128)(2,1)S(1)}, u32[]{:S(2)}, u32[]{:S(2)}) collective-permute-start(bf16[2,256,256]{2,1,0:T(8,128)(2,1)S(1)} %get-tuple-element.90), channel_id=1, source_target_pairs={{0,256},{1,257},{2,258},{3,259},{4,260},{5,261},{6,262},{7,263},{8... | collective-permute-start | bytes 786440 | tf_op jit(solution)/shard_map/ppermute | solution.py:19
  42.0 0.9 %copy-start.2 = (bf16[1,256,256]{2,1,0:T(8,128)(2,1)S(1)}, bf16[1,256,256]{2,1,0:T(8,128)(2,1)}, u32[]{:S(2)}) copy-start(bf16[1,256,256]{2,1,0:T(8,128)(2,1)} %param.21) | copy-start | bytes 393220
  43.0 8.9 %collective-permute-start.3 = (bf16[2,256,256]{2,1,0:T(8,128)(2,1)S(1)}, bf16[2,256,256]{2,1,0:T(8,128)(2,1)S(1)}, u32[]{:S(2)}, u32[]{:S(2)}) collective-permute-start(bf16[2,256,256]{2,1,0:T(8,128)(2,1)S(1)} %get-tuple-element.96), channel_id=1, source_target_pairs={{256,0},{257,1},{258,2},{259,3},{260,4},{261,5},{262,6},{263,7},{2... | collective-permute-start | bytes 786440 | tf_op jit(solution)/shard_map/ppermute | solution.py:19
  66.9 11.8 %collective-permute-start.4 = (bf16[40,2,2,256]{3,0,2,1:T(8,128)(2,1)S(1)}, bf16[40,2,2,256]{3,0,2,1:T(8,128)(2,1)S(1)}, u32[]{:S(2)}, u32[]{:S(2)}) collective-permute-start(bf16[40,2,2,256]{3,0,2,1:T(8,128)(2,1)S(1)} %get-tuple-element.121), channel_id=1, source_target_pairs={{0,4},{1,5},{2,6},{3,7},{4,8},{5,9},{6,10},{7,11},{8,12},{9,13},{1... | collective-permute-start | bytes 245768 | tf_op jit(solution)/shard_map/ppermute | solution.py:318
  70.4 11.1 %collective-permute-start.5 = (bf16[40,2,2,256]{3,0,2,1:T(8,128)(2,1)S(1)}, bf16[40,2,2,256]{3,0,2,1:T(8,128)(2,1)S(1)}, u32[]{:S(2)}, u32[]{:S(2)}) collective-permute-start(bf16[40,2,2,256]{3,0,2,1:T(8,128)(2,1)S(1)} %get-tuple-element.122), channel_id=1, source_target_pairs={{0,8},{1,9},{2,10},{3,11},{4,12},{5,13},{6,14},{7,15},{8,16},{9,17... | collective-permute-start | bytes 245768 | tf_op jit(solution)/shard_map/ppermute | solution.py:318

commit v5 on v4

--- a/solution.py
+++ b/solution.py
@@ -257,7 +257,7 @@
 
     def march(field_in):
         outs = (field_shape, jax.ShapeDtypeStruct(planes.shape, jnp.bfloat16))
-        flops = slice_count * 8 * dot_flops
+        flops = planes.shape[0] * 8 * dot_flops
         return tuple(run_kernel(march_kernel, outs, flops, field_in, planes, kernel_planes))
 
     def far_adjoint(field_in):
@@ -265,37 +265,19 @@
 
     def retreat(back_in, incidents):
         outs = (field_shape, jax.ShapeDtypeStruct(planes.shape, jnp.float32))
-        flops = slice_count * 8 * dot_flops
+        flops = planes.shape[0] * 8 * dot_flops
         return tuple(
             run_kernel(retreat_kernel, outs, flops, back_in, planes, incidents, kernel_planes)
         )
 
-    stored = jnp.zeros(planes.shape, jnp.bfloat16)
-    gradients = jnp.zeros(planes.shape, jnp.float32)
+    other = lax.ppermute(planes, "section", [(at, sections - 1 - at) for at in range(sections)])
+    both = jnp.concatenate((planes, other, planes), axis=0)
+    planes = lax.dynamic_slice_in_dim(both, section_now * slice_count, sections * slice_count, 0)
     waves = jnp.transpose(probe, (1, 0, 2))
-    for section_step in range(sections):
-        if section_step > 0:
-            waves = passed_along(waves, "section", 1)
-        waves, stored = lax.cond(
-            section_now == section_step,
-            lambda field_in, kept: march(field_in),
-            lambda field_in, kept: (field_in, kept),
-            waves,
-            stored,
-        )
-    adjoints = lax.cond(
-        is_last, lambda field_in: far_adjoint(field_in), lambda field_in: field_in, waves
-    )
-    for section_step in reversed(range(sections)):
-        if section_step < sections - 1:
-            adjoints = passed_along(adjoints, "section", -1)
-        adjoints, gradients = lax.cond(
-            section_now == section_step,
-            lambda field_in, kept: retreat(field_in, stored),
-            lambda field_in, kept: (field_in, kept),
-            adjoints,
-            gradients,
-        )
+    waves, stored = march(waves)
+    adjoints = far_adjoint(waves)
+    adjoints, gradients = retreat(adjoints, stored)
+    gradients = lax.dynamic_slice_in_dim(gradients, section_now * slice_count, slice_count, 0)
     gradients = jnp.transpose(gradients, (0, 2, 1, 3))[None]
     gradients = gradients * live_slots.astype(jnp.float32)[:, None, None, None, None]
     nearby = accumulate(gradients, offsets - tile_now * local_rows, 2 * row_size * local_rows)

time: 82.7 us -> 89.3 us (1.080)
  the two profiles are of different devices: /device:TPU:2 before, /device:TPU:1 now
where the time goes in v5:
time: 89.3 us; the launch traced here: 88.8 us
  starting transfers between devices  32 us (36%)
  waiting for transfers between devices  15.8 us (18%)
  blocking collectives  13.2 us (15%)
  Pallas kernels  12.9 us (14%)
  other arithmetic  10.7 us (12%)
  local copies, waits for them, and re-layouts  2.46 us (3%)
  between operations  1.66 us (2%)
    ppermute x2, starting transfers between devices, on_device(): lax.ppermute(object_slab, tile_axes, [(s, (s - ahead * row_size) % tile_c...  18.2 us
    all_to_all x1, blocking collectives, on_device(): incoming = lax.all_to_all(outgoing, row_axis, 0, 0).astype(jnp.float32)  13.2 us
    pallas_call x3, Pallas kernels, run_kernel(): pl.pallas_call(body, out_shape=outs, cost_estimate=pl.CostEstimate(flops=...  12.9 us
    ppermute x2, waiting for transfers between devices, on_device(): lax.ppermute(spill.astype(jnp.bfloat16), tile_axes, [(s, (s + ahead * row...  9.45 us
    ppermute x1, starting transfers between devices, on_device(): lax.ppermute(planes, 'section', [(at, sections - 1 - at) for at in range(...  5.51 us
    ppermute x2, starting transfers between devices, on_device(): lax.ppermute(spill.astype(jnp.bfloat16), tile_axes, [(s, (s + ahead * row...  4.23 us
    all_to_all x1, starting transfers between devices, on_device(): got = lax.all_to_all(sent, row_axis, 0, 0)  4.15 us
    all_to_all x1, waiting for transfers between devices, on_device(): got = lax.all_to_all(sent, row_axis, 0, 0)  3.97 us
  transfers between devices with their start and end apart: 6, of which 5 were waited for; matrix products, arithmetic and copies ran while one was open for 7% of the time, Pallas kernels for 0%

profile of v5, /device:TPU:1, one launch (start us, length us, event | category | flops | bytes accessed | tf_op | source)
XLA Modules:
  0.0 88.8 jit_solution(16640387479994557601)
XLA Ops:
  0.0 15.2 %collective-permute-start.1 = (bf16[2,40,2,256]{3,2,1,0:T(2,128)(2,1)}, bf16[2,40,2,256]{3,2,1,0:T(2,128)(2,1)S(1)}, u32[]{:S(2)}, u32[]{:S(2)}) collective-permute-start(bf16[2,40,2,256]{3,2,1,0:T(2,128)(2,1)} %param.8), channel_id=1, source_target_pairs={{0,248},{1,249},{2,250},{3,251},{4,252},{5,253},{6,254},{7,255},{8... | collective-permute-start | bytes 245768 | tf_op jit(solution)/shard_map/ppermute | solution.py:232
  15.2 3.0 %collective-permute-start = (bf16[2,40,2,256]{3,2,1,0:T(2,128)(2,1)}, bf16[2,40,2,256]{3,2,1,0:T(2,128)(2,1)S(1)}, u32[]{:S(2)}, u32[]{:S(2)}) collective-permute-start(bf16[2,40,2,256]{3,2,1,0:T(2,128)(2,1)} %param.8), channel_id=1, source_target_pairs={{0,252},{1,253},{2,254},{3,255},{4,0},{5,1},{6,2},{7,3},{8,4},{9,5... | collective-permute-start | bytes 245768 | tf_op jit(solution)/shard_map/ppermute | solution.py:232
  18.2 0.9 %collective-permute-done.1 = bf16[2,40,2,256]{3,2,1,0:T(2,128)(2,1)S(1)} collective-permute-done((bf16[2,40,2,256]{3,2,1,0:T(2,128)(2,1)}, bf16[2,40,2,256]{3,2,1,0:T(2,128)(2,1)S(1)}, u32[]{:S(2)}, u32[]{:S(2)}) %collective-permute-start.1) | collective-permute-done | bytes 81952 | tf_op jit(solution)/shard_map/ppermute | solution.py:232
  19.1 1.5 %collective-permute-done = bf16[2,40,2,256]{3,2,1,0:T(2,128)(2,1)S(1)} collective-permute-done((bf16[2,40,2,256]{3,2,1,0:T(2,128)(2,1)}, bf16[2,40,2,256]{3,2,1,0:T(2,128)(2,1)S(1)}, u32[]{:S(2)}, u32[]{:S(2)}) %collective-permute-start) | collective-permute-done | bytes 81952 | tf_op jit(solution)/shard_map/ppermute | solution.py:232
  20.6 1.2 %pad_maximum_fusion.2 = (bf16[2,2,40,2,256]{4,3,2,1,0:T(2,128)(2,1)S(1)}, bf16[2,2,40,2,256]{4,3,2,1,0:T(2,128)(2,1)S(1)}) fusion(bf16[1,2,40,2,256]{4,3,2,1,0:T(2,128)(2,1)S(1)} %bitcast.129, bf16[1,2,40,2,256]{4,3,2,1,0:T(2,128)(2,1)} %bitcast.127, bf16[1,2,40,2,256]{4,3,2,1,0:T(2,128)(2,1)S(1)} %bitcast.128), kind=kLoop, calls=%fused_computation.36 | loop fusion | flops 163840 | bytes 573440 | tf_op jit(solution)/shard_map/stack | solution.py:241
  21.9 1.0 %broadcast_select_fusion = bf16[4,2,2,40,2,256]{5,3,4,2,1,0:T(8,128)(2,1)} fusion(pred[4]{0:T(512)(128)(4,1)S(1)} %iota_compare_fusion, bf16[2,2,40,2,256]{4,2,3,1,0:T(8,128)(2,1)S(1)} %copy.16, bf16[2,2,40,2,256]{4,2,3,1,0:T(8,128)(2,1)S(1)} %copy.15), kind=kLoop, calls=%fused_computation.20 | loop fusion | flops 327680 | bytes 983044 | tf_op jit(solution)/shard_map/jit(_where)/select_n | solution.py:240
  22.8 0.0 copy-start.1
  22.8 4.1 %all-to-all-start = ((bf16[4,2,2,40,2,256]{5,3,4,2,1,0:T(8,128)(2,1)}), bf16[4,2,2,40,2,256]{5,3,4,2,1,0:T(8,128)(2,1)S(1)}, u32[]{:S(2)}, u32[]{:S(2)}) async-start(bf16[4,2,2,40,2,256]{5,3,4,2,1,0:T(8,128)(2,1)} %broadcast_select_fusion), calls=%async_computation | async-start | bytes 1310720 | tf_op jit(solution)/shard_map/all_to_all | solution.py:243
  28.3 1.0 %multiply_convert_fusion.1 = bf16[1,256,256]{1,2,0:T(8,128)(2,1)S(1)} fusion(), kind=kLoop, calls=%fused_computation.32 | loop fusion | flops 1048576 | bytes 131072 | tf_op jit(solution)/shard_map/slice | solution.py:203
  29.3 0.1 copy.19
  29.4 1.0 %multiply_convert_fusion = bf16[1,256,256]{1,2,0:T(8,128)(2,1)S(1)} fusion(), kind=kLoop, calls=%fused_computation.31 | loop fusion | flops 1114112 | bytes 131072 | tf_op jit(solution)/shard_map/slice | solution.py:203
  30.4 0.1 copy.20
  30.5 0.0 copy-done.1
  30.5 0.7 copy.30
  31.2 4.0 %all-to-all-done = bf16[4,2,2,40,2,256]{5,3,4,2,1,0:T(8,128)(2,1)S(1)} async-done(((bf16[4,2,2,40,2,256]{5,3,4,2,1,0:T(8,128)(2,1)}), bf16[4,2,2,40,2,256]{5,3,4,2,1,0:T(8,128)(2,1)S(1)}, u32[]{:S(2)}, u32[]{:S(2)}) %all-to-all-start) | async-done | bytes 655392 | tf_op jit(solution)/shard_map/all_to_all | solution.py:243
  35.2 0.2 fusion.4
  35.5 0.0 copy-start
  35.6 0.1 dynamic-slice_bitcast_fusion
  35.7 5.5 %collective-permute-start.2 = (bf16[2,2,256,256]{3,2,1,0:T(8,128)(2,1)S(1)}, bf16[2,2,256,256]{3,2,1,0:T(8,128)(2,1)S(1)}, u32[]{:S(2)}, u32[]{:S(2)}) collective-permute-start(bf16[2,2,256,256]{3,2,1,0:T(8,128)(2,1)S(1)} %dynamic-slice_bitcast_fusion), channel_id=1, source_target_pairs={{0,256},{256,0},{1,257},{257,1},{2,258},{258,2},{3,259},{259,3},{4... | collective-permute-start | bytes 1572872 | tf_op jit(solution)/shard_map/ppermute | solution.py:273
  41.3 0.0 copy-done
  41.3 0.1 copy.24
  41.4 0.1 copy.25
  41.5 1.1 %fusion.27 = (bf16[1,256,256]{2,1,0:T(8,128)(2,1)S(1)}, bf16[1,256,256]{2,1,0:T(8,128)(2,1)S(1)}) fusion(), kind=kLoop, calls=%fused_computation.71 | loop fusion | flops 1245184 | bytes 262144 | tf_op jit(solution)/shard_map/stack | solution.py:203
  42.6 0.9 pad_maximum_fusion.mat_ref
  43.5 0.9 pad_maximum_fusion.1.mat_ref
  44.4 0.0 collective-permute-done.2
  44.4 1.5 %fusion.2.patch_ref = bf16[4,2,256,256]{3,2,1,0:T(8,128)(2,1)} fusion(s32[]{:T(128)S(6)} %select_n.61, bf16[2,2,256,256]{3,2,1,0:T(8,128)(2,1)S(1)} %dynamic-slice_bitcast_fusion, bf16[2,2,256,256]{3,2,1,0:T(8,128)(2,1)S(1)} %collective-permute-done.2), kind=kLoop, calls=%fused_computation.10 | loop fusion | flops 1048576 | bytes 2097156 | tf_op jit(solution)/shard_map/concatenate | solution.py:274
  45.9 4.3 %shard_map.64 = (bf16[2,256,256]{2,1,0:T(8,128)(2,1)}, bf16[4,2,256,256]{3,2,1,0:T(8,128)(2,1)}) custom-call(bf16[2,256,256]{2,1,0:T(8,128)(2,1)} %bitcast.126, bf16[4,2,256,256]{3,2,1,0:T(8,128)(2,1)} %fusion.2.patch_ref, bf16[4,256,256]{2,1,0:T(8,128)(2,1)} %pad_maximum_fusion.mat_ref), custom_call_target="tpu_custom_call" | custom-call | flops 1073741824 | bytes 3145728 | tf_op jit(solution)/shard_map/pallas_call | solution.py:210
  50.2 3.1 %shard_map.65.back_ref = bf16[2,256,256]{2,1,0:T(8,128)(2,1)} custom-call(bf16[2,256,256]{2,1,0:T(8,128)(2,1)} %get-tuple-element.8.field_ref, bf16[256,256]{1,0:T(8,128)(2,1)} %bitcast.130, bf16[4,256,256]{2,1,0:T(8,128)(2,1)} %pad_maximum_fusion.1.mat_ref), custom_call_target="tpu_custom_call" | custom-call | flops 536870912 | bytes 1179648 | tf_op jit(solution)/shard_map/pallas_call | solution.py:210
  53.3 5.5 %shard_map.66 = (bf16[2,256,256]{2,1,0:T(8,128)(2,1)}, f32[4,2,256,256]{3,2,1,0:T(8,128)}) custom-call(bf16[2,256,256]{2,1,0:T(8,128)(2,1)} %shard_map.65.back_ref, bf16[4,2,256,256]{3,2,1,0:T(8,128)(2,1)} %fusion.2.patch_ref, bf16[4,2,256,256]{3,2,1,0:T(8,128)(2,1)} %get-tuple-element.9.incident_ref, bf16[4,256,256]{2,1,0:T(8,128)(2,1)} %pad_maximum_fusion.mat_ref), custom_call_target="tpu_custom_call" | custom-call | flops 1073741824 | bytes 5242880 | tf_op jit(solution)/shard_map/pallas_call | solution.py:210
  58.8 1.3 %multiply_bitcast_fusion = bf16[256,2,2,256]{3,0,2,1:T(8,128)(2,1)S(1)} fusion(f32[4,2,256,256]{3,2,1,0:T(8,128)} %get-tuple-element.10, s32[]{:T(128)S(6)} %select_n.63, f32[]{:T(128)} %bitcast.28), kind=kLoop, calls=%fused_computation.11 | loop fusion | flops 524288 | bytes 1572872 | tf_op jit(solution)/shard_map/mul | solution.py:282
  60.1 0.2 fusion
  60.5 0.3 fusion.3
  60.8 13.2 %all_to_all.10 = bf16[4,2,40,2,2,256]{5,2,4,3,1,0:T(8,128)(2,1)S(1)} all-to-all(bf16[4,2,40,2,2,256]{5,2,4,3,1,0:T(8,128)(2,1)S(1)} %fusion.3), channel_id=1, replica_groups=mesh['section'=2,'lines'=64,'x'=4] {'x'}, dimensions={0} | all-to-all | bytes 1310720 | tf_op jit(solution)/shard_map/all_to_all | solution.py:290
  73.9 0.2 convert_element_type.46
  74.1 0.2 select_reduce_fusion.1
  74.3 2.3 %collective-permute-start.3 = (bf16[40,2,2,256]{3,0,2,1:T(8,128)(2,1)S(1)}, bf16[40,2,2,256]{3,0,2,1:T(8,128)(2,1)S(1)}, u32[]{:S(2)}, u32[]{:S(2)}) collective-permute-start(bf16[40,2,2,256]{3,0,2,1:T(8,128)(2,1)S(1)} %get-tuple-element.22), channel_id=1, source_target_pairs={{0,4},{1,5},{2,6},{3,7},{4,8},{5,9},{6,10},{7,11},{8,12},{9,13},{1... | collective-permute-start | bytes 245768 | tf_op jit(solution)/shard_map/ppermute | solution.py:300
  76.6 1.9 %collective-permute-start.4 = (bf16[40,2,2,256]{3,0,2,1:T(8,128)(2,1)S(1)}, bf16[40,2,2,256]{3,0,2,1:T(8,128)(2,1)S(1)}, u32[]{:S(2)}, u32[]{:S(2)}) collective-permute-start(bf16[40,2,2,256]{3,0,2,1:T(8,128)(2,1)S(1)} %get-tuple-element.23), channel_id=1, source_target_pairs={{0,8},{1,9},{2,10},{3,11},{4,12},{5,13},{6,14},{7,15},{8,16},{9,17... | collective-permute-start | bytes 245768 | tf_op jit(solution)/shard_map/ppermute | solution.py:300
  78.5 4.4 %collective-permute-done.3 = bf16[40,2,2,256]{3,0,2,1:T(8,128)(2,1)S(1)} collective-permute-done((bf16[40,2,2,256]{3,0,2,1:T(8,128)(2,1)S(1)}, bf16[40,2,2,256]{3,0,2,1:T(8,128)(2,1)S(1)}, u32[]{:S(2)}, u32[]{:S(2)}) %collective-permute-start.3) | collective-permute-done | bytes 81952 | tf_op jit(solution)/shard_map/ppermute | solution.py:300
  82.9 5.1 %collective-permute-done.4 = bf16[40,2,2,256]{3,0,2,1:T(8,128)(2,1)S(1)} collective-permute-done((bf16[40,2,2,256]{3,0,2,1:T(8,128)(2,1)S(1)}, bf16[40,2,2,256]{3,0,2,1:T(8,128)(2,1)S(1)}, u32[]{:S(2)}, u32[]{:S(2)}) %collective-permute-start.4) | collective-permute-done | bytes 81952 | tf_op jit(solution)/shard_map/ppermute | solution.py:300
  88.0 0.8 copy.23
  (22 shorter events, 0.3 us)
Async XLA Ops:
  0.0 19.1 %collective-permute-start.1 = (bf16[2,40,2,256]{3,2,1,0:T(2,128)(2,1)}, bf16[2,40,2,256]{3,2,1,0:T(2,128)(2,1)S(1)}, u32[]{:S(2)}, u32[]{:S(2)}) collective-permute-start(bf16[2,40,2,256]{3,2,1,0:T(2,128)(2,1)} %param.8), channel_id=1, source_target_pairs={{0,248},{1,249},{2,250},{3,251},{4,252},{5,253},{6,254},{7,255},{8... | collective-permute-start | bytes 245768 | tf_op jit(solution)/shard_map/ppermute | solution.py:232
  15.2 5.4 %collective-permute-start = (bf16[2,40,2,256]{3,2,1,0:T(2,128)(2,1)}, bf16[2,40,2,256]{3,2,1,0:T(2,128)(2,1)S(1)}, u32[]{:S(2)}, u32[]{:S(2)}) collective-permute-start(bf16[2,40,2,256]{3,2,1,0:T(2,128)(2,1)} %param.8), channel_id=1, source_target_pairs={{0,252},{1,253},{2,254},{3,255},{4,0},{5,1},{6,2},{7,3},{8,4},{9,5... | collective-permute-start | bytes 245768 | tf_op jit(solution)/shard_map/ppermute | solution.py:232
  22.8 7.7 %copy-start.1 = (bf16[256,2,256]{2,1,0:T(2,128)(2,1)S(1)}, bf16[256,2,256]{2,1,0:T(2,128)(2,1)}, u32[]{:S(2)}) copy-start(bf16[256,2,256]{2,1,0:T(2,128)(2,1)} %param.6) | copy-start | bytes 786436
  22.8 12.4 %all-to-all-start = ((bf16[4,2,2,40,2,256]{5,3,4,2,1,0:T(8,128)(2,1)}), bf16[4,2,2,40,2,256]{5,3,4,2,1,0:T(8,128)(2,1)S(1)}, u32[]{:S(2)}, u32[]{:S(2)}) async-start(bf16[4,2,2,40,2,256]{5,3,4,2,1,0:T(8,128)(2,1)} %broadcast_select_fusion), calls=%async_computation | async-start | bytes 1310720 | tf_op jit(solution)/shard_map/all_to_all | solution.py:243
  35.5 5.8 %copy-start = (bf16[2,256,256]{2,1,0:T(8,128)(2,1)S(1)}, bf16[2,256,256]{2,1,0:T(8,128)(2,1)}, u32[]{:S(2)}) copy-start(bf16[2,256,256]{2,1,0:T(8,128)(2,1)} %param.7) | copy-start | bytes 786436
  35.7 8.6 %collective-permute-start.2 = (bf16[2,2,256,256]{3,2,1,0:T(8,128)(2,1)S(1)}, bf16[2,2,256,256]{3,2,1,0:T(8,128)(2,1)S(1)}, u32[]{:S(2)}, u32[]{:S(2)}) collective-permute-start(bf16[2,2,256,256]{3,2,1,0:T(8,128)(2,1)S(1)} %dynamic-slice_bitcast_fusion), channel_id=1, source_target_pairs={{0,256},{256,0},{1,257},{257,1},{2,258},{258,2},{3,259},{259,3},{4... | collective-permute-start | bytes 1572872 | tf_op jit(solution)/shard_map/ppermute | solution.py:273
  74.3 8.6 %collective-permute-start.3 = (bf16[40,2,2,256]{3,0,2,1:T(8,128)(2,1)S(1)}, bf16[40,2,2,256]{3,0,2,1:T(8,128)(2,1)S(1)}, u32[]{:S(2)}, u32[]{:S(2)}) collective-permute-start(bf16[40,2,2,256]{3,0,2,1:T(8,128)(2,1)S(1)} %get-tuple-element.22), channel_id=1, source_target_pairs={{0,4},{1,5},{2,6},{3,7},{4,8},{5,9},{6,10},{7,11},{8,12},{9,13},{1... | collective-permute-start | bytes 245768 | tf_op jit(solution)/shard_map/ppermute | solution.py:300
  76.6 11.4 %collective-permute-start.4 = (bf16[40,2,2,256]{3,0,2,1:T(8,128)(2,1)S(1)}, bf16[40,2,2,256]{3,0,2,1:T(8,128)(2,1)S(1)}, u32[]{:S(2)}, u32[]{:S(2)}) collective-permute-start(bf16[40,2,2,256]{3,0,2,1:T(8,128)(2,1)S(1)} %get-tuple-element.23), channel_id=1, source_target_pairs={{0,8},{1,9},{2,10},{3,11},{4,12},{5,13},{6,14},{7,15},{8,16},{9,17... | collective-permute-start | bytes 245768 | tf_op jit(solution)/shard_map/ppermute | solution.py:300

commit v6 on v5

--- a/solution.py
+++ b/solution.py
@@ -1,6 +1,8 @@
 import functools
 
 import jax
+import ml_dtypes
+import numpy as np
 from jax.experimental import pallas as pl
 import jax.numpy as jnp
 from jax import lax
@@ -201,6 +203,15 @@
 
 def planes_of(matrix):
     return jnp.stack((matrix[0], matrix[1], matrix[0].T, matrix[1].T))
+
+
+def dft_planes_of(length):
+    points = np.arange(length)
+    angle = 2.0 * np.pi * (np.outer(points, points) % length) / length
+    real = np.cos(angle) / np.sqrt(length)
+    imag = -np.sin(angle) / np.sqrt(length)
+    table = np.stack((real, imag, real.T, imag.T)).astype(ml_dtypes.bfloat16)
+    return jnp.asarray(table)
 
 
 def run_kernel(body, outs, flops, *args):
@@ -251,13 +262,13 @@
 
     planes = jnp.transpose(patches[0], (0, 2, 1, 3))
     kernel_planes = planes_of(kernel)
-    dft_planes = planes_of(dft_matrix(width))
+    dft_planes = dft_planes_of(width)
     field_shape = jax.ShapeDtypeStruct((2, width, width), jnp.bfloat16)
     dot_flops = 2 * width**3
 
     def march(field_in):
         outs = (field_shape, jax.ShapeDtypeStruct(planes.shape, jnp.bfloat16))
-        flops = planes.shape[0] * 8 * dot_flops
+        flops = slice_count * 8 * dot_flops
         return tuple(run_kernel(march_kernel, outs, flops, field_in, planes, kernel_planes))
 
     def far_adjoint(field_in):
@@ -265,19 +276,18 @@
 
     def retreat(back_in, incidents):
         outs = (field_shape, jax.ShapeDtypeStruct(planes.shape, jnp.float32))
-        flops = planes.shape[0] * 8 * dot_flops
+        flops = slice_count * 8 * dot_flops
         return tuple(
             run_kernel(retreat_kernel, outs, flops, back_in, planes, incidents, kernel_planes)
         )
 
-    other = lax.ppermute(planes, "section", [(at, sections - 1 - at) for at in range(sections)])
-    both = jnp.concatenate((planes, other, planes), axis=0)
-    planes = lax.dynamic_slice_in_dim(both, section_now * slice_count, sections * slice_count, 0)
-    waves = jnp.transpose(probe, (1, 0, 2))
-    waves, stored = march(waves)
-    adjoints = far_adjoint(waves)
-    adjoints, gradients = retreat(adjoints, stored)
-    gradients = lax.dynamic_slice_in_dim(gradients, section_now * slice_count, slice_count, 0)
+    first_section = section_now == 0
+    waves, early = march(jnp.transpose(probe, (1, 0, 2)))
+    waves, late = march(passed_along(waves, "section", 1))
+    stored = jnp.where(first_section, early, late)
+    adjoints, late = retreat(far_adjoint(waves), stored)
+    adjoints, early = retreat(passed_along(adjoints, "section", -1), stored)
+    gradients = jnp.where(first_section, early, late)
     gradients = jnp.transpose(gradients, (0, 2, 1, 3))[None]
     gradients = gradients * live_slots.astype(jnp.float32)[:, None, None, None, None]
     nearby = accumulate(gradients, offsets - tile_now * local_rows, 2 * row_size * local_rows)

time: 89.3 us -> 94.7 us (1.060)
  the two profiles are of different devices: /device:TPU:1 before, /device:TPU:2 now
where the time goes in v6:
time: 94.7 us; the launch traced here: 94.2 us
  starting transfers between devices  31.1 us (33%)
  waiting for transfers between devices  21.4 us (23%)
  Pallas kernels  16.6 us (18%)
  blocking collectives  12.6 us (13%)
  other arithmetic  6.21 us (7%)
  local copies, waits for them, and re-layouts  4.51 us (5%)
  between operations  1.64 us (2%)
    ppermute x2, starting transfers between devices, on_device(): lax.ppermute(object_slab, tile_axes, [(s, (s - ahead * row_size) % tile_c...  17.9 us
    pallas_call x5, Pallas kernels, run_kernel(): pl.pallas_call(body, out_shape=outs, cost_estimate=pl.CostEstimate(flops=...  16.6 us
    all_to_all x1, blocking collectives, on_device(): incoming = lax.all_to_all(outgoing, row_axis, 0, 0).astype(jnp.float32)  12.6 us
    ppermute x2, waiting for transfers between devices, on_device(): lax.ppermute(spill.astype(jnp.bfloat16), tile_axes, [(s, (s + ahead * row...  9.13 us
    all_to_all x1, waiting for transfers between devices, on_device(): got = lax.all_to_all(sent, row_axis, 0, 0)  5.57 us
    ppermute x2, starting transfers between devices, on_device(): lax.ppermute(spill.astype(jnp.bfloat16), tile_axes, [(s, (s + ahead * row...  5.46 us
    all_to_all x1, starting transfers between devices, on_device(): got = lax.all_to_all(sent, row_axis, 0, 0)  4.96 us
    ppermute x2, waiting for transfers between devices, on_device(): lax.ppermute(object_slab, tile_axes, [(s, (s - ahead * row_size) % tile_c...  3.37 us
  transfers between devices with their start and end apart: 7, of which 6 were waited for; matrix products, arithmetic and copies ran while one was open for 2% of the time, Pallas kernels for 0%

profile of v6, /device:TPU:2, one launch (start us, length us, event | category | flops | bytes accessed | tf_op | source)
XLA Modules:
  0.0 94.2 jit_solution(6790449675260062742)
XLA Ops:
  0.0 13.8 %collective-permute-start = (bf16[2,40,2,256]{3,2,1,0:T(2,128)(2,1)}, bf16[2,40,2,256]{3,2,1,0:T(2,128)(2,1)S(1)}, u32[]{:S(2)}, u32[]{:S(2)}) collective-permute-start(bf16[2,40,2,256]{3,2,1,0:T(2,128)(2,1)} %param.9), channel_id=1, source_target_pairs={{0,252},{1,253},{2,254},{3,255},{4,0},{5,1},{6,2},{7,3},{8,4},{9,5... | collective-permute-start | bytes 245768 | tf_op jit(solution)/shard_map/ppermute | solution.py:243
  13.9 4.1 %collective-permute-start.1 = (bf16[2,40,2,256]{3,2,1,0:T(2,128)(2,1)}, bf16[2,40,2,256]{3,2,1,0:T(2,128)(2,1)S(1)}, u32[]{:S(2)}, u32[]{:S(2)}) collective-permute-start(bf16[2,40,2,256]{3,2,1,0:T(2,128)(2,1)} %param.9), channel_id=1, source_target_pairs={{0,248},{1,249},{2,250},{3,251},{4,252},{5,253},{6,254},{7,255},{8... | collective-permute-start | bytes 245768 | tf_op jit(solution)/shard_map/ppermute | solution.py:243
  17.9 0.0 collective-permute-done
  17.9 3.4 %collective-permute-done.1 = bf16[2,40,2,256]{3,2,1,0:T(2,128)(2,1)S(1)} collective-permute-done((bf16[2,40,2,256]{3,2,1,0:T(2,128)(2,1)}, bf16[2,40,2,256]{3,2,1,0:T(2,128)(2,1)S(1)}, u32[]{:S(2)}, u32[]{:S(2)}) %collective-permute-start.1) | collective-permute-done | bytes 81952 | tf_op jit(solution)/shard_map/ppermute | solution.py:243
  21.3 1.2 %pad_maximum_fusion.1 = (bf16[2,2,40,2,256]{4,3,2,1,0:T(2,128)(2,1)S(1)}, bf16[2,2,40,2,256]{4,3,2,1,0:T(2,128)(2,1)S(1)}) fusion(bf16[1,2,40,2,256]{4,3,2,1,0:T(2,128)(2,1)S(1)} %bitcast.116, bf16[1,2,40,2,256]{4,3,2,1,0:T(2,128)(2,1)} %bitcast.115, bf16[1,2,40,2,256]{4,3,2,1,0:T(2,128)(2,1)S(1)} %bitcast.117), kind=kLoop, calls=%fused_computation.20 | loop fusion | flops 163840 | bytes 573440 | tf_op jit(solution)/shard_map/stack | solution.py:252
  22.6 0.0 copy-start.1
  22.6 1.0 %broadcast_select_fusion = bf16[4,2,2,40,2,256]{5,3,4,2,1,0:T(8,128)(2,1)} fusion(pred[4]{0:T(512)(128)(4,1)S(1)} %iota_compare_fusion, bf16[2,2,40,2,256]{4,2,3,1,0:T(8,128)(2,1)S(1)} %copy.15, bf16[2,2,40,2,256]{4,2,3,1,0:T(8,128)(2,1)S(1)} %copy.14), kind=kLoop, calls=%fused_computation.15 | loop fusion | flops 327680 | bytes 983044 | tf_op jit(solution)/shard_map/jit(_where)/select_n | solution.py:251
  23.6 0.0 copy-start.3
  23.6 5.0 %all-to-all-start = ((bf16[4,2,2,40,2,256]{5,3,4,2,1,0:T(8,128)(2,1)}), bf16[4,2,2,40,2,256]{5,3,4,2,1,0:T(8,128)(2,1)S(1)}, u32[]{:S(2)}, u32[]{:S(2)}) async-start(bf16[4,2,2,40,2,256]{5,3,4,2,1,0:T(8,128)(2,1)} %broadcast_select_fusion), calls=%async_computation | async-start | bytes 1310720 | tf_op jit(solution)/shard_map/all_to_all | solution.py:254
  29.2 0.0 copy-done.1
  29.2 0.1 copy.21
  29.3 0.1 copy.22
  29.4 0.0 copy-done.3
  29.4 0.7 copy.27
  30.2 0.9 pad_maximum_fusion.mat_ref
  31.1 5.6 %all-to-all-done = bf16[4,2,2,40,2,256]{5,3,4,2,1,0:T(8,128)(2,1)S(1)} async-done(((bf16[4,2,2,40,2,256]{5,3,4,2,1,0:T(8,128)(2,1)}), bf16[4,2,2,40,2,256]{5,3,4,2,1,0:T(8,128)(2,1)S(1)}, u32[]{:S(2)}, u32[]{:S(2)}) %all-to-all-start) | async-done | bytes 655392 | tf_op jit(solution)/shard_map/all_to_all | solution.py:254
  36.6 0.2 fusion.2
  37.0 0.9 %dynamic-slice_bitcast_fusion.patch_ref = bf16[2,2,256,256]{3,2,1,0:T(8,128)(2,1)} fusion(bf16[2,320,2,256]{3,1,2,0:T(8,128)(2,1)S(1)} %fusion.11, s32[]{:T(128)} %bitcast.13), kind=kLoop, calls=%fused_computation.17 | loop fusion | bytes 1048580 | tf_op jit(solution)/shard_map/transpose | solution.py:263
  37.9 3.1 %shard_map.73 = (bf16[2,256,256]{2,1,0:T(8,128)(2,1)}, bf16[2,2,256,256]{3,2,1,0:T(8,128)(2,1)}) custom-call(bf16[2,256,256]{2,1,0:T(8,128)(2,1)} %bitcast.114, bf16[2,2,256,256]{3,2,1,0:T(8,128)(2,1)} %dynamic-slice_bitcast_fusion.patch_ref, bf16[4,256,256]{2,1,0:T(8,128)(2,1)} %pad_maximum_fusion.mat_ref), custom_call_target="tpu_custom_call" | custom-call | flops 536870912 | bytes 2097152 | tf_op jit(solution)/shard_map/pallas_call | solution.py:221
  41.0 0.0 copy-start.2
  41.0 1.4 %collective-permute-start.2 = (bf16[2,256,256]{2,1,0:T(8,128)(2,1)}, bf16[2,256,256]{2,1,0:T(8,128)(2,1)S(1)}, u32[]{:S(2)}, u32[]{:S(2)}) collective-permute-start(bf16[2,256,256]{2,1,0:T(8,128)(2,1)} %get-tuple-element.12), channel_id=1, source_target_pairs={{0,256},{1,257},{2,258},{3,259},{4,260},{5,261},{6,262},{7,263},{8... | collective-permute-start | bytes 786440 | tf_op jit(solution)/shard_map/ppermute | solution.py:21
  42.5 1.3 %collective-permute-done.2.field_ref = bf16[2,256,256]{2,1,0:T(8,128)(2,1)S(1)} collective-permute-done((bf16[2,256,256]{2,1,0:T(8,128)(2,1)}, bf16[2,256,256]{2,1,0:T(8,128)(2,1)S(1)}, u32[]{:S(2)}, u32[]{:S(2)}) %collective-permute-start.2) | collective-permute-done | bytes 262176 | tf_op jit(solution)/shard_map/ppermute | solution.py:21
  43.8 0.0 copy-start.5
  43.8 0.7 copy-done.5
  44.5 3.1 %shard_map.74 = (bf16[2,256,256]{2,1,0:T(8,128)(2,1)}, bf16[2,2,256,256]{3,2,1,0:T(8,128)(2,1)}) custom-call(bf16[2,256,256]{2,1,0:T(8,128)(2,1)} %copy-done.5, bf16[2,2,256,256]{3,2,1,0:T(8,128)(2,1)} %dynamic-slice_bitcast_fusion.patch_ref, bf16[4,256,256]{2,1,0:T(8,128)(2,1)} %pad_maximum_fusion.mat_ref), custom_call_target="tpu_custom_call" | custom-call | flops 536870912 | bytes 2097152 | tf_op jit(solution)/shard_map/pallas_call | solution.py:221
  47.6 0.0 copy-done.2
  47.6 0.9 broadcast_select_fusion.1.incident_ref
  48.5 3.0 %shard_map.75.back_ref = bf16[2,256,256]{2,1,0:T(8,128)(2,1)} custom-call(bf16[2,256,256]{2,1,0:T(8,128)(2,1)} %get-tuple-element.13.field_ref, bf16[256,256]{1,0:T(8,128)(2,1)} %bitcast.118, bf16[4,256,256]{2,1,0:T(8,128)(2,1)} %constant.44.clone.mat_ref), custom_call_target="tpu_custom_call" | custom-call | flops 536870912 | bytes 1179648 | tf_op jit(solution)/shard_map/pallas_call | solution.py:221
  51.5 3.7 %shard_map.76 = (bf16[2,256,256]{2,1,0:T(8,128)(2,1)}, f32[2,2,256,256]{3,2,1,0:T(8,128)}) custom-call(bf16[2,256,256]{2,1,0:T(8,128)(2,1)} %shard_map.75.back_ref, bf16[2,2,256,256]{3,2,1,0:T(8,128)(2,1)} %dynamic-slice_bitcast_fusion.patch_ref, bf16[2,2,256,256]{3,2,1,0:T(8,128)(2,1)} %broadcast_select_fusion.1.incident_ref, ...), custom_call_target="tpu_custom_call" | custom-call | flops 536870912 | bytes 3145728 | tf_op jit(solution)/shard_map/pallas_call | solution.py:221
  55.3 0.0 copy-start
  55.3 1.4 %collective-permute-start.3 = (bf16[2,256,256]{2,1,0:T(8,128)(2,1)}, bf16[2,256,256]{2,1,0:T(8,128)(2,1)S(1)}, u32[]{:S(2)}, u32[]{:S(2)}) collective-permute-start(bf16[2,256,256]{2,1,0:T(8,128)(2,1)} %get-tuple-element.16), channel_id=1, source_target_pairs={{256,0},{257,1},{258,2},{259,3},{260,4},{261,5},{262,6},{263,7},{2... | collective-permute-start | bytes 786440 | tf_op jit(solution)/shard_map/ppermute | solution.py:21
  57.3 2.0 %collective-permute-done.3.back_ref = bf16[2,256,256]{2,1,0:T(8,128)(2,1)S(1)} collective-permute-done((bf16[2,256,256]{2,1,0:T(8,128)(2,1)}, bf16[2,256,256]{2,1,0:T(8,128)(2,1)S(1)}, u32[]{:S(2)}, u32[]{:S(2)}) %collective-permute-start.3) | collective-permute-done | bytes 262176 | tf_op jit(solution)/shard_map/ppermute | solution.py:21
  59.3 0.0 copy-start.4
  59.3 0.7 copy-done.4
  60.0 3.7 %shard_map.77 = (bf16[2,256,256]{2,1,0:T(8,128)(2,1)}, f32[2,2,256,256]{3,2,1,0:T(8,128)}) custom-call(bf16[2,256,256]{2,1,0:T(8,128)(2,1)} %copy-done.4, bf16[2,2,256,256]{3,2,1,0:T(8,128)(2,1)} %dynamic-slice_bitcast_fusion.patch_ref, bf16[2,2,256,256]{3,2,1,0:T(8,128)(2,1)} %broadcast_select_fusion.1.incident_ref, ...), custom_call_target="tpu_custom_call" | custom-call | flops 536870912 | bytes 3145728 | tf_op jit(solution)/shard_map/pallas_call | solution.py:221
  63.7 0.0 copy-done
  63.7 1.4 %multiply_bitcast_fusion = bf16[256,2,2,256]{3,0,2,1:T(8,128)(2,1)S(1)} fusion(f32[2,2,256,256]{3,2,1,0:T(8,128)} %get-tuple-element.17, f32[2,2,256,256]{3,2,1,0:T(8,128)S(1)} %copy-done, f32[]{:T(128)} %bitcast.22, pred[]{:T(512)S(6)} %eq.3), kind=kLoop, calls=%fused_computation.6 | loop fusion | flops 786432 | bytes 2621445 | tf_op jit(solution)/shard_map/mul | solution.py:292
  65.1 0.2 fusion
  65.5 0.3 fusion.1
  65.7 12.6 %all_to_all.10 = bf16[4,2,40,2,2,256]{5,2,4,3,1,0:T(8,128)(2,1)S(1)} all-to-all(bf16[4,2,40,2,2,256]{5,2,4,3,1,0:T(8,128)(2,1)S(1)} %fusion.1), channel_id=1, replica_groups=mesh['section'=2,'lines'=64,'x'=4] {'x'}, dimensions={0} | all-to-all | bytes 1310720 | tf_op jit(solution)/shard_map/all_to_all | solution.py:300
  78.4 0.2 convert_element_type.24
  78.5 0.2 select_reduce_fusion.1
  78.8 3.5 %collective-permute-start.4 = (bf16[40,2,2,256]{3,0,2,1:T(8,128)(2,1)S(1)}, bf16[40,2,2,256]{3,0,2,1:T(8,128)(2,1)S(1)}, u32[]{:S(2)}, u32[]{:S(2)}) collective-permute-start(bf16[40,2,2,256]{3,0,2,1:T(8,128)(2,1)S(1)} %get-tuple-element.30), channel_id=1, source_target_pairs={{0,4},{1,5},{2,6},{3,7},{4,8},{5,9},{6,10},{7,11},{8,12},{9,13},{1... | collective-permute-start | bytes 245768 | tf_op jit(solution)/shard_map/ppermute | solution.py:310
  82.3 1.9 %collective-permute-start.5 = (bf16[40,2,2,256]{3,0,2,1:T(8,128)(2,1)S(1)}, bf16[40,2,2,256]{3,0,2,1:T(8,128)(2,1)S(1)}, u32[]{:S(2)}, u32[]{:S(2)}) collective-permute-start(bf16[40,2,2,256]{3,0,2,1:T(8,128)(2,1)S(1)} %get-tuple-element.31), channel_id=1, source_target_pairs={{0,8},{1,9},{2,10},{3,11},{4,12},{5,13},{6,14},{7,15},{8,16},{9,17... | collective-permute-start | bytes 245768 | tf_op jit(solution)/shard_map/ppermute | solution.py:310
  84.2 6.7 %collective-permute-done.4 = bf16[40,2,2,256]{3,0,2,1:T(8,128)(2,1)S(1)} collective-permute-done((bf16[40,2,2,256]{3,0,2,1:T(8,128)(2,1)S(1)}, bf16[40,2,2,256]{3,0,2,1:T(8,128)(2,1)S(1)}, u32[]{:S(2)}, u32[]{:S(2)}) %collective-permute-start.4) | collective-permute-done | bytes 81952 | tf_op jit(solution)/shard_map/ppermute | solution.py:310
  91.0 2.4 %collective-permute-done.5 = bf16[40,2,2,256]{3,0,2,1:T(8,128)(2,1)S(1)} collective-permute-done((bf16[40,2,2,256]{3,0,2,1:T(8,128)(2,1)S(1)}, bf16[40,2,2,256]{3,0,2,1:T(8,128)(2,1)S(1)}, u32[]{:S(2)}, u32[]{:S(2)}) %collective-permute-start.5) | collective-permute-done | bytes 81952 | tf_op jit(solution)/shard_map/ppermute | solution.py:310
  93.4 0.8 copy.20
  (22 shorter events, 0.3 us)
Async XLA Ops:
  0.0 17.9 %collective-permute-start = (bf16[2,40,2,256]{3,2,1,0:T(2,128)(2,1)}, bf16[2,40,2,256]{3,2,1,0:T(2,128)(2,1)S(1)}, u32[]{:S(2)}, u32[]{:S(2)}) collective-permute-start(bf16[2,40,2,256]{3,2,1,0:T(2,128)(2,1)} %param.9), channel_id=1, source_target_pairs={{0,252},{1,253},{2,254},{3,255},{4,0},{5,1},{6,2},{7,3},{8,4},{9,5... | collective-permute-start | bytes 245768 | tf_op jit(solution)/shard_map/ppermute | solution.py:243
  13.9 7.5 %collective-permute-start.1 = (bf16[2,40,2,256]{3,2,1,0:T(2,128)(2,1)}, bf16[2,40,2,256]{3,2,1,0:T(2,128)(2,1)S(1)}, u32[]{:S(2)}, u32[]{:S(2)}) collective-permute-start(bf16[2,40,2,256]{3,2,1,0:T(2,128)(2,1)} %param.9), channel_id=1, source_target_pairs={{0,248},{1,249},{2,250},{3,251},{4,252},{5,253},{6,254},{7,255},{8... | collective-permute-start | bytes 245768 | tf_op jit(solution)/shard_map/ppermute | solution.py:243
  22.6 6.6 %copy-start.1 = (bf16[2,256,256]{2,1,0:T(8,128)(2,1)S(1)}, bf16[2,256,256]{2,1,0:T(8,128)(2,1)}, u32[]{:S(2)}) copy-start(bf16[2,256,256]{2,1,0:T(8,128)(2,1)} %param.8) | copy-start | bytes 786436
  23.6 5.9 %copy-start.3 = (bf16[256,2,256]{2,1,0:T(2,128)(2,1)S(1)}, bf16[256,2,256]{2,1,0:T(2,128)(2,1)}, u32[]{:S(2)}) copy-start(bf16[256,2,256]{2,1,0:T(2,128)(2,1)} %param.7) | copy-start | bytes 786436
  23.6 13.0 %all-to-all-start = ((bf16[4,2,2,40,2,256]{5,3,4,2,1,0:T(8,128)(2,1)}), bf16[4,2,2,40,2,256]{5,3,4,2,1,0:T(8,128)(2,1)S(1)}, u32[]{:S(2)}, u32[]{:S(2)}) async-start(bf16[4,2,2,40,2,256]{5,3,4,2,1,0:T(8,128)(2,1)} %broadcast_select_fusion), calls=%async_computation | async-start | bytes 1310720 | tf_op jit(solution)/shard_map/all_to_all | solution.py:254
  41.0 6.6 %copy-start.2 = (bf16[2,2,256,256]{3,2,1,0:T(8,128)(2,1)S(1)}, bf16[2,2,256,256]{3,2,1,0:T(8,128)(2,1)}, u32[]{:S(2)}) copy-start(bf16[2,2,256,256]{3,2,1,0:T(8,128)(2,1)} %get-tuple-element.14) | copy-start | bytes 1572868
  41.0 2.8 %collective-permute-start.2 = (bf16[2,256,256]{2,1,0:T(8,128)(2,1)}, bf16[2,256,256]{2,1,0:T(8,128)(2,1)S(1)}, u32[]{:S(2)}, u32[]{:S(2)}) collective-permute-start(bf16[2,256,256]{2,1,0:T(8,128)(2,1)} %get-tuple-element.12), channel_id=1, source_target_pairs={{0,256},{1,257},{2,258},{3,259},{4,260},{5,261},{6,262},{7,263},{8... | collective-permute-start | bytes 786440 | tf_op jit(solution)/shard_map/ppermute | solution.py:21
  43.8 0.7 copy-start.5
  55.3 8.4 %copy-start = (f32[2,2,256,256]{3,2,1,0:T(8,128)S(1)}, f32[2,2,256,256]{3,2,1,0:T(8,128)}, u32[]{:S(2)}) copy-start(f32[2,2,256,256]{3,2,1,0:T(8,128)} %get-tuple-element.18) | copy-start | bytes 3145732
  55.3 4.0 %collective-permute-start.3 = (bf16[2,256,256]{2,1,0:T(8,128)(2,1)}, bf16[2,256,256]{2,1,0:T(8,128)(2,1)S(1)}, u32[]{:S(2)}, u32[]{:S(2)}) collective-permute-start(bf16[2,256,256]{2,1,0:T(8,128)(2,1)} %get-tuple-element.16), channel_id=1, source_target_pairs={{256,0},{257,1},{258,2},{259,3},{260,4},{261,5},{262,6},{263,7},{2... | collective-permute-start | bytes 786440 | tf_op jit(solution)/shard_map/ppermute | solution.py:21
  59.3 0.7 copy-start.4
  78.8 12.2 %collective-permute-start.4 = (bf16[40,2,2,256]{3,0,2,1:T(8,128)(2,1)S(1)}, bf16[40,2,2,256]{3,0,2,1:T(8,128)(2,1)S(1)}, u32[]{:S(2)}, u32[]{:S(2)}) collective-permute-start(bf16[40,2,2,256]{3,0,2,1:T(8,128)(2,1)S(1)} %get-tuple-element.30), channel_id=1, source_target_pairs={{0,4},{1,5},{2,6},{3,7},{4,8},{5,9},{6,10},{7,11},{8,12},{9,13},{1... | collective-permute-start | bytes 245768 | tf_op jit(solution)/shard_map/ppermute | solution.py:310
  82.3 11.1 %collective-permute-start.5 = (bf16[40,2,2,256]{3,0,2,1:T(8,128)(2,1)S(1)}, bf16[40,2,2,256]{3,0,2,1:T(8,128)(2,1)S(1)}, u32[]{:S(2)}, u32[]{:S(2)}) collective-permute-start(bf16[40,2,2,256]{3,0,2,1:T(8,128)(2,1)S(1)} %get-tuple-element.31), channel_id=1, source_target_pairs={{0,8},{1,9},{2,10},{3,11},{4,12},{5,13},{6,14},{7,15},{8,16},{9,17... | collective-permute-start | bytes 245768 | tf_op jit(solution)/shard_map/ppermute | solution.py:310

commit v7 on v4

--- a/solution.py
+++ b/solution.py
@@ -146,9 +146,9 @@
     return (pair[0].astype(jnp.bfloat16), pair[1].astype(jnp.bfloat16))
 
 
-def march_kernel(field_ref, patch_ref, mat_ref, out_ref, incident_ref):
-    real, imag, real_t, imag_t = mat_ref[0], mat_ref[1], mat_ref[2], mat_ref[3]
-    field_real, field_imag = field_ref[0], field_ref[1]
+def march_steps(field, patch_ref, mats, incident_ref):
+    real, imag, real_t, imag_t = mats
+    field_real, field_imag = field
     for slice_at in range(patch_ref.shape[0]):
         incident_ref[slice_at, 0] = field_real
         incident_ref[slice_at, 1] = field_imag
@@ -164,25 +164,21 @@
         )
         middle = rounded(times_left(real, imag, *phase))
         field_real, field_imag = rounded(times_right(*middle, real_t, imag_t))
-    out_ref[0] = field_real
-    out_ref[1] = field_imag
-
-
-def far_kernel(field_ref, measured_ref, mat_ref, out_ref):
-    real, imag, real_t, imag_t = mat_ref[0], mat_ref[1], mat_ref[2], mat_ref[3]
-    half_far = rounded(times_left(real, imag, field_ref[0], field_ref[1]))
+    return (field_real, field_imag)
+
+
+def far_steps(field, measured, mats):
+    real, imag, real_t, imag_t = mats
+    half_far = rounded(times_left(real, imag, *field))
     far_real, far_imag = times_right(*half_far, real_t, imag_t)
-    misfit = far_real * far_real + far_imag * far_imag - measured_ref[...].astype(jnp.float32)
+    misfit = far_real * far_real + far_imag * far_imag - measured.astype(jnp.float32)
     grad_far = rounded((far_real * misfit, far_imag * misfit))
     half_back = rounded(times_left_adj(real_t, imag_t, *grad_far))
-    back_real, back_imag = rounded(times_right_conj(*half_back, real, imag))
-    out_ref[0] = back_real
-    out_ref[1] = back_imag
-
-
-def retreat_kernel(back_ref, patch_ref, incident_ref, mat_ref, out_ref, grad_ref):
-    real, imag, real_t, imag_t = mat_ref[0], mat_ref[1], mat_ref[2], mat_ref[3]
-    back = (back_ref[0], back_ref[1])
+    return rounded(times_right_conj(*half_back, real, imag))
+
+
+def retreat_steps(back, patch_ref, incident_ref, mats, grad_ref):
+    real, imag, real_t, imag_t = mats
     for slice_at in reversed(range(patch_ref.shape[0])):
         middle = rounded(times_left_adj(real_t, imag_t, *back))
         bar_real, bar_imag = times_right_conj(*middle, real, imag)
@@ -195,6 +191,34 @@
         back = rounded(
             (pat_real * bar_real + pat_imag * bar_imag, pat_real * bar_imag - pat_imag * bar_real)
         )
+    return back
+
+
+def mats_of(mat_ref):
+    return (mat_ref[0], mat_ref[1], mat_ref[2], mat_ref[3])
+
+
+def march_kernel(field_ref, patch_ref, mat_ref, out_ref, incident_ref):
+    field = march_steps((field_ref[0], field_ref[1]), patch_ref, mats_of(mat_ref), incident_ref)
+    out_ref[0] = field[0]
+    out_ref[1] = field[1]
+
+
+def middle_kernel(
+    field_ref, patch_ref, mat_ref, measured_ref, dft_ref, out_ref, grad_ref, incident_ref
+):
+    mats = mats_of(mat_ref)
+    field = march_steps((field_ref[0], field_ref[1]), patch_ref, mats, incident_ref)
+    back = far_steps(field, measured_ref[...], mats_of(dft_ref))
+    back = retreat_steps(back, patch_ref, incident_ref, mats, grad_ref)
+    out_ref[0] = back[0]
+    out_ref[1] = back[1]
+
+
+def retreat_kernel(back_ref, patch_ref, incident_ref, mat_ref, out_ref, grad_ref):
+    back = retreat_steps(
+        (back_ref[0], back_ref[1]), patch_ref, incident_ref, mats_of(mat_ref), grad_ref
+    )
     out_ref[0] = back[0]
     out_ref[1] = back[1]
 
@@ -260,9 +284,6 @@
         flops = slice_count * 8 * dot_flops
         return tuple(run_kernel(march_kernel, outs, flops, field_in, planes, kernel_planes))
 
-    def far_adjoint(field_in):
-        return run_kernel(far_kernel, field_shape, 16 * dot_flops, field_in, intensity[0], dft_planes)
-
     def retreat(back_in, incidents):
         outs = (field_shape, jax.ShapeDtypeStruct(planes.shape, jnp.float32))
         flops = slice_count * 8 * dot_flops
@@ -270,10 +291,22 @@
             run_kernel(retreat_kernel, outs, flops, back_in, planes, incidents, kernel_planes)
         )
 
+    def whole(field_in):
+        outs = (
+            field_shape,
+            jax.ShapeDtypeStruct(planes.shape, jnp.float32),
+            jax.ShapeDtypeStruct(planes.shape, jnp.bfloat16),
+        )
+        flops = slice_count * 16 * dot_flops + 16 * dot_flops
+        back, grads, _ = run_kernel(
+            middle_kernel, outs, flops, field_in, planes, kernel_planes, intensity[0], dft_planes
+        )
+        return (back, grads)
+
     stored = jnp.zeros(planes.shape, jnp.bfloat16)
     gradients = jnp.zeros(planes.shape, jnp.float32)
     waves = jnp.transpose(probe, (1, 0, 2))
-    for section_step in range(sections):
+    for section_step in range(sections - 1):
         if section_step > 0:
             waves = passed_along(waves, "section", 1)
         waves, stored = lax.cond(
@@ -283,12 +316,16 @@
             waves,
             stored,
         )
-    adjoints = lax.cond(
-        is_last, lambda field_in: far_adjoint(field_in), lambda field_in: field_in, waves
-    )
-    for section_step in reversed(range(sections)):
-        if section_step < sections - 1:
-            adjoints = passed_along(adjoints, "section", -1)
+    waves = passed_along(waves, "section", 1)
+    adjoints, gradients = lax.cond(
+        is_last,
+        lambda field_in, kept: whole(field_in),
+        lambda field_in, kept: (field_in, kept),
+        waves,
+        gradients,
+    )
+    for section_step in reversed(range(sections - 1)):
+        adjoints = passed_along(adjoints, "section", -1)
         adjoints, gradients = lax.cond(
             section_now == section_step,
             lambda field_in, kept: retreat(field_in, stored),

time: 82.7 us -> 79.5 us (0.961)
  waiting for transfers between devices: 25.5 us -> 21.7 us
    ppermute x2, waiting for transfers between devices: 6.91 us -> 3.1 us  [passed_along(): return lax.ppermute(shard, axis, pairs)]
    unnamed x23, local copies, waits for them, and re-layouts: 1.22 us -> 0.35 us
  transfers between devices with their start and end apart: 7 -> 7, of which waited for: 5 -> 5; matrix products, arithmetic and copies ran while one was open for 4% -> 5% of each run, Pallas kernels for 0% -> 0%
where the time goes in v7:
time: 79.5 us; the launch traced here: 79.1 us
  starting transfers between devices  31 us (39%)
  waiting for transfers between devices  21.7 us (27%)
  blocking collectives  12 us (15%)
  other arithmetic  6.41 us (8%)
  Pallas kernels  3.71 us (5%)
  local copies, waits for them, and re-layouts  2.54 us (3%)
  between operations  1.72 us (2%)
    ppermute x2, starting transfers between devices, on_device(): lax.ppermute(object_slab, tile_axes, [(s, (s - ahead * row_size) % tile_c...  17.9 us
    all_to_all x1, blocking collectives, on_device(): incoming = lax.all_to_all(outgoing, row_axis, 0, 0).astype(jnp.float32)  12 us
    ppermute x2, waiting for transfers between devices, on_device(): lax.ppermute(spill.astype(jnp.bfloat16), tile_axes, [(s, (s + ahead * row...  9.12 us
    all_to_all x1, waiting for transfers between devices, on_device(): got = lax.all_to_all(sent, row_axis, 0, 0)  6.07 us
    ppermute x2, starting transfers between devices, on_device(): lax.ppermute(spill.astype(jnp.bfloat16), tile_axes, [(s, (s + ahead * row...  5.46 us
    all_to_all x1, starting transfers between devices, on_device(): got = lax.all_to_all(sent, row_axis, 0, 0)  4.96 us
    pallas_call x2, Pallas kernels, run_kernel(): pl.pallas_call(body, out_shape=outs, cost_estimate=pl.CostEstimate(flops=...  3.71 us
    ppermute x2, waiting for transfers between devices, on_device(): lax.ppermute(object_slab, tile_axes, [(s, (s - ahead * row_size) % tile_c...  3.37 us
  transfers between devices with their start and end apart: 7, of which 5 were waited for; matrix products, arithmetic and copies ran while one was open for 5% of the time, Pallas kernels for 0%

profile of v7, /device:TPU:2, one launch (start us, length us, event | category | flops | bytes accessed | tf_op | source)
XLA Modules:
  0.0 79.1 jit_solution(1155130110995563574)
XLA Ops:
  0.0 13.8 %collective-permute-start = (bf16[2,40,2,256]{3,2,1,0:T(2,128)(2,1)}, bf16[2,40,2,256]{3,2,1,0:T(2,128)(2,1)S(1)}, u32[]{:S(2)}, u32[]{:S(2)}) collective-permute-start(bf16[2,40,2,256]{3,2,1,0:T(2,128)(2,1)} %param.14), channel_id=1, source_target_pairs={{0,252},{1,253},{2,254},{3,255},{4,0},{5,1},{6,2},{7,3},{8,4},{9,5... | collective-permute-start | bytes 245768 | tf_op jit(solution)/shard_map/ppermute | solution.py:256
  13.9 4.1 %collective-permute-start.1 = (bf16[2,40,2,256]{3,2,1,0:T(2,128)(2,1)}, bf16[2,40,2,256]{3,2,1,0:T(2,128)(2,1)S(1)}, u32[]{:S(2)}, u32[]{:S(2)}) collective-permute-start(bf16[2,40,2,256]{3,2,1,0:T(2,128)(2,1)} %param.14), channel_id=1, source_target_pairs={{0,248},{1,249},{2,250},{3,251},{4,252},{5,253},{6,254},{7,255},{8... | collective-permute-start | bytes 245768 | tf_op jit(solution)/shard_map/ppermute | solution.py:256
  17.9 0.0 collective-permute-done
  17.9 3.4 %collective-permute-done.1 = bf16[2,40,2,256]{3,2,1,0:T(2,128)(2,1)S(1)} collective-permute-done((bf16[2,40,2,256]{3,2,1,0:T(2,128)(2,1)}, bf16[2,40,2,256]{3,2,1,0:T(2,128)(2,1)S(1)}, u32[]{:S(2)}, u32[]{:S(2)}) %collective-permute-start.1) | collective-permute-done | bytes 81952 | tf_op jit(solution)/shard_map/ppermute | solution.py:256
  21.3 1.2 %pad_maximum_fusion.2 = (bf16[2,2,40,2,256]{4,3,2,1,0:T(2,128)(2,1)S(1)}, bf16[2,2,40,2,256]{4,3,2,1,0:T(2,128)(2,1)S(1)}) fusion(bf16[1,2,40,2,256]{4,3,2,1,0:T(2,128)(2,1)S(1)} %bitcast.127, bf16[1,2,40,2,256]{4,3,2,1,0:T(2,128)(2,1)} %bitcast.126, bf16[1,2,40,2,256]{4,3,2,1,0:T(2,128)(2,1)S(1)} %bitcast.128), kind=kLoop, calls=%fused_computation.30 | loop fusion | flops 163840 | bytes 573440 | tf_op jit(solution)/shard_map/stack | solution.py:265
  22.6 0.0 copy-start
  22.6 1.0 %broadcast_select_fusion = bf16[4,2,2,40,2,256]{5,3,4,2,1,0:T(8,128)(2,1)} fusion(pred[4]{0:T(512)(128)(4,1)S(1)} %iota_compare_fusion, bf16[2,2,40,2,256]{4,2,3,1,0:T(8,128)(2,1)S(1)} %copy.26, bf16[2,2,40,2,256]{4,2,3,1,0:T(8,128)(2,1)S(1)} %copy.25), kind=kLoop, calls=%fused_computation.14 | loop fusion | flops 327680 | bytes 983044 | tf_op jit(solution)/shard_map/jit(_where)/select_n | solution.py:264
  23.6 0.0 copy-start.1
  23.6 5.0 %all-to-all-start = ((bf16[4,2,2,40,2,256]{5,3,4,2,1,0:T(8,128)(2,1)}), bf16[4,2,2,40,2,256]{5,3,4,2,1,0:T(8,128)(2,1)S(1)}, u32[]{:S(2)}, u32[]{:S(2)}) async-start(bf16[4,2,2,40,2,256]{5,3,4,2,1,0:T(8,128)(2,1)} %broadcast_select_fusion), calls=%async_computation | async-start | bytes 1310720 | tf_op jit(solution)/shard_map/all_to_all | solution.py:267
  29.2 0.0 copy-done
  29.2 0.1 copy.34
  29.3 0.1 copy.35
  29.4 0.0 copy-done.1
  29.5 1.0 %multiply_convert_fusion.1 = bf16[1,256,256]{1,2,0:T(8,128)(2,1)S(1)} fusion(), kind=kLoop, calls=%fused_computation.26 | loop fusion | flops 1048576 | bytes 131072 | tf_op jit(solution)/shard_map/slice | solution.py:227
  30.5 0.1 pad_maximum_fusion
  30.6 6.1 %all-to-all-done = bf16[4,2,2,40,2,256]{5,3,4,2,1,0:T(8,128)(2,1)S(1)} async-done(((bf16[4,2,2,40,2,256]{5,3,4,2,1,0:T(8,128)(2,1)}), bf16[4,2,2,40,2,256]{5,3,4,2,1,0:T(8,128)(2,1)S(1)}, u32[]{:S(2)}, u32[]{:S(2)}) %all-to-all-start) | async-done | bytes 655392 | tf_op jit(solution)/shard_map/all_to_all | solution.py:267
  36.6 0.2 fusion.2
  37.0 0.1 dynamic-slice_bitcast_fusion
  37.1 1.8 %conditional.3 = ((bf16[2,256,256]{2,1,0:T(8,128)(2,1)}, bf16[2,2,256,256]{3,2,1,0:T(8,128)(2,1)S(1)})) conditional(s32[]{:T(128)} %convert_element_type.51, bf16[2,256,256]{2,1,0:T(8,128)(2,1)S(1)} %bitcast.121, (bf16[2,256,256]{2,1,0:T(8,128)(2,1)S(1)}, bf16[2,2,256,256]{3,2,1,0:T(8,128)(2,1)S(1)}, bf16[4,256,256]{2,1,0:T(8,128)(2,1)S(1)}) %tuple.51), branch_computations={%region_0.1_spmd, %region_1.2_spmd} | conditional | flops 536870912 | bytes 2097160 | solution.py:312
  37.2 1.8 %branch_1_fun.3 = (bf16[2,256,256]{2,1,0:T(8,128)(2,1)}, bf16[2,2,256,256]{3,2,1,0:T(8,128)(2,1)S(1)}) custom-call(bf16[2,256,256]{2,1,0:T(8,128)(2,1)S(1)} %get-tuple-element.36.field_ref, bf16[2,2,256,256]{3,2,1,0:T(8,128)(2,1)S(1)} %get-tuple-element.37.patch_ref, bf16[4,256,256]{2,1,0:T(8,128)(2,1)S(1)} %get-tuple-element.38.mat_ref), custom_call_target="tpu_custom_call" | custom-call | flops 536870912 | bytes 2097152 | tf_op jit(solution)/shard_map/cond/branch_1_fun/pallas_call | solution.py:234
  39.0 0.0 copy-start.2
  39.0 1.4 %collective-permute-start.2 = (bf16[2,256,256]{2,1,0:T(8,128)(2,1)}, bf16[2,256,256]{2,1,0:T(8,128)(2,1)S(1)}, u32[]{:S(2)}, u32[]{:S(2)}) collective-permute-start(bf16[2,256,256]{2,1,0:T(8,128)(2,1)} %get-tuple-element.55), channel_id=1, source_target_pairs={{0,256},{1,257},{2,258},{3,259},{4,260},{5,261},{6,262},{7,263},{8... | collective-permute-start | bytes 786440 | tf_op jit(solution)/shard_map/ppermute | solution.py:19
  40.4 1.0 %multiply_convert_fusion = bf16[1,256,256]{1,2,0:T(8,128)(2,1)S(1)} fusion(), kind=kLoop, calls=%fused_computation.25 | loop fusion | flops 1114112 | bytes 131072 | tf_op jit(solution)/shard_map/slice | solution.py:227
  41.4 0.1 copy.29
  41.5 0.1 copy.30
  41.6 1.1 %fusion.25 = (bf16[1,256,256]{2,1,0:T(8,128)(2,1)S(1)}, bf16[1,256,256]{2,1,0:T(8,128)(2,1)S(1)}) fusion(), kind=kLoop, calls=%fused_computation.65 | loop fusion | flops 1245184 | bytes 262144 | tf_op jit(solution)/shard_map/stack | solution.py:227
  42.7 0.1 pad_maximum_fusion.1
  42.8 0.0 collective-permute-done.2
  42.8 0.0 copy-done.2
  42.8 0.8 %conditional.4 = (bf16[2,256,256]{2,1,0:T(8,128)(2,1)}, f32[2,2,256,256]{3,2,1,0:T(8,128)S(1)}) conditional(s32[]{:T(128)} %convert_element_type.52, bf16[2,256,256]{2,1,0:T(8,128)(2,1)S(1)} %collective-permute-done.2, (bf16[1,256,256]{2,1,0:T(8,128)(2,1)S(1)}, bf16[2,256,256]{2,1,0:T(8,128)(2,1)S(1)}, bf16[2,2,256,256]{3,2,1,0:T(8,128)(2,1)S(1)}, ...), branch_computations={%region_2.3_spmd, %region_3.4_spmd} | conditional | flops 1610612736 | bytes 3801104 | solution.py:320
  42.9 0.7 copy.50
  43.6 0.1 broadcast_in_dim.47
  43.7 1.3 %collective-permute-start.3 = (bf16[2,256,256]{2,1,0:T(8,128)(2,1)}, bf16[2,256,256]{2,1,0:T(8,128)(2,1)S(1)}, u32[]{:S(2)}, u32[]{:S(2)}) collective-permute-start(bf16[2,256,256]{2,1,0:T(8,128)(2,1)} %get-tuple-element.57), channel_id=1, source_target_pairs={{256,0},{257,1},{258,2},{259,3},{260,4},{261,5},{262,6},{263,7},{2... | collective-permute-start | bytes 786440 | tf_op jit(solution)/shard_map/ppermute | solution.py:19
  45.6 3.1 %collective-permute-done.3 = bf16[2,256,256]{2,1,0:T(8,128)(2,1)S(1)} collective-permute-done((bf16[2,256,256]{2,1,0:T(8,128)(2,1)}, bf16[2,256,256]{2,1,0:T(8,128)(2,1)S(1)}, u32[]{:S(2)}, u32[]{:S(2)}) %collective-permute-start.3) | collective-permute-done | bytes 262176 | tf_op jit(solution)/shard_map/ppermute | solution.py:19
  48.7 1.9 %conditional.5 = (f32[2,2,256,256]{3,2,1,0:T(8,128)S(1)}) conditional(s32[]{:T(128)} %convert_element_type.51, f32[2,2,256,256]{3,2,1,0:T(8,128)S(1)} %get-tuple-element.56, (bf16[2,256,256]{2,1,0:T(8,128)(2,1)S(1)}, bf16[2,2,256,256]{3,2,1,0:T(8,128)(2,1)S(1)}, bf16[2,2,256,256]{3,2,1,0:T(8,128)(2,1)S(1)}, bf16[4,256,256]{2,1,0:T(8,128)(2,1)S(1)}) %tuple.32), branch_computations={%region_4.5_spmd, %region_5.6_spmd} | conditional | flops 536870912 | bytes 3145736 | solution.py:329
  48.7 1.9 %branch_1_fun.5 = (bf16[2,256,256]{2,1,0:T(8,128)(2,1)}, f32[2,2,256,256]{3,2,1,0:T(8,128)S(1)}) custom-call(bf16[2,256,256]{2,1,0:T(8,128)(2,1)S(1)} %get-tuple-element.46.back_ref, bf16[2,2,256,256]{3,2,1,0:T(8,128)(2,1)S(1)} %get-tuple-element.47.patch_ref, bf16[2,2,256,256]{3,2,1,0:T(8,128)(2,1)S(1)} %get-tuple-element.48.incident_ref, ...), custom_call_target="tpu_custom_call" | custom-call | flops 536870912 | bytes 3145728 | tf_op jit(solution)/shard_map/cond/branch_1_fun/pallas_call | solution.py:234
  50.6 0.1 multiply_bitcast_fusion
  50.7 0.2 fusion
  51.0 0.3 fusion.1
  51.4 12.0 %all_to_all.10 = bf16[4,2,40,2,2,256]{5,2,4,3,1,0:T(8,128)(2,1)S(1)} all-to-all(bf16[4,2,40,2,2,256]{5,2,4,3,1,0:T(8,128)(2,1)S(1)} %copy.31), channel_id=1, replica_groups=mesh['section'=2,'lines'=64,'x'=4] {'x'}, dimensions={0} | all-to-all | bytes 1310720 | tf_op jit(solution)/shard_map/all_to_all | solution.py:345
  63.3 0.2 convert_element_type.55
  63.5 0.2 select_reduce_fusion.1
  63.7 3.5 %collective-permute-start.4 = (bf16[40,2,2,256]{3,0,2,1:T(8,128)(2,1)S(1)}, bf16[40,2,2,256]{3,0,2,1:T(8,128)(2,1)S(1)}, u32[]{:S(2)}, u32[]{:S(2)}) collective-permute-start(bf16[40,2,2,256]{3,0,2,1:T(8,128)(2,1)S(1)} %get-tuple-element.72), channel_id=1, source_target_pairs={{0,4},{1,5},{2,6},{3,7},{4,8},{5,9},{6,10},{7,11},{8,12},{9,13},{1... | collective-permute-start | bytes 245768 | tf_op jit(solution)/shard_map/ppermute | solution.py:355
  67.3 1.9 %collective-permute-start.5 = (bf16[40,2,2,256]{3,0,2,1:T(8,128)(2,1)S(1)}, bf16[40,2,2,256]{3,0,2,1:T(8,128)(2,1)S(1)}, u32[]{:S(2)}, u32[]{:S(2)}) collective-permute-start(bf16[40,2,2,256]{3,0,2,1:T(8,128)(2,1)S(1)} %get-tuple-element.73), channel_id=1, source_target_pairs={{0,8},{1,9},{2,10},{3,11},{4,12},{5,13},{6,14},{7,15},{8,16},{9,17... | collective-permute-start | bytes 245768 | tf_op jit(solution)/shard_map/ppermute | solution.py:355
  69.2 6.3 %collective-permute-done.4 = bf16[40,2,2,256]{3,0,2,1:T(8,128)(2,1)S(1)} collective-permute-done((bf16[40,2,2,256]{3,0,2,1:T(8,128)(2,1)S(1)}, bf16[40,2,2,256]{3,0,2,1:T(8,128)(2,1)S(1)}, u32[]{:S(2)}, u32[]{:S(2)}) %collective-permute-start.4) | collective-permute-done | bytes 81952 | tf_op jit(solution)/shard_map/ppermute | solution.py:355
  75.5 2.8 %collective-permute-done.5 = bf16[40,2,2,256]{3,0,2,1:T(8,128)(2,1)S(1)} collective-permute-done((bf16[40,2,2,256]{3,0,2,1:T(8,128)(2,1)S(1)}, bf16[40,2,2,256]{3,0,2,1:T(8,128)(2,1)S(1)}, u32[]{:S(2)}, u32[]{:S(2)}) %collective-permute-start.5) | collective-permute-done | bytes 81952 | tf_op jit(solution)/shard_map/ppermute | solution.py:355
  78.4 0.8 copy.33
  (23 shorter events, 0.3 us)
Async XLA Ops:
  0.0 17.9 %collective-permute-start = (bf16[2,40,2,256]{3,2,1,0:T(2,128)(2,1)}, bf16[2,40,2,256]{3,2,1,0:T(2,128)(2,1)S(1)}, u32[]{:S(2)}, u32[]{:S(2)}) collective-permute-start(bf16[2,40,2,256]{3,2,1,0:T(2,128)(2,1)} %param.14), channel_id=1, source_target_pairs={{0,252},{1,253},{2,254},{3,255},{4,0},{5,1},{6,2},{7,3},{8,4},{9,5... | collective-permute-start | bytes 245768 | tf_op jit(solution)/shard_map/ppermute | solution.py:256
  13.9 7.5 %collective-permute-start.1 = (bf16[2,40,2,256]{3,2,1,0:T(2,128)(2,1)}, bf16[2,40,2,256]{3,2,1,0:T(2,128)(2,1)S(1)}, u32[]{:S(2)}, u32[]{:S(2)}) collective-permute-start(bf16[2,40,2,256]{3,2,1,0:T(2,128)(2,1)} %param.14), channel_id=1, source_target_pairs={{0,248},{1,249},{2,250},{3,251},{4,252},{5,253},{6,254},{7,255},{8... | collective-permute-start | bytes 245768 | tf_op jit(solution)/shard_map/ppermute | solution.py:256
  22.6 6.6 %copy-start = (bf16[2,256,256]{2,1,0:T(8,128)(2,1)S(1)}, bf16[2,256,256]{2,1,0:T(8,128)(2,1)}, u32[]{:S(2)}) copy-start(bf16[2,256,256]{2,1,0:T(8,128)(2,1)} %param.13) | copy-start | bytes 786436
  23.6 5.9 %copy-start.1 = (bf16[256,2,256]{2,1,0:T(2,128)(2,1)S(1)}, bf16[256,2,256]{2,1,0:T(2,128)(2,1)}, u32[]{:S(2)}) copy-start(bf16[256,2,256]{2,1,0:T(2,128)(2,1)} %param.12) | copy-start | bytes 786436
  23.6 13.0 %all-to-all-start = ((bf16[4,2,2,40,2,256]{5,3,4,2,1,0:T(8,128)(2,1)}), bf16[4,2,2,40,2,256]{5,3,4,2,1,0:T(8,128)(2,1)S(1)}, u32[]{:S(2)}, u32[]{:S(2)}) async-start(bf16[4,2,2,40,2,256]{5,3,4,2,1,0:T(8,128)(2,1)} %broadcast_select_fusion), calls=%async_computation | async-start | bytes 1310720 | tf_op jit(solution)/shard_map/all_to_all | solution.py:267
  39.0 3.9 %copy-start.2 = (bf16[1,256,256]{2,1,0:T(8,128)(2,1)S(1)}, bf16[1,256,256]{2,1,0:T(8,128)(2,1)}, u32[]{:S(2)}) copy-start(bf16[1,256,256]{2,1,0:T(8,128)(2,1)} %param.17) | copy-start | bytes 393220
  39.0 3.8 %collective-permute-start.2 = (bf16[2,256,256]{2,1,0:T(8,128)(2,1)}, bf16[2,256,256]{2,1,0:T(8,128)(2,1)S(1)}, u32[]{:S(2)}, u32[]{:S(2)}) collective-permute-start(bf16[2,256,256]{2,1,0:T(8,128)(2,1)} %get-tuple-element.55), channel_id=1, source_target_pairs={{0,256},{1,257},{2,258},{3,259},{4,260},{5,261},{6,262},{7,263},{8... | collective-permute-start | bytes 786440 | tf_op jit(solution)/shard_map/ppermute | solution.py:19
  43.7 5.1 %collective-permute-start.3 = (bf16[2,256,256]{2,1,0:T(8,128)(2,1)}, bf16[2,256,256]{2,1,0:T(8,128)(2,1)S(1)}, u32[]{:S(2)}, u32[]{:S(2)}) collective-permute-start(bf16[2,256,256]{2,1,0:T(8,128)(2,1)} %get-tuple-element.57), channel_id=1, source_target_pairs={{256,0},{257,1},{258,2},{259,3},{260,4},{261,5},{262,6},{263,7},{2... | collective-permute-start | bytes 786440 | tf_op jit(solution)/shard_map/ppermute | solution.py:19
  63.7 11.8 %collective-permute-start.4 = (bf16[40,2,2,256]{3,0,2,1:T(8,128)(2,1)S(1)}, bf16[40,2,2,256]{3,0,2,1:T(8,128)(2,1)S(1)}, u32[]{:S(2)}, u32[]{:S(2)}) collective-permute-start(bf16[40,2,2,256]{3,0,2,1:T(8,128)(2,1)S(1)} %get-tuple-element.72), channel_id=1, source_target_pairs={{0,4},{1,5},{2,6},{3,7},{4,8},{5,9},{6,10},{7,11},{8,12},{9,13},{1... | collective-permute-start | bytes 245768 | tf_op jit(solution)/shard_map/ppermute | solution.py:355
  67.3 11.0 %collective-permute-start.5 = (bf16[40,2,2,256]{3,0,2,1:T(8,128)(2,1)S(1)}, bf16[40,2,2,256]{3,0,2,1:T(8,128)(2,1)S(1)}, u32[]{:S(2)}, u32[]{:S(2)}) collective-permute-start(bf16[40,2,2,256]{3,0,2,1:T(8,128)(2,1)S(1)} %get-tuple-element.73), channel_id=1, source_target_pairs={{0,8},{1,9},{2,10},{3,11},{4,12},{5,13},{6,14},{7,15},{8,16},{9,17... | collective-permute-start | bytes 245768 | tf_op jit(solution)/shard_map/ppermute | solution.py:355

commit v8 on v7

--- a/solution.py
+++ b/solution.py
@@ -114,31 +114,45 @@
     return jnp.dot(first, second, preferred_element_type=jnp.float32)
 
 
-def times_left(real, imag, field_real, field_imag):
+def times_left(stacked, field_real, field_imag):
+    side = field_real.shape[0]
+    with_real = real_dot(stacked, field_real)
+    with_imag = real_dot(stacked, field_imag)
     return (
-        real_dot(real, field_real) - real_dot(imag, field_imag),
-        real_dot(real, field_imag) + real_dot(imag, field_real),
-    )
-
-
-def times_left_adj(real_t, imag_t, field_real, field_imag):
+        with_real[:side] - with_imag[side:],
+        with_imag[:side] + with_real[side:],
+    )
+
+
+def times_left_adj(stacked_t, field_real, field_imag):
+    side = field_real.shape[0]
+    with_real = real_dot(stacked_t, field_real)
+    with_imag = real_dot(stacked_t, field_imag)
     return (
-        real_dot(real_t, field_real) + real_dot(imag_t, field_imag),
-        real_dot(real_t, field_imag) - real_dot(imag_t, field_real),
+        with_real[:side] + with_imag[side:],
+        with_imag[:side] - with_real[side:],
     )
 
 
 def times_right(field_real, field_imag, real_t, imag_t):
+    side = field_real.shape[0]
+    both = jnp.concatenate((field_real, field_imag), axis=0)
+    with_real = real_dot(both, real_t)
+    with_imag = real_dot(both, imag_t)
     return (
-        real_dot(field_real, real_t) - real_dot(field_imag, imag_t),
-        real_dot(field_real, imag_t) + real_dot(field_imag, real_t),
+        with_real[:side] - with_imag[side:],
+        with_imag[:side] + with_real[side:],
     )
 
 
 def times_right_conj(field_real, field_imag, real, imag):
+    side = field_real.shape[0]
+    both = jnp.concatenate((field_real, field_imag), axis=0)
+    with_real = real_dot(both, real)
+    with_imag = real_dot(both, imag)
     return (
-        real_dot(field_real, real) + real_dot(field_imag, imag),
-        real_dot(field_imag, real) - real_dot(field_real, imag),
+        with_real[:side] + with_imag[side:],
+        with_real[side:] - with_imag[:side],
     )
 
 
@@ -147,7 +161,7 @@
 
 
 def march_steps(field, patch_ref, mats, incident_ref):
-    real, imag, real_t, imag_t = mats
+    stacked, stacked_t, real, imag, real_t, imag_t = mats
     field_real, field_imag = field
     for slice_at in range(patch_ref.shape[0]):
         incident_ref[slice_at, 0] = field_real
@@ -162,25 +176,25 @@
                 first_real * second_imag + first_imag * second_real,
             )
         )
-        middle = rounded(times_left(real, imag, *phase))
+        middle = rounded(times_left(stacked, *phase))
         field_real, field_imag = rounded(times_right(*middle, real_t, imag_t))
     return (field_real, field_imag)
 
 
 def far_steps(field, measured, mats):
-    real, imag, real_t, imag_t = mats
-    half_far = rounded(times_left(real, imag, *field))
+    stacked, stacked_t, real, imag, real_t, imag_t = mats
+    half_far = rounded(times_left(stacked, *field))
     far_real, far_imag = times_right(*half_far, real_t, imag_t)
     misfit = far_real * far_real + far_imag * far_imag - measured.astype(jnp.float32)
     grad_far = rounded((far_real * misfit, far_imag * misfit))
-    half_back = rounded(times_left_adj(real_t, imag_t, *grad_far))
+    half_back = rounded(times_left_adj(stacked_t, *grad_far))
     return rounded(times_right_conj(*half_back, real, imag))
 
 
 def retreat_steps(back, patch_ref, incident_ref, mats, grad_ref):
-    real, imag, real_t, imag_t = mats
+    stacked, stacked_t, real, imag, real_t, imag_t = mats
     for slice_at in reversed(range(patch_ref.shape[0])):
-        middle = rounded(times_left_adj(real_t, imag_t, *back))
+        middle = rounded(times_left_adj(stacked_t, *back))
         bar_real, bar_imag = times_right_conj(*middle, real, imag)
         inc_real = incident_ref[slice_at, 0].astype(jnp.float32)
         inc_imag = incident_ref[slice_at, 1].astype(jnp.float32)
@@ -195,7 +209,9 @@
 
 
 def mats_of(mat_ref):
-    return (mat_ref[0], mat_ref[1], mat_ref[2], mat_ref[3])
+    stacked, stacked_t = mat_ref[0], mat_ref[1]
+    side = stacked.shape[1]
+    return (stacked, stacked_t, stacked[:side], stacked[side:], stacked_t[:side], stacked_t[side:])
 
 
 def march_kernel(field_ref, patch_ref, mat_ref, out_ref, incident_ref):
@@ -224,7 +240,9 @@
 
 
 def planes_of(matrix):
-    return jnp.stack((matrix[0], matrix[1], matrix[0].T, matrix[1].T))
+    stacked = jnp.concatenate((matrix[0], matrix[1]), axis=0)
+    stacked_t = jnp.concatenate((matrix[0].T, matrix[1].T), axis=0)
+    return jnp.stack((stacked, stacked_t))
 
 
 def run_kernel(body, outs, flops, *args):

time: 79.5 us -> 80.1 us (level)
  local copies, waits for them, and re-layouts: 2.54 us -> 3.57 us
  other arithmetic: 6.41 us -> 5.59 us
    ppermute x2, waiting for transfers between devices: 3.1 us -> 6.26 us  [passed_along(): return lax.ppermute(shard, axis, pairs)]
    slice x2 -> x0, other arithmetic: 1.97 us -> none  [planes_of(): return jnp.stack((matrix[0], matrix[1], matrix[0].T, matrix[1].T))]
    ppermute x2, waiting for transfers between devices: 3.37 us -> 2.16 us  [on_device(): lax.ppermute(object_slab, tile_axes, [(s, (s - ahead * row_size) % tile_c...]
    all_to_all x1, waiting for transfers between devices: 6.07 us -> 4.89 us  [on_device(): got = lax.all_to_all(sent, row_axis, 0, 0)]
    squeeze x0 -> x1, other arithmetic: none -> 1.11 us  [planes_of(): stacked = jnp.concatenate((matrix[0], matrix[1]), axis=0)]
    transpose x0 -> x1, other arithmetic: none -> 1.11 us  [planes_of(): stacked_t = jnp.concatenate((matrix[0].T, matrix[1].T), axis=0)]
    another operation x3 -> x6, other arithmetic: 1.24 us -> 0.18 us  [planes_of(): return jnp.stack((stacked, stacked_t))]
  transfers between devices with their start and end apart: 7 -> 7, of which waited for: 5 -> 6; matrix products, arithmetic and copies ran while one was open for 5% -> 5% of each run, Pallas kernels for 0% -> 0%
where the time goes in v8:
time: 80.1 us; the launch traced here: 79.7 us
  starting transfers between devices  30.9 us (39%)
  waiting for transfers between devices  22.4 us (28%)
  blocking collectives  11.5 us (14%)
  other arithmetic  5.59 us (7%)
  Pallas kernels  3.89 us (5%)
  local copies, waits for them, and re-layouts  3.57 us (4%)
  between operations  1.73 us (2%)
    ppermute x2, starting transfers between devices, on_device(): lax.ppermute(object_slab, tile_axes, [(s, (s - ahead * row_size) % tile_c...  17.9 us
    all_to_all x1, blocking collectives, on_device(): incoming = lax.all_to_all(outgoing, row_axis, 0, 0).astype(jnp.float32)  11.5 us
    ppermute x2, waiting for transfers between devices, on_device(): lax.ppermute(spill.astype(jnp.bfloat16), tile_axes, [(s, (s + ahead * row...  9.13 us
    ppermute x2, waiting for transfers between devices, passed_along(): return lax.ppermute(shard, axis, pairs)  6.26 us
    ppermute x2, starting transfers between devices, on_device(): lax.ppermute(spill.astype(jnp.bfloat16), tile_axes, [(s, (s + ahead * row...  5.46 us
    all_to_all x1, starting transfers between devices, on_device(): got = lax.all_to_all(sent, row_axis, 0, 0)  4.96 us
    all_to_all x1, waiting for transfers between devices, on_device(): got = lax.all_to_all(sent, row_axis, 0, 0)  4.89 us
    pallas_call x2, Pallas kernels, run_kernel(): pl.pallas_call(body, out_shape=outs, cost_estimate=pl.CostEstimate(flops=...  3.89 us
  transfers between devices with their start and end apart: 7, of which 6 were waited for; matrix products, arithmetic and copies ran while one was open for 5% of the time, Pallas kernels for 0%

profile of v8, /device:TPU:2, one launch (start us, length us, event | category | flops | bytes accessed | tf_op | source)
XLA Modules:
  0.0 79.7 jit_solution(8253165379442379399)
XLA Ops:
  0.0 13.8 %collective-permute-start = (bf16[2,40,2,256]{3,2,1,0:T(2,128)(2,1)}, bf16[2,40,2,256]{3,2,1,0:T(2,128)(2,1)S(1)}, u32[]{:S(2)}, u32[]{:S(2)}) collective-permute-start(bf16[2,40,2,256]{3,2,1,0:T(2,128)(2,1)} %param.14), channel_id=1, source_target_pairs={{0,252},{1,253},{2,254},{3,255},{4,0},{5,1},{6,2},{7,3},{8,4},{9,5... | collective-permute-start | bytes 245768 | tf_op jit(solution)/shard_map/ppermute | solution.py:274
  13.9 4.1 %collective-permute-start.1 = (bf16[2,40,2,256]{3,2,1,0:T(2,128)(2,1)}, bf16[2,40,2,256]{3,2,1,0:T(2,128)(2,1)S(1)}, u32[]{:S(2)}, u32[]{:S(2)}) collective-permute-start(bf16[2,40,2,256]{3,2,1,0:T(2,128)(2,1)} %param.14), channel_id=1, source_target_pairs={{0,248},{1,249},{2,250},{3,251},{4,252},{5,253},{6,254},{7,255},{8... | collective-permute-start | bytes 245768 | tf_op jit(solution)/shard_map/ppermute | solution.py:274
  17.9 1.0 %fusion.29 = (bf16[1,256,256]{2,1,0:T(8,128)(2,1)S(1)}, bf16[1,256,256]{2,1,0:T(8,128)(2,1)S(1)}) fusion(bf16[2,256,256]{2,1,0:T(8,128)(2,1)} %param.13), kind=kLoop, calls=%fused_computation.74 | loop fusion | bytes 524288 | tf_op jit(solution)/shard_map/slice | solution.py:243
  18.9 0.1 copy.34
  19.0 0.1 copy.35
  19.1 0.0 collective-permute-done
  19.1 2.2 %collective-permute-done.1 = bf16[2,40,2,256]{3,2,1,0:T(2,128)(2,1)S(1)} collective-permute-done((bf16[2,40,2,256]{3,2,1,0:T(2,128)(2,1)}, bf16[2,40,2,256]{3,2,1,0:T(2,128)(2,1)S(1)}, u32[]{:S(2)}, u32[]{:S(2)}) %collective-permute-start.1) | collective-permute-done | bytes 81952 | tf_op jit(solution)/shard_map/ppermute | solution.py:274
  21.3 1.2 %pad_maximum_fusion.2 = (bf16[2,2,40,2,256]{4,3,2,1,0:T(2,128)(2,1)S(1)}, bf16[2,2,40,2,256]{4,3,2,1,0:T(2,128)(2,1)S(1)}) fusion(bf16[1,2,40,2,256]{4,3,2,1,0:T(2,128)(2,1)S(1)} %bitcast.131, bf16[1,2,40,2,256]{4,3,2,1,0:T(2,128)(2,1)} %bitcast.130, bf16[1,2,40,2,256]{4,3,2,1,0:T(2,128)(2,1)S(1)} %bitcast.132), kind=kLoop, calls=%fused_computation.34 | loop fusion | flops 163840 | bytes 573440 | tf_op jit(solution)/shard_map/stack | solution.py:283
  22.6 1.0 %broadcast_select_fusion = bf16[4,2,2,40,2,256]{5,3,4,2,1,0:T(8,128)(2,1)} fusion(pred[4]{0:T(512)(128)(4,1)S(1)} %iota_compare_fusion, bf16[2,2,40,2,256]{4,2,3,1,0:T(8,128)(2,1)S(1)} %copy.26, bf16[2,2,40,2,256]{4,2,3,1,0:T(8,128)(2,1)S(1)} %copy.25), kind=kLoop, calls=%fused_computation.14 | loop fusion | flops 327680 | bytes 983044 | tf_op jit(solution)/shard_map/jit(_where)/select_n | solution.py:282
  23.6 0.0 copy-start
  23.6 5.0 %all-to-all-start = ((bf16[4,2,2,40,2,256]{5,3,4,2,1,0:T(8,128)(2,1)}), bf16[4,2,2,40,2,256]{5,3,4,2,1,0:T(8,128)(2,1)S(1)}, u32[]{:S(2)}, u32[]{:S(2)}) async-start(bf16[4,2,2,40,2,256]{5,3,4,2,1,0:T(8,128)(2,1)} %broadcast_select_fusion), calls=%async_computation | async-start | bytes 1310720 | tf_op jit(solution)/shard_map/all_to_all | solution.py:285
  29.2 0.1 copy.29
  29.3 0.0 copy-done
  29.4 1.1 %fusion.10 = (bf16[256,256]{0,1:T(8,128)(2,1)S(1)}, bf16[256,256]{0,1:T(8,128)(2,1)S(1)}) fusion(), kind=kLoop, calls=%fused_computation.38 | loop fusion | flops 1245184 | bytes 262144 | tf_op jit(solution)/shard_map/squeeze | solution.py:243
  30.5 1.1 %fusion.9 = (bf16[256,256]{1,0:T(8,128)(2,1)S(1)}, bf16[256,256]{1,0:T(8,128)(2,1)S(1)}) fusion(), kind=kLoop, calls=%fused_computation.37 | loop fusion | flops 1245184 | bytes 262144 | tf_op jit(solution)/shard_map/transpose | solution.py:244
  31.7 0.1 pad_maximum_fusion
  31.7 4.9 %all-to-all-done = bf16[4,2,2,40,2,256]{5,3,4,2,1,0:T(8,128)(2,1)S(1)} async-done(((bf16[4,2,2,40,2,256]{5,3,4,2,1,0:T(8,128)(2,1)}), bf16[4,2,2,40,2,256]{5,3,4,2,1,0:T(8,128)(2,1)S(1)}, u32[]{:S(2)}, u32[]{:S(2)}) %all-to-all-start) | async-done | bytes 655392 | tf_op jit(solution)/shard_map/all_to_all | solution.py:285
  36.6 0.2 fusion.2
  37.0 0.1 dynamic-slice_bitcast_fusion
  37.1 1.6 %conditional.3 = ((bf16[2,256,256]{2,1,0:T(8,128)(2,1)S(1)}, bf16[2,2,256,256]{3,2,1,0:T(8,128)(2,1)S(1)})) conditional(s32[]{:T(128)} %convert_element_type.51, bf16[2,256,256]{2,1,0:T(8,128)(2,1)S(1)} %bitcast.127, (bf16[2,256,256]{2,1,0:T(8,128)(2,1)S(1)}, bf16[2,2,256,256]{3,2,1,0:T(8,128)(2,1)S(1)}, bf16[2,512,256]{2,1,0:T(8,128)(2,1)S(1)}) %tuple.52), branch_computations={%region_0.1_spmd, %region_1.2_spmd} | conditional | flops 536870912 | bytes 2097160 | solution.py:330
  37.1 1.6 %branch_1_fun.3 = (bf16[2,256,256]{2,1,0:T(8,128)(2,1)S(1)}, bf16[2,2,256,256]{3,2,1,0:T(8,128)(2,1)S(1)}) custom-call(bf16[2,256,256]{2,1,0:T(8,128)(2,1)S(1)} %get-tuple-element.36.field_ref, bf16[2,2,256,256]{3,2,1,0:T(8,128)(2,1)S(1)} %get-tuple-element.37.patch_ref, bf16[2,512,256]{2,1,0:T(8,128)(2,1)S(1)} %get-tuple-element.38.mat_ref), custom_call_target="tpu_custom_call" | custom-call | flops 536870912 | bytes 2097152 | tf_op jit(solution)/shard_map/cond/branch_1_fun/pallas_call | solution.py:252
  38.7 1.3 %collective-permute-start.2 = (bf16[2,256,256]{2,1,0:T(8,128)(2,1)S(1)}, bf16[2,256,256]{2,1,0:T(8,128)(2,1)S(1)}, u32[]{:S(2)}, u32[]{:S(2)}) collective-permute-start(bf16[2,256,256]{2,1,0:T(8,128)(2,1)S(1)} %get-tuple-element.55), channel_id=1, source_target_pairs={{0,256},{1,257},{2,258},{3,259},{4,260},{5,261},{6,262},{7,263},{8... | collective-permute-start | bytes 786440 | tf_op jit(solution)/shard_map/ppermute | solution.py:19
  40.0 0.0 copy-start.1
  40.1 0.1 copy.30
  40.2 0.1 pad_maximum_fusion.1
  40.3 0.9 %collective-permute-done.2 = bf16[2,256,256]{2,1,0:T(8,128)(2,1)S(1)} collective-permute-done((bf16[2,256,256]{2,1,0:T(8,128)(2,1)S(1)}, bf16[2,256,256]{2,1,0:T(8,128)(2,1)S(1)}, u32[]{:S(2)}, u32[]{:S(2)}) %collective-permute-start.2) | collective-permute-done | bytes 262176 | tf_op jit(solution)/shard_map/ppermute | solution.py:19
  41.2 0.0 copy-done.1
  41.2 0.8 conditional.4
  41.2 0.7 copy.50
  41.9 0.1 broadcast_in_dim.47
  42.0 1.3 %collective-permute-start.3 = (bf16[2,256,256]{2,1,0:T(8,128)(2,1)}, bf16[2,256,256]{2,1,0:T(8,128)(2,1)S(1)}, u32[]{:S(2)}, u32[]{:S(2)}) collective-permute-start(bf16[2,256,256]{2,1,0:T(8,128)(2,1)} %get-tuple-element.57), channel_id=1, source_target_pairs={{256,0},{257,1},{258,2},{259,3},{260,4},{261,5},{262,6},{263,7},{2... | collective-permute-start | bytes 786440 | tf_op jit(solution)/shard_map/ppermute | solution.py:19
  43.9 5.4 %collective-permute-done.3 = bf16[2,256,256]{2,1,0:T(8,128)(2,1)S(1)} collective-permute-done((bf16[2,256,256]{2,1,0:T(8,128)(2,1)}, bf16[2,256,256]{2,1,0:T(8,128)(2,1)S(1)}, u32[]{:S(2)}, u32[]{:S(2)}) %collective-permute-start.3) | collective-permute-done | bytes 262176 | tf_op jit(solution)/shard_map/ppermute | solution.py:19
  49.3 2.3 %conditional.5 = (f32[2,2,256,256]{3,2,1,0:T(8,128)S(1)}) conditional(s32[]{:T(128)} %convert_element_type.51, f32[2,2,256,256]{3,2,1,0:T(8,128)S(1)} %get-tuple-element.56, (bf16[2,256,256]{2,1,0:T(8,128)(2,1)S(1)}, bf16[2,2,256,256]{3,2,1,0:T(8,128)(2,1)S(1)}, bf16[2,2,256,256]{3,2,1,0:T(8,128)(2,1)S(1)}, bf16[2,512,256]{2,1,0:T(8,128)(2,1)S(1)}) %tuple.32), branch_computations={%region_4.5_spmd, %region_5.6_spmd} | conditional | flops 536870912 | bytes 3145736 | solution.py:347
  49.3 2.3 %branch_1_fun.5 = (bf16[2,256,256]{2,1,0:T(8,128)(2,1)}, f32[2,2,256,256]{3,2,1,0:T(8,128)S(1)}) custom-call(bf16[2,256,256]{2,1,0:T(8,128)(2,1)S(1)} %get-tuple-element.46.back_ref, bf16[2,2,256,256]{3,2,1,0:T(8,128)(2,1)S(1)} %get-tuple-element.47.patch_ref, bf16[2,2,256,256]{3,2,1,0:T(8,128)(2,1)S(1)} %get-tuple-element.48.incident_ref, ...), custom_call_target="tpu_custom_call" | custom-call | flops 536870912 | bytes 3145728 | tf_op jit(solution)/shard_map/cond/branch_1_fun/pallas_call | solution.py:252
  51.7 0.1 multiply_bitcast_fusion
  51.8 0.2 fusion
  52.1 0.3 fusion.1
  52.4 11.5 %all_to_all.10 = bf16[4,2,40,2,2,256]{5,2,4,3,1,0:T(8,128)(2,1)S(1)} all-to-all(bf16[4,2,40,2,2,256]{5,2,4,3,1,0:T(8,128)(2,1)S(1)} %copy.31), channel_id=1, replica_groups=mesh['section'=2,'lines'=64,'x'=4] {'x'}, dimensions={0} | all-to-all | bytes 1310720 | tf_op jit(solution)/shard_map/all_to_all | solution.py:363
  63.9 0.2 convert_element_type.55
  64.1 0.2 select_reduce_fusion.1
  64.3 3.5 %collective-permute-start.4 = (bf16[40,2,2,256]{3,0,2,1:T(8,128)(2,1)S(1)}, bf16[40,2,2,256]{3,0,2,1:T(8,128)(2,1)S(1)}, u32[]{:S(2)}, u32[]{:S(2)}) collective-permute-start(bf16[40,2,2,256]{3,0,2,1:T(8,128)(2,1)S(1)} %get-tuple-element.72), channel_id=1, source_target_pairs={{0,4},{1,5},{2,6},{3,7},{4,8},{5,9},{6,10},{7,11},{8,12},{9,13},{1... | collective-permute-start | bytes 245768 | tf_op jit(solution)/shard_map/ppermute | solution.py:373
  67.9 1.9 %collective-permute-start.5 = (bf16[40,2,2,256]{3,0,2,1:T(8,128)(2,1)S(1)}, bf16[40,2,2,256]{3,0,2,1:T(8,128)(2,1)S(1)}, u32[]{:S(2)}, u32[]{:S(2)}) collective-permute-start(bf16[40,2,2,256]{3,0,2,1:T(8,128)(2,1)S(1)} %get-tuple-element.73), channel_id=1, source_target_pairs={{0,8},{1,9},{2,10},{3,11},{4,12},{5,13},{6,14},{7,15},{8,16},{9,17... | collective-permute-start | bytes 245768 | tf_op jit(solution)/shard_map/ppermute | solution.py:373
  69.8 5.8 %collective-permute-done.4 = bf16[40,2,2,256]{3,0,2,1:T(8,128)(2,1)S(1)} collective-permute-done((bf16[40,2,2,256]{3,0,2,1:T(8,128)(2,1)S(1)}, bf16[40,2,2,256]{3,0,2,1:T(8,128)(2,1)S(1)}, u32[]{:S(2)}, u32[]{:S(2)}) %collective-permute-start.4) | collective-permute-done | bytes 81952 | tf_op jit(solution)/shard_map/ppermute | solution.py:373
  75.5 3.4 %collective-permute-done.5 = bf16[40,2,2,256]{3,0,2,1:T(8,128)(2,1)S(1)} collective-permute-done((bf16[40,2,2,256]{3,0,2,1:T(8,128)(2,1)S(1)}, bf16[40,2,2,256]{3,0,2,1:T(8,128)(2,1)S(1)}, u32[]{:S(2)}, u32[]{:S(2)}) %collective-permute-start.5) | collective-permute-done | bytes 81952 | tf_op jit(solution)/shard_map/ppermute | solution.py:373
  79.0 0.8 copy.33
  (26 shorter events, 0.4 us)
Async XLA Ops:
  0.0 19.1 %collective-permute-start = (bf16[2,40,2,256]{3,2,1,0:T(2,128)(2,1)}, bf16[2,40,2,256]{3,2,1,0:T(2,128)(2,1)S(1)}, u32[]{:S(2)}, u32[]{:S(2)}) collective-permute-start(bf16[2,40,2,256]{3,2,1,0:T(2,128)(2,1)} %param.14), channel_id=1, source_target_pairs={{0,252},{1,253},{2,254},{3,255},{4,0},{5,1},{6,2},{7,3},{8,4},{9,5... | collective-permute-start | bytes 245768 | tf_op jit(solution)/shard_map/ppermute | solution.py:274
  13.9 7.5 %collective-permute-start.1 = (bf16[2,40,2,256]{3,2,1,0:T(2,128)(2,1)}, bf16[2,40,2,256]{3,2,1,0:T(2,128)(2,1)S(1)}, u32[]{:S(2)}, u32[]{:S(2)}) collective-permute-start(bf16[2,40,2,256]{3,2,1,0:T(2,128)(2,1)} %param.14), channel_id=1, source_target_pairs={{0,248},{1,249},{2,250},{3,251},{4,252},{5,253},{6,254},{7,255},{8... | collective-permute-start | bytes 245768 | tf_op jit(solution)/shard_map/ppermute | solution.py:274
  23.6 5.8 %copy-start = (bf16[256,2,256]{2,1,0:T(2,128)(2,1)S(1)}, bf16[256,2,256]{2,1,0:T(2,128)(2,1)}, u32[]{:S(2)}) copy-start(bf16[256,2,256]{2,1,0:T(2,128)(2,1)} %param.12) | copy-start | bytes 786436
  23.6 13.0 %all-to-all-start = ((bf16[4,2,2,40,2,256]{5,3,4,2,1,0:T(8,128)(2,1)}), bf16[4,2,2,40,2,256]{5,3,4,2,1,0:T(8,128)(2,1)S(1)}, u32[]{:S(2)}, u32[]{:S(2)}) async-start(bf16[4,2,2,40,2,256]{5,3,4,2,1,0:T(8,128)(2,1)} %broadcast_select_fusion), calls=%async_computation | async-start | bytes 1310720 | tf_op jit(solution)/shard_map/all_to_all | solution.py:285
  38.7 2.4 %collective-permute-start.2 = (bf16[2,256,256]{2,1,0:T(8,128)(2,1)S(1)}, bf16[2,256,256]{2,1,0:T(8,128)(2,1)S(1)}, u32[]{:S(2)}, u32[]{:S(2)}) collective-permute-start(bf16[2,256,256]{2,1,0:T(8,128)(2,1)S(1)} %get-tuple-element.55), channel_id=1, source_target_pairs={{0,256},{1,257},{2,258},{3,259},{4,260},{5,261},{6,262},{7,263},{8... | collective-permute-start | bytes 786440 | tf_op jit(solution)/shard_map/ppermute | solution.py:19
  40.0 1.1 %copy-start.1 = (bf16[1,256,256]{2,1,0:T(8,128)(2,1)S(1)}, bf16[1,256,256]{2,1,0:T(8,128)(2,1)}, u32[]{:S(2)}) copy-start(bf16[1,256,256]{2,1,0:T(8,128)(2,1)} %param.17) | copy-start | bytes 393220
  42.0 7.4 %collective-permute-start.3 = (bf16[2,256,256]{2,1,0:T(8,128)(2,1)}, bf16[2,256,256]{2,1,0:T(8,128)(2,1)S(1)}, u32[]{:S(2)}, u32[]{:S(2)}) collective-permute-start(bf16[2,256,256]{2,1,0:T(8,128)(2,1)} %get-tuple-element.57), channel_id=1, source_target_pairs={{256,0},{257,1},{258,2},{259,3},{260,4},{261,5},{262,6},{263,7},{2... | collective-permute-start | bytes 786440 | tf_op jit(solution)/shard_map/ppermute | solution.py:19
  64.3 11.2 %collective-permute-start.4 = (bf16[40,2,2,256]{3,0,2,1:T(8,128)(2,1)S(1)}, bf16[40,2,2,256]{3,0,2,1:T(8,128)(2,1)S(1)}, u32[]{:S(2)}, u32[]{:S(2)}) collective-permute-start(bf16[40,2,2,256]{3,0,2,1:T(8,128)(2,1)S(1)} %get-tuple-element.72), channel_id=1, source_target_pairs={{0,4},{1,5},{2,6},{3,7},{4,8},{5,9},{6,10},{7,11},{8,12},{9,13},{1... | collective-permute-start | bytes 245768 | tf_op jit(solution)/shard_map/ppermute | solution.py:373
  67.9 11.1 %collective-permute-start.5 = (bf16[40,2,2,256]{3,0,2,1:T(8,128)(2,1)S(1)}, bf16[40,2,2,256]{3,0,2,1:T(8,128)(2,1)S(1)}, u32[]{:S(2)}, u32[]{:S(2)}) collective-permute-start(bf16[40,2,2,256]{3,0,2,1:T(8,128)(2,1)S(1)} %get-tuple-element.73), channel_id=1, source_target_pairs={{0,8},{1,9},{2,10},{3,11},{4,12},{5,13},{6,14},{7,15},{8,16},{9,17... | collective-permute-start | bytes 245768 | tf_op jit(solution)/shard_map/ppermute | solution.py:373

commit v9 on v7

--- a/solution.py
+++ b/solution.py
@@ -252,28 +252,26 @@
     is_last = section_now == sections - 1
     dft_table = dft_matrix(width)
     chunk_ids = jnp.arange(row_size, dtype=jnp.int32)
-    later = [object_slab] + [
+    slab = jnp.transpose(object_slab, (0, 2, 1, 3))
+    later = [slab] + [
         lax.ppermute(
-            object_slab,
+            slab,
             tile_axes,
             [(s, (s - ahead * row_size) % tile_count) for s in range(tile_count)],
         )
         for ahead in (1, 2)
     ]
     own_row = (chunk_ids <= place)[:, None, None, None, None, None]
-    sent = jnp.where(
-        own_row, jnp.stack(later[:2])[None], jnp.stack(later[1:])[None]
-    )
+    sent = jnp.where(own_row, jnp.stack(later[:2])[None], jnp.stack(later[1:])[None])
     got = lax.all_to_all(sent, row_axis, 0, 0)
     got = lax.dynamic_slice_in_dim(jnp.concatenate((got, got), axis=0), place, row_size, 0)
     window = jnp.concatenate(
-        [got[at % row_size, at // row_size] for at in range(2 * row_size)], axis=1
+        [got[at % row_size, at // row_size] for at in range(2 * row_size)], axis=2
     )
     relative = offsets - tile_now * local_rows
-    patches = jax.vmap(lambda offset: lax.dynamic_slice_in_dim(window, offset, width, 1))(relative)
+    planes = lax.dynamic_slice_in_dim(window, relative[0], width, 2)
     live_slots = jnp.arange(slot_count, dtype=jnp.int32) < counts[0]
 
-    planes = jnp.transpose(patches[0], (0, 2, 1, 3))
     kernel_planes = planes_of(kernel)
     dft_planes = planes_of(dft_matrix(width))
     field_shape = jax.ShapeDtypeStruct((2, width, width), jnp.bfloat16)
@@ -333,13 +331,13 @@
             adjoints,
             gradients,
         )
-    gradients = jnp.transpose(gradients, (0, 2, 1, 3))[None]
-    gradients = gradients * live_slots.astype(jnp.float32)[:, None, None, None, None]
-    nearby = accumulate(gradients, offsets - tile_now * local_rows, 2 * row_size * local_rows)
-    tiles = jnp.stack(
-        [nearby[at * local_rows : (at + 1) * local_rows] for at in range(2 * row_size)], axis=0
-    ).astype(jnp.bfloat16)
-    tiles = tiles.reshape((2, row_size) + tiles.shape[1:]).swapaxes(0, 1)
+    gradients = gradients * live_slots[0].astype(jnp.float32)
+    span = 2 * row_size * local_rows
+    margin = span - width
+    padded = jnp.pad(gradients, ((0, 0), (0, 0), (margin, margin), (0, 0)))
+    nearby = lax.dynamic_slice_in_dim(padded, margin - relative[0], span, 2)
+    tiles = nearby.reshape(nearby.shape[:2] + (2, row_size, local_rows, width))
+    tiles = jnp.transpose(tiles, (3, 2, 0, 1, 4, 5)).astype(jnp.bfloat16)
     tiles = jnp.concatenate((tiles, tiles), axis=0)
     outgoing = lax.dynamic_slice_in_dim(tiles, row_size - place, row_size, 0)
     incoming = lax.all_to_all(outgoing, row_axis, 0, 0).astype(jnp.float32)
@@ -357,7 +355,7 @@
             tile_axes,
             [(s, (s + ahead * row_size) % tile_count) for s in range(tile_count)],
         ).astype(jnp.float32)
-    return jnp.transpose(own_rows, (1, 0, 2, 3))
+    return jnp.transpose(own_rows, (0, 2, 1, 3))
 
 
 def row_length(devices):

time: 79.5 us -> 79.4 us (level)
  no operation moved by 1% of the time
where the time goes in v9:
time: 79.4 us; the launch traced here: 79 us
  starting transfers between devices  31 us (39%)
  waiting for transfers between devices  21.7 us (27%)
  blocking collectives  12 us (15%)
  other arithmetic  6.4 us (8%)
  Pallas kernels  3.72 us (5%)
  local copies, waits for them, and re-layouts  2.49 us (3%)
  between operations  1.66 us (2%)
    ppermute x2, starting transfers between devices, on_device(): lax.ppermute(slab, tile_axes, [(s, (s - ahead * row_size) % tile_count) f...  17.9 us
    all_to_all x1, blocking collectives, on_device(): incoming = lax.all_to_all(outgoing, row_axis, 0, 0).astype(jnp.float32)  12 us
    ppermute x2, waiting for transfers between devices, on_device(): lax.ppermute(spill.astype(jnp.bfloat16), tile_axes, [(s, (s + ahead * row...  9.14 us
    all_to_all x1, waiting for transfers between devices, on_device(): got = lax.all_to_all(sent, row_axis, 0, 0)  6.07 us
    ppermute x2, starting transfers between devices, on_device(): lax.ppermute(spill.astype(jnp.bfloat16), tile_axes, [(s, (s + ahead * row...  5.46 us
    all_to_all x1, starting transfers between devices, on_device(): got = lax.all_to_all(sent, row_axis, 0, 0)  4.96 us
    pallas_call x2, Pallas kernels, run_kernel(): pl.pallas_call(body, out_shape=outs, cost_estimate=pl.CostEstimate(flops=...  3.72 us
    ppermute x2, waiting for transfers between devices, on_device(): lax.ppermute(slab, tile_axes, [(s, (s - ahead * row_size) % tile_count) f...  3.37 us
  transfers between devices with their start and end apart: 7, of which 5 were waited for; matrix products, arithmetic and copies ran while one was open for 5% of the time, Pallas kernels for 0%

profile of v9, /device:TPU:2, one launch (start us, length us, event | category | flops | bytes accessed | tf_op | source)
XLA Modules:
  0.0 79.0 jit_solution(15580900731306782312)
XLA Ops:
  0.0 13.8 %collective-permute-start = (bf16[2,2,40,256]{3,1,2,0:T(2,128)(2,1)}, bf16[2,2,40,256]{3,1,2,0:T(2,128)(2,1)S(1)}, u32[]{:S(2)}, u32[]{:S(2)}) collective-permute-start(bf16[2,2,40,256]{3,1,2,0:T(2,128)(2,1)} %bitcast.90), channel_id=1, source_target_pairs={{0,252},{1,253},{2,254},{3,255},{4,0},{5,1},{6,2},{7,3},{8,4},{9,5... | collective-permute-start | bytes 245768 | tf_op jit(solution)/shard_map/ppermute | solution.py:257
  13.9 4.1 %collective-permute-start.1 = (bf16[2,2,40,256]{3,1,2,0:T(2,128)(2,1)}, bf16[2,2,40,256]{3,1,2,0:T(2,128)(2,1)S(1)}, u32[]{:S(2)}, u32[]{:S(2)}) collective-permute-start(bf16[2,2,40,256]{3,1,2,0:T(2,128)(2,1)} %bitcast.91), channel_id=1, source_target_pairs={{0,248},{1,249},{2,250},{3,251},{4,252},{5,253},{6,254},{7,255},{8... | collective-permute-start | bytes 245768 | tf_op jit(solution)/shard_map/ppermute | solution.py:257
  17.9 0.0 collective-permute-done
  17.9 3.4 %collective-permute-done.1 = bf16[2,2,40,256]{3,1,2,0:T(2,128)(2,1)S(1)} collective-permute-done((bf16[2,2,40,256]{3,1,2,0:T(2,128)(2,1)}, bf16[2,2,40,256]{3,1,2,0:T(2,128)(2,1)S(1)}, u32[]{:S(2)}, u32[]{:S(2)}) %collective-permute-start.1) | collective-permute-done | bytes 81952 | tf_op jit(solution)/shard_map/ppermute | solution.py:257
  21.3 1.2 %pad_maximum_fusion.2 = (bf16[2,2,2,40,256]{4,2,3,1,0:T(2,128)(2,1)S(1)}, bf16[2,2,2,40,256]{4,2,3,1,0:T(2,128)(2,1)S(1)}) fusion(bf16[1,2,2,40,256]{4,2,3,1,0:T(2,128)(2,1)S(1)} %bitcast.93, bf16[1,2,2,40,256]{4,2,3,1,0:T(2,128)(2,1)} %bitcast.92, bf16[1,2,2,40,256]{4,2,3,1,0:T(2,128)(2,1)S(1)} %bitcast.94), kind=kLoop, calls=%fused_computation.29 | loop fusion | flops 163840 | bytes 573440 | tf_op jit(solution)/shard_map/stack | solution.py:265
  22.6 0.0 copy-start
  22.6 1.0 %broadcast_select_fusion = bf16[4,2,2,2,40,256]{5,4,3,2,1,0:T(8,128)(2,1)} fusion(pred[4]{0:T(512)(128)(4,1)S(1)} %iota_compare_fusion, bf16[2,2,2,40,256]{4,3,2,1,0:T(8,128)(2,1)S(1)} %copy.30, bf16[2,2,2,40,256]{4,3,2,1,0:T(8,128)(2,1)S(1)} %copy.29), kind=kLoop, calls=%fused_computation.13 | loop fusion | flops 327680 | bytes 983044 | tf_op jit(solution)/shard_map/jit(_where)/select_n | solution.py:265
  23.6 0.0 copy-start.1
  23.6 5.0 %all-to-all-start = ((bf16[4,2,2,2,40,256]{5,4,3,2,1,0:T(8,128)(2,1)}), bf16[4,2,2,2,40,256]{5,4,3,2,1,0:T(8,128)(2,1)S(1)}, u32[]{:S(2)}, u32[]{:S(2)}) async-start(bf16[4,2,2,2,40,256]{5,4,3,2,1,0:T(8,128)(2,1)} %broadcast_select_fusion), calls=%async_computation | async-start | bytes 1310720 | tf_op jit(solution)/shard_map/all_to_all | solution.py:266
  29.2 0.0 copy-done
  29.2 0.1 copy.44
  29.3 0.1 copy.45
  29.4 0.0 copy-done.1
  29.5 1.0 %multiply_convert_fusion.1 = bf16[1,256,256]{1,2,0:T(8,128)(2,1)S(1)} fusion(), kind=kLoop, calls=%fused_computation.25 | loop fusion | flops 1048576 | bytes 131072 | tf_op jit(solution)/shard_map/slice | solution.py:227
  30.5 0.1 pad_maximum_fusion
  30.6 6.1 %all-to-all-done = bf16[4,2,2,2,40,256]{5,4,3,2,1,0:T(8,128)(2,1)S(1)} async-done(((bf16[4,2,2,2,40,256]{5,4,3,2,1,0:T(8,128)(2,1)}), bf16[4,2,2,2,40,256]{5,4,3,2,1,0:T(8,128)(2,1)S(1)}, u32[]{:S(2)}, u32[]{:S(2)}) %all-to-all-start) | async-done | bytes 655392 | tf_op jit(solution)/shard_map/all_to_all | solution.py:266
  36.6 0.2 fusion.2
  37.0 0.1 constant_dynamic-slice_fusion
  37.1 1.9 %conditional.3 = ((bf16[2,256,256]{2,1,0:T(8,128)(2,1)}, bf16[2,2,256,256]{3,2,1,0:T(8,128)(2,1)S(1)})) conditional(s32[]{:T(128)} %convert_element_type.60, bf16[2,256,256]{2,1,0:T(8,128)(2,1)S(1)} %bitcast.86, (bf16[2,256,256]{2,1,0:T(8,128)(2,1)S(1)}, bf16[2,2,256,256]{3,2,1,0:T(8,128)(2,1)S(1)}, bf16[4,256,256]{2,1,0:T(8,128)(2,1)S(1)}) %tuple.46), branch_computations={%region_0.1_spmd, %region_1.2_spmd} | conditional | flops 536870912 | bytes 2097160 | solution.py:310
  37.2 1.8 %branch_1_fun.3 = (bf16[2,256,256]{2,1,0:T(8,128)(2,1)}, bf16[2,2,256,256]{3,2,1,0:T(8,128)(2,1)S(1)}) custom-call(bf16[2,256,256]{2,1,0:T(8,128)(2,1)S(1)} %get-tuple-element.36.field_ref, bf16[2,2,256,256]{3,2,1,0:T(8,128)(2,1)S(1)} %get-tuple-element.37.patch_ref, bf16[4,256,256]{2,1,0:T(8,128)(2,1)S(1)} %get-tuple-element.38.mat_ref), custom_call_target="tpu_custom_call" | custom-call | flops 536870912 | bytes 2097152 | tf_op jit(solution)/shard_map/cond/branch_1_fun/pallas_call | solution.py:234
  39.0 0.0 copy-start.2
  39.0 1.4 %collective-permute-start.2 = (bf16[2,256,256]{2,1,0:T(8,128)(2,1)}, bf16[2,256,256]{2,1,0:T(8,128)(2,1)S(1)}, u32[]{:S(2)}, u32[]{:S(2)}) collective-permute-start(bf16[2,256,256]{2,1,0:T(8,128)(2,1)} %get-tuple-element.55), channel_id=1, source_target_pairs={{0,256},{1,257},{2,258},{3,259},{4,260},{5,261},{6,262},{7,263},{8... | collective-permute-start | bytes 786440 | tf_op jit(solution)/shard_map/ppermute | solution.py:19
  40.4 1.0 %multiply_convert_fusion = bf16[1,256,256]{1,2,0:T(8,128)(2,1)S(1)} fusion(), kind=kLoop, calls=%fused_computation.24 | loop fusion | flops 1114112 | bytes 131072 | tf_op jit(solution)/shard_map/slice | solution.py:227
  41.4 0.1 copy.33
  41.5 0.1 copy.34
  41.6 1.1 %fusion.17 = (bf16[1,256,256]{2,1,0:T(8,128)(2,1)S(1)}, bf16[1,256,256]{2,1,0:T(8,128)(2,1)S(1)}) fusion(), kind=kLoop, calls=%fused_computation.48 | loop fusion | flops 1245184 | bytes 262144 | tf_op jit(solution)/shard_map/stack | solution.py:227
  42.8 0.1 pad_maximum_fusion.1
  42.8 0.0 collective-permute-done.2
  42.8 0.0 copy-done.2
  42.9 0.8 %conditional.4 = (bf16[2,256,256]{2,1,0:T(8,128)(2,1)}, f32[2,2,256,256]{3,2,1,0:T(8,128)S(1)}) conditional(s32[]{:T(128)} %convert_element_type.61, bf16[2,256,256]{2,1,0:T(8,128)(2,1)S(1)} %collective-permute-done.2, (bf16[1,256,256]{2,1,0:T(8,128)(2,1)S(1)}, bf16[2,256,256]{2,1,0:T(8,128)(2,1)S(1)}, bf16[2,2,256,256]{3,2,1,0:T(8,128)(2,1)S(1)}, ...), branch_computations={%region_2.3_spmd, %region_3.4_spmd} | conditional | flops 1610612736 | bytes 3801104 | solution.py:318
  42.9 0.7 copy.60
  43.6 0.1 broadcast_in_dim.56
  43.7 1.3 %collective-permute-start.3 = (bf16[2,256,256]{2,1,0:T(8,128)(2,1)}, bf16[2,256,256]{2,1,0:T(8,128)(2,1)S(1)}, u32[]{:S(2)}, u32[]{:S(2)}) collective-permute-start(bf16[2,256,256]{2,1,0:T(8,128)(2,1)} %get-tuple-element.57), channel_id=1, source_target_pairs={{256,0},{257,1},{258,2},{259,3},{260,4},{261,5},{262,6},{263,7},{2... | collective-permute-start | bytes 786440 | tf_op jit(solution)/shard_map/ppermute | solution.py:19
  45.6 3.1 %collective-permute-done.3 = bf16[2,256,256]{2,1,0:T(8,128)(2,1)S(1)} collective-permute-done((bf16[2,256,256]{2,1,0:T(8,128)(2,1)}, bf16[2,256,256]{2,1,0:T(8,128)(2,1)S(1)}, u32[]{:S(2)}, u32[]{:S(2)}) %collective-permute-start.3) | collective-permute-done | bytes 262176 | tf_op jit(solution)/shard_map/ppermute | solution.py:19
  48.7 1.9 %conditional.5 = (f32[2,2,256,256]{3,2,1,0:T(8,128)S(1)}) conditional(s32[]{:T(128)} %convert_element_type.60, f32[2,2,256,256]{3,2,1,0:T(8,128)S(1)} %get-tuple-element.56, (bf16[2,256,256]{2,1,0:T(8,128)(2,1)S(1)}, bf16[2,2,256,256]{3,2,1,0:T(8,128)(2,1)S(1)}, bf16[2,2,256,256]{3,2,1,0:T(8,128)(2,1)S(1)}, bf16[4,256,256]{2,1,0:T(8,128)(2,1)S(1)}) %tuple.32), branch_computations={%region_4.5_spmd, %region_5.6_spmd} | conditional | flops 536870912 | bytes 3145736 | solution.py:327
  48.7 1.9 %branch_1_fun.5 = (bf16[2,256,256]{2,1,0:T(8,128)(2,1)}, f32[2,2,256,256]{3,2,1,0:T(8,128)S(1)}) custom-call(bf16[2,256,256]{2,1,0:T(8,128)(2,1)S(1)} %get-tuple-element.46.back_ref, bf16[2,2,256,256]{3,2,1,0:T(8,128)(2,1)S(1)} %get-tuple-element.47.patch_ref, bf16[2,2,256,256]{3,2,1,0:T(8,128)(2,1)S(1)} %get-tuple-element.48.incident_ref, ...), custom_call_target="tpu_custom_call" | custom-call | flops 536870912 | bytes 3145728 | tf_op jit(solution)/shard_map/cond/branch_1_fun/pallas_call | solution.py:234
  50.6 0.1 broadcast_multiply_fusion
  50.7 0.2 fusion
  50.9 0.3 fusion.1
  51.2 12.0 %all_to_all.10 = bf16[4,2,2,2,40,256]{5,4,1,3,2,0:T(8,128)(2,1)S(1)} all-to-all(bf16[4,2,2,2,40,256]{5,4,1,3,2,0:T(8,128)(2,1)S(1)} %copy.35), channel_id=1, replica_groups=mesh['section'=2,'lines'=64,'x'=4] {'x'}, dimensions={0} | all-to-all | bytes 1310720 | tf_op jit(solution)/shard_map/all_to_all | solution.py:343
  63.2 0.2 convert_element_type.68
  63.4 0.2 select_reduce_fusion.1
  63.6 3.5 %collective-permute-start.4 = (bf16[2,2,40,256]{3,2,1,0:T(8,128)(2,1)S(1)}, bf16[2,2,40,256]{3,2,1,0:T(8,128)(2,1)S(1)}, u32[]{:S(2)}, u32[]{:S(2)}) collective-permute-start(bf16[2,2,40,256]{3,2,1,0:T(8,128)(2,1)S(1)} %get-tuple-element.61), channel_id=1, source_target_pairs={{0,4},{1,5},{2,6},{3,7},{4,8},{5,9},{6,10},{7,11},{8,12},{9,13},{1... | collective-permute-start | bytes 245768 | tf_op jit(solution)/shard_map/ppermute | solution.py:353
  67.1 1.9 %collective-permute-start.5 = (bf16[2,2,40,256]{3,2,1,0:T(8,128)(2,1)S(1)}, bf16[2,2,40,256]{3,2,1,0:T(8,128)(2,1)S(1)}, u32[]{:S(2)}, u32[]{:S(2)}) collective-permute-start(bf16[2,2,40,256]{3,2,1,0:T(8,128)(2,1)S(1)} %get-tuple-element.62), channel_id=1, source_target_pairs={{0,8},{1,9},{2,10},{3,11},{4,12},{5,13},{6,14},{7,15},{8,16},{9,17... | collective-permute-start | bytes 245768 | tf_op jit(solution)/shard_map/ppermute | solution.py:353
  69.1 6.3 %collective-permute-done.4 = bf16[2,2,40,256]{3,2,1,0:T(8,128)(2,1)S(1)} collective-permute-done((bf16[2,2,40,256]{3,2,1,0:T(8,128)(2,1)S(1)}, bf16[2,2,40,256]{3,2,1,0:T(8,128)(2,1)S(1)}, u32[]{:S(2)}, u32[]{:S(2)}) %collective-permute-start.4) | collective-permute-done | bytes 81952 | tf_op jit(solution)/shard_map/ppermute | solution.py:353
  75.4 2.8 %collective-permute-done.5 = bf16[2,2,40,256]{3,2,1,0:T(8,128)(2,1)S(1)} collective-permute-done((bf16[2,2,40,256]{3,2,1,0:T(8,128)(2,1)S(1)}, bf16[2,2,40,256]{3,2,1,0:T(8,128)(2,1)S(1)}, u32[]{:S(2)}, u32[]{:S(2)}) %collective-permute-start.5) | collective-permute-done | bytes 81952 | tf_op jit(solution)/shard_map/ppermute | solution.py:353
  78.2 0.8 copy.40
  (15 shorter events, 0.2 us)
Async XLA Ops:
  0.0 17.9 %collective-permute-start = (bf16[2,2,40,256]{3,1,2,0:T(2,128)(2,1)}, bf16[2,2,40,256]{3,1,2,0:T(2,128)(2,1)S(1)}, u32[]{:S(2)}, u32[]{:S(2)}) collective-permute-start(bf16[2,2,40,256]{3,1,2,0:T(2,128)(2,1)} %bitcast.90), channel_id=1, source_target_pairs={{0,252},{1,253},{2,254},{3,255},{4,0},{5,1},{6,2},{7,3},{8,4},{9,5... | collective-permute-start | bytes 245768 | tf_op jit(solution)/shard_map/ppermute | solution.py:257
  13.9 7.5 %collective-permute-start.1 = (bf16[2,2,40,256]{3,1,2,0:T(2,128)(2,1)}, bf16[2,2,40,256]{3,1,2,0:T(2,128)(2,1)S(1)}, u32[]{:S(2)}, u32[]{:S(2)}) collective-permute-start(bf16[2,2,40,256]{3,1,2,0:T(2,128)(2,1)} %bitcast.91), channel_id=1, source_target_pairs={{0,248},{1,249},{2,250},{3,251},{4,252},{5,253},{6,254},{7,255},{8... | collective-permute-start | bytes 245768 | tf_op jit(solution)/shard_map/ppermute | solution.py:257
  22.6 6.6 %copy-start = (bf16[2,256,256]{2,1,0:T(8,128)(2,1)S(1)}, bf16[2,256,256]{2,1,0:T(8,128)(2,1)}, u32[]{:S(2)}) copy-start(bf16[2,256,256]{2,1,0:T(8,128)(2,1)} %param.13) | copy-start | bytes 786436
  23.6 5.9 %copy-start.1 = (bf16[256,2,256]{2,1,0:T(2,128)(2,1)S(1)}, bf16[256,2,256]{2,1,0:T(2,128)(2,1)}, u32[]{:S(2)}) copy-start(bf16[256,2,256]{2,1,0:T(2,128)(2,1)} %param.12) | copy-start | bytes 786436
  23.6 13.0 %all-to-all-start = ((bf16[4,2,2,2,40,256]{5,4,3,2,1,0:T(8,128)(2,1)}), bf16[4,2,2,2,40,256]{5,4,3,2,1,0:T(8,128)(2,1)S(1)}, u32[]{:S(2)}, u32[]{:S(2)}) async-start(bf16[4,2,2,2,40,256]{5,4,3,2,1,0:T(8,128)(2,1)} %broadcast_select_fusion), calls=%async_computation | async-start | bytes 1310720 | tf_op jit(solution)/shard_map/all_to_all | solution.py:266
  39.0 3.9 %copy-start.2 = (bf16[1,256,256]{2,1,0:T(8,128)(2,1)S(1)}, bf16[1,256,256]{2,1,0:T(8,128)(2,1)}, u32[]{:S(2)}) copy-start(bf16[1,256,256]{2,1,0:T(8,128)(2,1)} %param.17) | copy-start | bytes 393220
  39.0 3.8 %collective-permute-start.2 = (bf16[2,256,256]{2,1,0:T(8,128)(2,1)}, bf16[2,256,256]{2,1,0:T(8,128)(2,1)S(1)}, u32[]{:S(2)}, u32[]{:S(2)}) collective-permute-start(bf16[2,256,256]{2,1,0:T(8,128)(2,1)} %get-tuple-element.55), channel_id=1, source_target_pairs={{0,256},{1,257},{2,258},{3,259},{4,260},{5,261},{6,262},{7,263},{8... | collective-permute-start | bytes 786440 | tf_op jit(solution)/shard_map/ppermute | solution.py:19
  43.7 5.1 %collective-permute-start.3 = (bf16[2,256,256]{2,1,0:T(8,128)(2,1)}, bf16[2,256,256]{2,1,0:T(8,128)(2,1)S(1)}, u32[]{:S(2)}, u32[]{:S(2)}) collective-permute-start(bf16[2,256,256]{2,1,0:T(8,128)(2,1)} %get-tuple-element.57), channel_id=1, source_target_pairs={{256,0},{257,1},{258,2},{259,3},{260,4},{261,5},{262,6},{263,7},{2... | collective-permute-start | bytes 786440 | tf_op jit(solution)/shard_map/ppermute | solution.py:19
  63.6 11.8 %collective-permute-start.4 = (bf16[2,2,40,256]{3,2,1,0:T(8,128)(2,1)S(1)}, bf16[2,2,40,256]{3,2,1,0:T(8,128)(2,1)S(1)}, u32[]{:S(2)}, u32[]{:S(2)}) collective-permute-start(bf16[2,2,40,256]{3,2,1,0:T(8,128)(2,1)S(1)} %get-tuple-element.61), channel_id=1, source_target_pairs={{0,4},{1,5},{2,6},{3,7},{4,8},{5,9},{6,10},{7,11},{8,12},{9,13},{1... | collective-permute-start | bytes 245768 | tf_op jit(solution)/shard_map/ppermute | solution.py:353
  67.1 11.1 %collective-permute-start.5 = (bf16[2,2,40,256]{3,2,1,0:T(8,128)(2,1)S(1)}, bf16[2,2,40,256]{3,2,1,0:T(8,128)(2,1)S(1)}, u32[]{:S(2)}, u32[]{:S(2)}) collective-permute-start(bf16[2,2,40,256]{3,2,1,0:T(8,128)(2,1)S(1)} %get-tuple-element.62), channel_id=1, source_target_pairs={{0,8},{1,9},{2,10},{3,11},{4,12},{5,13},{6,14},{7,15},{8,16},{9,17... | collective-permute-start | bytes 245768 | tf_op jit(solution)/shard_map/ppermute | solution.py:353

commit v10 on v9

--- a/solution.py
+++ b/solution.py
@@ -2,6 +2,7 @@
 
 import jax
 from jax.experimental import pallas as pl
+from jax.experimental.pallas import tpu as pltpu
 import jax.numpy as jnp
 from jax import lax
 from jax.sharding import PartitionSpec as P
@@ -184,8 +185,8 @@
         bar_real, bar_imag = times_right_conj(*middle, real, imag)
         inc_real = incident_ref[slice_at, 0].astype(jnp.float32)
         inc_imag = incident_ref[slice_at, 1].astype(jnp.float32)
-        grad_ref[slice_at, 0] = inc_real * bar_real + inc_imag * bar_imag
-        grad_ref[slice_at, 1] = inc_real * bar_imag - inc_imag * bar_real
+        grad_ref[slice_at, 0] = (inc_real * bar_real + inc_imag * bar_imag).astype(grad_ref.dtype)
+        grad_ref[slice_at, 1] = (inc_real * bar_imag - inc_imag * bar_real).astype(grad_ref.dtype)
         pat_real = patch_ref[slice_at, 0].astype(jnp.float32)
         pat_imag = patch_ref[slice_at, 1].astype(jnp.float32)
         back = rounded(
@@ -209,7 +210,8 @@
 ):
     mats = mats_of(mat_ref)
     field = march_steps((field_ref[0], field_ref[1]), patch_ref, mats, incident_ref)
-    back = far_steps(field, measured_ref[...], mats_of(dft_ref))
+    dft = (dft_ref[0], dft_ref[1], dft_ref[0], dft_ref[1])
+    back = far_steps(field, measured_ref[...], dft)
     back = retreat_steps(back, patch_ref, incident_ref, mats, grad_ref)
     out_ref[0] = back[0]
     out_ref[1] = back[1]
@@ -227,13 +229,14 @@
     return jnp.stack((matrix[0], matrix[1], matrix[0].T, matrix[1].T))
 
 
-def run_kernel(body, outs, flops, *args):
+def run_kernel(body, outs, flops, *args, scratch=()):
     moved = sum(arg.size * arg.dtype.itemsize for arg in args)
     listed = outs if isinstance(outs, tuple) else (outs,)
     moved += sum(out.size * jnp.dtype(out.dtype).itemsize for out in listed)
     return pl.pallas_call(
         body,
         out_shape=outs,
+        scratch_shapes=list(scratch),
         cost_estimate=pl.CostEstimate(flops=flops, transcendentals=0, bytes_accessed=moved),
     )(*args)
 
@@ -273,7 +276,7 @@
     live_slots = jnp.arange(slot_count, dtype=jnp.int32) < counts[0]
 
     kernel_planes = planes_of(kernel)
-    dft_planes = planes_of(dft_matrix(width))
+    dft_table = dft_matrix(width)
     field_shape = jax.ShapeDtypeStruct((2, width, width), jnp.bfloat16)
     dot_flops = 2 * width**3
 
@@ -283,26 +286,31 @@
         return tuple(run_kernel(march_kernel, outs, flops, field_in, planes, kernel_planes))
 
     def retreat(back_in, incidents):
-        outs = (field_shape, jax.ShapeDtypeStruct(planes.shape, jnp.float32))
+        outs = (field_shape, jax.ShapeDtypeStruct(planes.shape, jnp.bfloat16))
         flops = slice_count * 8 * dot_flops
         return tuple(
             run_kernel(retreat_kernel, outs, flops, back_in, planes, incidents, kernel_planes)
         )
 
     def whole(field_in):
-        outs = (
-            field_shape,
-            jax.ShapeDtypeStruct(planes.shape, jnp.float32),
-            jax.ShapeDtypeStruct(planes.shape, jnp.bfloat16),
-        )
+        outs = (field_shape, jax.ShapeDtypeStruct(planes.shape, jnp.bfloat16))
         flops = slice_count * 16 * dot_flops + 16 * dot_flops
-        back, grads, _ = run_kernel(
-            middle_kernel, outs, flops, field_in, planes, kernel_planes, intensity[0], dft_planes
+        scratch = (pltpu.VMEM(planes.shape, jnp.bfloat16),)
+        back, grads = run_kernel(
+            middle_kernel,
+            outs,
+            flops,
+            field_in,
+            planes,
+            kernel_planes,
+            intensity[0],
+            dft_table,
+            scratch=scratch,
         )
         return (back, grads)
 
     stored = jnp.zeros(planes.shape, jnp.bfloat16)
-    gradients = jnp.zeros(planes.shape, jnp.float32)
+    gradients = jnp.zeros(planes.shape, jnp.bfloat16)
     waves = jnp.transpose(probe, (1, 0, 2))
     for section_step in range(sections - 1):
         if section_step > 0:

time: 79.4 us -> 77.4 us (0.975)
  other arithmetic: 6.4 us -> 4.38 us
  waiting for transfers between devices: 21.7 us -> 23.5 us
  local copies, waits for them, and re-layouts: 2.49 us -> 1.56 us
    slice x2 -> x0, other arithmetic: 1.97 us -> none  [planes_of(): return jnp.stack((matrix[0], matrix[1], matrix[0].T, matrix[1].T))]
    another operation x3 -> x1, other arithmetic: 1.24 us -> 0.06 us  [planes_of(): return jnp.stack((matrix[0], matrix[1], matrix[0].T, matrix[1].T))]
    another operation x0 -> x2, other arithmetic: none -> 1.13 us
    all_to_all x1, waiting for transfers between devices: 6.07 us -> 7.05 us  [on_device(): got = lax.all_to_all(sent, row_axis, 0, 0)]
    ppermute x2, waiting for transfers between devices: 3.1 us -> 3.96 us  [passed_along(): return lax.ppermute(shard, axis, pairs)]
  transfers between devices with their start and end apart: 7 -> 7, of which waited for: 5 -> 5; matrix products, arithmetic and copies ran while one was open for 5% -> 2% of each run, Pallas kernels for 0% -> 0%
where the time goes in v10:
time: 77.4 us; the launch traced here: 77.1 us
  starting transfers between devices  30.9 us (40%)
  waiting for transfers between devices  23.5 us (30%)
  blocking collectives  12 us (16%)
  other arithmetic  4.38 us (6%)
  Pallas kernels  3.02 us (4%)
  between operations  1.65 us (2%)
  local copies, waits for them, and re-layouts  1.56 us (2%)
    ppermute x2, starting transfers between devices, on_device(): lax.ppermute(slab, tile_axes, [(s, (s - ahead * row_size) % tile_count) f...  17.9 us
    all_to_all x1, blocking collectives, on_device(): incoming = lax.all_to_all(outgoing, row_axis, 0, 0).astype(jnp.float32)  12 us
    ppermute x2, waiting for transfers between devices, on_device(): lax.ppermute(spill.astype(jnp.bfloat16), tile_axes, [(s, (s + ahead * row...  9.13 us
    all_to_all x1, waiting for transfers between devices, on_device(): got = lax.all_to_all(sent, row_axis, 0, 0)  7.05 us
    ppermute x2, starting transfers between devices, on_device(): lax.ppermute(spill.astype(jnp.bfloat16), tile_axes, [(s, (s + ahead * row...  5.45 us
    all_to_all x1, starting transfers between devices, on_device(): got = lax.all_to_all(sent, row_axis, 0, 0)  4.96 us
    ppermute x2, waiting for transfers between devices, passed_along(): return lax.ppermute(shard, axis, pairs)  3.96 us
    ppermute x2, waiting for transfers between devices, on_device(): lax.ppermute(slab, tile_axes, [(s, (s - ahead * row_size) % tile_count) f...  3.37 us
  transfers between devices with their start and end apart: 7, of which 5 were waited for; matrix products, arithmetic and copies ran while one was open for 2% of the time, Pallas kernels for 0%

profile of v10, /device:TPU:2, one launch (start us, length us, event | category | flops | bytes accessed | tf_op | source)
XLA Modules:
  0.0 77.1 jit_solution(7259980805724703731)
XLA Ops:
  0.0 13.8 %collective-permute-start = (bf16[2,2,40,256]{3,1,2,0:T(2,128)(2,1)}, bf16[2,2,40,256]{3,1,2,0:T(2,128)(2,1)S(1)}, u32[]{:S(2)}, u32[]{:S(2)}) collective-permute-start(bf16[2,2,40,256]{3,1,2,0:T(2,128)(2,1)} %bitcast.78), channel_id=1, source_target_pairs={{0,252},{1,253},{2,254},{3,255},{4,0},{5,1},{6,2},{7,3},{8,4},{9,5... | collective-permute-start | bytes 245768 | tf_op jit(solution)/shard_map/ppermute | solution.py:260
  13.9 4.1 %collective-permute-start.1 = (bf16[2,2,40,256]{3,1,2,0:T(2,128)(2,1)}, bf16[2,2,40,256]{3,1,2,0:T(2,128)(2,1)S(1)}, u32[]{:S(2)}, u32[]{:S(2)}) collective-permute-start(bf16[2,2,40,256]{3,1,2,0:T(2,128)(2,1)} %bitcast.79), channel_id=1, source_target_pairs={{0,248},{1,249},{2,250},{3,251},{4,252},{5,253},{6,254},{7,255},{8... | collective-permute-start | bytes 245768 | tf_op jit(solution)/shard_map/ppermute | solution.py:260
  17.9 0.0 collective-permute-done
  17.9 3.4 %collective-permute-done.1 = bf16[2,2,40,256]{3,1,2,0:T(2,128)(2,1)S(1)} collective-permute-done((bf16[2,2,40,256]{3,1,2,0:T(2,128)(2,1)}, bf16[2,2,40,256]{3,1,2,0:T(2,128)(2,1)S(1)}, u32[]{:S(2)}, u32[]{:S(2)}) %collective-permute-start.1) | collective-permute-done | bytes 81952 | tf_op jit(solution)/shard_map/ppermute | solution.py:260
  21.3 1.2 %pad_maximum_fusion.2 = (bf16[2,2,2,40,256]{4,2,3,1,0:T(2,128)(2,1)S(1)}, bf16[2,2,2,40,256]{4,2,3,1,0:T(2,128)(2,1)S(1)}) fusion(bf16[1,2,2,40,256]{4,2,3,1,0:T(2,128)(2,1)S(1)} %bitcast.81, bf16[1,2,2,40,256]{4,2,3,1,0:T(2,128)(2,1)} %bitcast.80, bf16[1,2,2,40,256]{4,2,3,1,0:T(2,128)(2,1)S(1)} %bitcast.82), kind=kLoop, calls=%fused_computation.29 | loop fusion | flops 163840 | bytes 573440 | tf_op jit(solution)/shard_map/stack | solution.py:268
  22.6 0.0 copy-start
  22.6 1.0 %broadcast_select_fusion = bf16[4,2,2,2,40,256]{5,4,3,2,1,0:T(8,128)(2,1)} fusion(pred[4]{0:T(512)(128)(4,1)S(1)} %iota_compare_fusion, bf16[2,2,2,40,256]{4,3,2,1,0:T(8,128)(2,1)S(1)} %copy.26, bf16[2,2,2,40,256]{4,3,2,1,0:T(8,128)(2,1)S(1)} %copy.25), kind=kLoop, calls=%fused_computation.14 | loop fusion | flops 327680 | bytes 983044 | tf_op jit(solution)/shard_map/jit(_where)/select_n | solution.py:268
  23.6 0.0 copy-start.1
  23.6 5.0 %all-to-all-start = ((bf16[4,2,2,2,40,256]{5,4,3,2,1,0:T(8,128)(2,1)}), bf16[4,2,2,2,40,256]{5,4,3,2,1,0:T(8,128)(2,1)S(1)}, u32[]{:S(2)}, u32[]{:S(2)}) async-start(bf16[4,2,2,2,40,256]{5,4,3,2,1,0:T(8,128)(2,1)} %broadcast_select_fusion), calls=%async_computation | async-start | bytes 1310720 | tf_op jit(solution)/shard_map/all_to_all | solution.py:269
  29.2 0.0 copy-done
  29.2 0.1 copy.38
  29.3 0.1 copy.39
  29.4 0.0 copy-done.1
  29.5 0.1 pad_maximum_fusion
  29.6 7.1 %all-to-all-done = bf16[4,2,2,2,40,256]{5,4,3,2,1,0:T(8,128)(2,1)S(1)} async-done(((bf16[4,2,2,2,40,256]{5,4,3,2,1,0:T(8,128)(2,1)}), bf16[4,2,2,2,40,256]{5,4,3,2,1,0:T(8,128)(2,1)S(1)}, u32[]{:S(2)}, u32[]{:S(2)}) %all-to-all-start) | async-done | bytes 655392 | tf_op jit(solution)/shard_map/all_to_all | solution.py:269
  36.6 0.2 fusion.2
  37.0 0.1 constant_dynamic-slice_fusion
  37.1 0.0 copy-start.2
  37.2 1.1 %conditional.3 = ((bf16[2,256,256]{2,1,0:T(8,128)(2,1)S(1)}, bf16[2,2,256,256]{3,2,1,0:T(8,128)(2,1)S(1)})) conditional(s32[]{:T(128)} %convert_element_type.65, bf16[2,256,256]{2,1,0:T(8,128)(2,1)S(1)} %bitcast.74, (bf16[2,256,256]{2,1,0:T(8,128)(2,1)S(1)}, bf16[2,2,256,256]{3,2,1,0:T(8,128)(2,1)S(1)}, bf16[4,256,256]{2,1,0:T(8,128)(2,1)S(1)}) %tuple.57), branch_computations={%region_0.1_spmd, %region_1.2_spmd} | conditional | flops 536870912 | bytes 2097160 | solution.py:318
  37.2 1.1 %branch_1_fun.3 = (bf16[2,256,256]{2,1,0:T(8,128)(2,1)S(1)}, bf16[2,2,256,256]{3,2,1,0:T(8,128)(2,1)S(1)}) custom-call(bf16[2,256,256]{2,1,0:T(8,128)(2,1)S(1)} %get-tuple-element.44.field_ref, bf16[2,2,256,256]{3,2,1,0:T(8,128)(2,1)S(1)} %get-tuple-element.45.patch_ref, bf16[4,256,256]{2,1,0:T(8,128)(2,1)S(1)} %get-tuple-element.46.mat_ref), custom_call_target="tpu_custom_call" | custom-call | flops 536870912 | bytes 2097152 | tf_op jit(solution)/shard_map/cond/branch_1_fun/pallas_call | solution.py:236
  38.3 1.3 %collective-permute-start.2 = (bf16[2,256,256]{2,1,0:T(8,128)(2,1)S(1)}, bf16[2,256,256]{2,1,0:T(8,128)(2,1)S(1)}, u32[]{:S(2)}, u32[]{:S(2)}) collective-permute-start(bf16[2,256,256]{2,1,0:T(8,128)(2,1)S(1)} %get-tuple-element.61), channel_id=1, source_target_pairs={{0,256},{1,257},{2,258},{3,259},{4,260},{5,261},{6,262},{7,263},{8... | collective-permute-start | bytes 786440 | tf_op jit(solution)/shard_map/ppermute | solution.py:20
  39.6 1.1 %multiply_convert_fusion = (bf16[1,256,256]{2,1,0:T(8,128)(2,1)S(1)}, bf16[1,256,256]{2,1,0:T(8,128)(2,1)S(1)}) fusion(), kind=kLoop, calls=%fused_computation.24 | loop fusion | flops 1245184 | bytes 262144 | tf_op jit(solution)/shard_map/convert.2
  40.8 0.0 collective-permute-done.2
  40.8 0.0 copy-done.2
  40.8 0.1 conditional.4
  40.9 1.3 %collective-permute-start.3 = (bf16[2,256,256]{2,1,0:T(8,128)(2,1)S(1)}, bf16[2,256,256]{2,1,0:T(8,128)(2,1)S(1)}, u32[]{:S(2)}, u32[]{:S(2)}) collective-permute-start(bf16[2,256,256]{2,1,0:T(8,128)(2,1)S(1)} %get-tuple-element.63), channel_id=1, source_target_pairs={{256,0},{257,1},{258,2},{259,3},{260,4},{261,5},{262,6},{263,7},{2... | collective-permute-start | bytes 786440 | tf_op jit(solution)/shard_map/ppermute | solution.py:20
  42.8 4.0 %collective-permute-done.3 = bf16[2,256,256]{2,1,0:T(8,128)(2,1)S(1)} collective-permute-done((bf16[2,256,256]{2,1,0:T(8,128)(2,1)S(1)}, bf16[2,256,256]{2,1,0:T(8,128)(2,1)S(1)}, u32[]{:S(2)}, u32[]{:S(2)}) %collective-permute-start.3) | collective-permute-done | bytes 262176 | tf_op jit(solution)/shard_map/ppermute | solution.py:20
  46.8 1.9 %conditional.5 = (bf16[2,2,256,256]{3,2,1,0:T(8,128)(2,1)S(1)}) conditional(s32[]{:T(128)} %convert_element_type.65, bf16[2,2,256,256]{3,2,1,0:T(8,128)(2,1)S(1)} %get-tuple-element.62, (bf16[2,256,256]{2,1,0:T(8,128)(2,1)S(1)}, bf16[2,2,256,256]{3,2,1,0:T(8,128)(2,1)S(1)}, bf16[2,2,256,256]{3,2,1,0:T(8,128)(2,1)S(1)}, ...), branch_computations={%region_4.5_spmd, %region_5.6_spmd} | conditional | flops 536870912 | bytes 2621448 | solution.py:335
  46.8 1.9 %branch_1_fun.5 = (bf16[2,256,256]{2,1,0:T(8,128)(2,1)}, bf16[2,2,256,256]{3,2,1,0:T(8,128)(2,1)S(1)}) custom-call(bf16[2,256,256]{2,1,0:T(8,128)(2,1)S(1)} %get-tuple-element.52.back_ref, bf16[2,2,256,256]{3,2,1,0:T(8,128)(2,1)S(1)} %get-tuple-element.53.patch_ref, bf16[2,2,256,256]{3,2,1,0:T(8,128)(2,1)S(1)} %get-tuple-element.54.incident_ref, ...), custom_call_target="tpu_custom_call" | custom-call | flops 536870912 | bytes 2621440 | tf_op jit(solution)/shard_map/cond/branch_1_fun/pallas_call | solution.py:236
  48.7 0.1 convert_multiply_fusion
  48.8 0.2 fusion
  49.0 0.3 fusion.1
  49.3 12.0 %all_to_all.10 = bf16[4,2,2,2,40,256]{5,4,1,3,2,0:T(8,128)(2,1)S(1)} all-to-all(bf16[4,2,2,2,40,256]{5,4,1,3,2,0:T(8,128)(2,1)S(1)} %copy.29), channel_id=1, replica_groups=mesh['section'=2,'lines'=64,'x'=4] {'x'}, dimensions={0} | all-to-all | bytes 1310720 | tf_op jit(solution)/shard_map/all_to_all | solution.py:351
  61.3 0.2 convert_element_type.74
  61.5 0.2 select_reduce_fusion.1
  61.7 3.5 %collective-permute-start.4 = (bf16[2,2,40,256]{3,2,1,0:T(8,128)(2,1)S(1)}, bf16[2,2,40,256]{3,2,1,0:T(8,128)(2,1)S(1)}, u32[]{:S(2)}, u32[]{:S(2)}) collective-permute-start(bf16[2,2,40,256]{3,2,1,0:T(8,128)(2,1)S(1)} %get-tuple-element.67), channel_id=1, source_target_pairs={{0,4},{1,5},{2,6},{3,7},{4,8},{5,9},{6,10},{7,11},{8,12},{9,13},{1... | collective-permute-start | bytes 245768 | tf_op jit(solution)/shard_map/ppermute | solution.py:361
  65.2 1.9 %collective-permute-start.5 = (bf16[2,2,40,256]{3,2,1,0:T(8,128)(2,1)S(1)}, bf16[2,2,40,256]{3,2,1,0:T(8,128)(2,1)S(1)}, u32[]{:S(2)}, u32[]{:S(2)}) collective-permute-start(bf16[2,2,40,256]{3,2,1,0:T(8,128)(2,1)S(1)} %get-tuple-element.68), channel_id=1, source_target_pairs={{0,8},{1,9},{2,10},{3,11},{4,12},{5,13},{6,14},{7,15},{8,16},{9,17... | collective-permute-start | bytes 245768 | tf_op jit(solution)/shard_map/ppermute | solution.py:361
  67.1 6.3 %collective-permute-done.4 = bf16[2,2,40,256]{3,2,1,0:T(8,128)(2,1)S(1)} collective-permute-done((bf16[2,2,40,256]{3,2,1,0:T(8,128)(2,1)S(1)}, bf16[2,2,40,256]{3,2,1,0:T(8,128)(2,1)S(1)}, u32[]{:S(2)}, u32[]{:S(2)}) %collective-permute-start.4) | collective-permute-done | bytes 81952 | tf_op jit(solution)/shard_map/ppermute | solution.py:361
  73.5 2.8 %collective-permute-done.5 = bf16[2,2,40,256]{3,2,1,0:T(8,128)(2,1)S(1)} collective-permute-done((bf16[2,2,40,256]{3,2,1,0:T(8,128)(2,1)S(1)}, bf16[2,2,40,256]{3,2,1,0:T(8,128)(2,1)S(1)}, u32[]{:S(2)}, u32[]{:S(2)}) %collective-permute-start.5) | collective-permute-done | bytes 81952 | tf_op jit(solution)/shard_map/ppermute | solution.py:361
  76.3 0.8 copy.34
  (18 shorter events, 0.3 us)
Async XLA Ops:
  0.0 17.9 %collective-permute-start = (bf16[2,2,40,256]{3,1,2,0:T(2,128)(2,1)}, bf16[2,2,40,256]{3,1,2,0:T(2,128)(2,1)S(1)}, u32[]{:S(2)}, u32[]{:S(2)}) collective-permute-start(bf16[2,2,40,256]{3,1,2,0:T(2,128)(2,1)} %bitcast.78), channel_id=1, source_target_pairs={{0,252},{1,253},{2,254},{3,255},{4,0},{5,1},{6,2},{7,3},{8,4},{9,5... | collective-permute-start | bytes 245768 | tf_op jit(solution)/shard_map/ppermute | solution.py:260
  13.9 7.5 %collective-permute-start.1 = (bf16[2,2,40,256]{3,1,2,0:T(2,128)(2,1)}, bf16[2,2,40,256]{3,1,2,0:T(2,128)(2,1)S(1)}, u32[]{:S(2)}, u32[]{:S(2)}) collective-permute-start(bf16[2,2,40,256]{3,1,2,0:T(2,128)(2,1)} %bitcast.79), channel_id=1, source_target_pairs={{0,248},{1,249},{2,250},{3,251},{4,252},{5,253},{6,254},{7,255},{8... | collective-permute-start | bytes 245768 | tf_op jit(solution)/shard_map/ppermute | solution.py:260
  22.6 6.6 %copy-start = (bf16[2,256,256]{2,1,0:T(8,128)(2,1)S(1)}, bf16[2,256,256]{2,1,0:T(8,128)(2,1)}, u32[]{:S(2)}) copy-start(bf16[2,256,256]{2,1,0:T(8,128)(2,1)} %param.13) | copy-start | bytes 786436
  23.6 5.9 %copy-start.1 = (bf16[256,2,256]{2,1,0:T(2,128)(2,1)S(1)}, bf16[256,2,256]{2,1,0:T(2,128)(2,1)}, u32[]{:S(2)}) copy-start(bf16[256,2,256]{2,1,0:T(2,128)(2,1)} %param.12) | copy-start | bytes 786436
  23.6 13.0 %all-to-all-start = ((bf16[4,2,2,2,40,256]{5,4,3,2,1,0:T(8,128)(2,1)}), bf16[4,2,2,2,40,256]{5,4,3,2,1,0:T(8,128)(2,1)S(1)}, u32[]{:S(2)}, u32[]{:S(2)}) async-start(bf16[4,2,2,2,40,256]{5,4,3,2,1,0:T(8,128)(2,1)} %broadcast_select_fusion), calls=%async_computation | async-start | bytes 1310720 | tf_op jit(solution)/shard_map/all_to_all | solution.py:269
  37.1 3.6 %copy-start.2 = (bf16[1,256,256]{2,1,0:T(8,128)(2,1)S(1)}, bf16[1,256,256]{2,1,0:T(8,128)(2,1)}, u32[]{:S(2)}) copy-start(bf16[1,256,256]{2,1,0:T(8,128)(2,1)} %param.17) | copy-start | bytes 393220
  38.3 2.5 %collective-permute-start.2 = (bf16[2,256,256]{2,1,0:T(8,128)(2,1)S(1)}, bf16[2,256,256]{2,1,0:T(8,128)(2,1)S(1)}, u32[]{:S(2)}, u32[]{:S(2)}) collective-permute-start(bf16[2,256,256]{2,1,0:T(8,128)(2,1)S(1)} %get-tuple-element.61), channel_id=1, source_target_pairs={{0,256},{1,257},{2,258},{3,259},{4,260},{5,261},{6,262},{7,263},{8... | collective-permute-start | bytes 786440 | tf_op jit(solution)/shard_map/ppermute | solution.py:20
  40.9 5.9 %collective-permute-start.3 = (bf16[2,256,256]{2,1,0:T(8,128)(2,1)S(1)}, bf16[2,256,256]{2,1,0:T(8,128)(2,1)S(1)}, u32[]{:S(2)}, u32[]{:S(2)}) collective-permute-start(bf16[2,256,256]{2,1,0:T(8,128)(2,1)S(1)} %get-tuple-element.63), channel_id=1, source_target_pairs={{256,0},{257,1},{258,2},{259,3},{260,4},{261,5},{262,6},{263,7},{2... | collective-permute-start | bytes 786440 | tf_op jit(solution)/shard_map/ppermute | solution.py:20
  61.7 11.8 %collective-permute-start.4 = (bf16[2,2,40,256]{3,2,1,0:T(8,128)(2,1)S(1)}, bf16[2,2,40,256]{3,2,1,0:T(8,128)(2,1)S(1)}, u32[]{:S(2)}, u32[]{:S(2)}) collective-permute-start(bf16[2,2,40,256]{3,2,1,0:T(8,128)(2,1)S(1)} %get-tuple-element.67), channel_id=1, source_target_pairs={{0,4},{1,5},{2,6},{3,7},{4,8},{5,9},{6,10},{7,11},{8,12},{9,13},{1... | collective-permute-start | bytes 245768 | tf_op jit(solution)/shard_map/ppermute | solution.py:361
  65.2 11.1 %collective-permute-start.5 = (bf16[2,2,40,256]{3,2,1,0:T(8,128)(2,1)S(1)}, bf16[2,2,40,256]{3,2,1,0:T(8,128)(2,1)S(1)}, u32[]{:S(2)}, u32[]{:S(2)}) collective-permute-start(bf16[2,2,40,256]{3,2,1,0:T(8,128)(2,1)S(1)} %get-tuple-element.68), channel_id=1, source_target_pairs={{0,8},{1,9},{2,10},{3,11},{4,12},{5,13},{6,14},{7,15},{8,16},{9,17... | collective-permute-start | bytes 245768 | tf_op jit(solution)/shard_map/ppermute | solution.py:361

commit v11 on v10

--- a/solution.py
+++ b/solution.py
@@ -264,8 +264,10 @@
         )
         for ahead in (1, 2)
     ]
-    own_row = (chunk_ids <= place)[:, None, None, None, None, None]
-    sent = jnp.where(own_row, jnp.stack(later[:2])[None], jnp.stack(later[1:])[None])
+    own_row = (chunk_ids <= place)[:, None, None, None, None]
+    sent = jnp.stack(
+        [jnp.where(own_row, later[half][None], later[half + 1][None]) for half in (0, 1)], axis=1
+    )
     got = lax.all_to_all(sent, row_axis, 0, 0)
     got = lax.dynamic_slice_in_dim(jnp.concatenate((got, got), axis=0), place, row_size, 0)
     window = jnp.concatenate(

time: 77.4 us -> 76.2 us (0.984)
  other arithmetic: 4.38 us -> 3.2 us
  waiting for transfers between devices: 23.5 us -> 22.6 us
  local copies, waits for them, and re-layouts: 1.56 us -> 2.45 us
    ppermute x2, waiting for transfers between devices: 3.37 us -> 2.44 us  [on_device(): lax.ppermute(slab, tile_axes, [(s, (s - ahead * row_size) % tile_count) f...]
    transpose x0 -> x1, local copies, waits for them, and re-layouts: none -> 0.9 us  [on_device(): slab = jnp.transpose(object_slab, (0, 2, 1, 3))]
    select_n x1, other arithmetic: 0.96 us -> 0.12 us  [on_device(): jnp.where(own_row, later[half][None], later[half + 1][None])]
  transfers between devices with their start and end apart: 7 -> 7, of which waited for: 5 -> 5; matrix products, arithmetic and copies ran while one was open for 2% -> 3% of each run, Pallas kernels for 0% -> 0%
where the time goes in v11:
time: 76.2 us; the launch traced here: 75.8 us
  starting transfers between devices  30.9 us (41%)
  waiting for transfers between devices  22.6 us (30%)
  blocking collectives  12 us (16%)
  other arithmetic  3.2 us (4%)
  Pallas kernels  3.03 us (4%)
  local copies, waits for them, and re-layouts  2.45 us (3%)
  between operations  1.65 us (2%)
    ppermute x2, starting transfers between devices, on_device(): lax.ppermute(slab, tile_axes, [(s, (s - ahead * row_size) % tile_count) f...  17.9 us
    all_to_all x1, blocking collectives, on_device(): incoming = lax.all_to_all(outgoing, row_axis, 0, 0).astype(jnp.float32)  12 us
    ppermute x2, waiting for transfers between devices, on_device(): lax.ppermute(spill.astype(jnp.bfloat16), tile_axes, [(s, (s + ahead * row...  9.12 us
    all_to_all x1, waiting for transfers between devices, on_device(): got = lax.all_to_all(sent, row_axis, 0, 0)  7.05 us
    ppermute x2, starting transfers between devices, on_device(): lax.ppermute(spill.astype(jnp.bfloat16), tile_axes, [(s, (s + ahead * row...  5.47 us
    all_to_all x1, starting transfers between devices, on_device(): got = lax.all_to_all(sent, row_axis, 0, 0)  4.96 us
    ppermute x2, waiting for transfers between devices, passed_along(): return lax.ppermute(shard, axis, pairs)  3.96 us
    pallas_call x2, Pallas kernels, run_kernel(): pl.pallas_call(body, out_shape=outs, scratch_shapes=list(scratch), cost_e...  3.03 us
  transfers between devices with their start and end apart: 7, of which 5 were waited for; matrix products, arithmetic and copies ran while one was open for 3% of the time, Pallas kernels for 0%

profile of v11, /device:TPU:2, one launch (start us, length us, event | category | flops | bytes accessed | tf_op | source)
XLA Modules:
  0.0 75.8 jit_solution(8952960797301175118)
XLA Ops:
  0.0 13.8 %collective-permute-start = (bf16[2,2,40,256]{3,1,2,0:T(2,128)(2,1)}, bf16[2,2,40,256]{3,1,2,0:T(2,128)(2,1)S(1)}, u32[]{:S(2)}, u32[]{:S(2)}) collective-permute-start(bf16[2,2,40,256]{3,1,2,0:T(2,128)(2,1)} %bitcast.74), channel_id=1, source_target_pairs={{0,252},{1,253},{2,254},{3,255},{4,0},{5,1},{6,2},{7,3},{8,4},{9,5... | collective-permute-start | bytes 245768 | tf_op jit(solution)/shard_map/ppermute | solution.py:260
  13.8 4.0 %collective-permute-start.1 = (bf16[2,2,40,256]{3,1,2,0:T(2,128)(2,1)}, bf16[2,2,40,256]{3,1,2,0:T(2,128)(2,1)S(1)}, u32[]{:S(2)}, u32[]{:S(2)}) collective-permute-start(bf16[2,2,40,256]{3,1,2,0:T(2,128)(2,1)} %bitcast.75), channel_id=1, source_target_pairs={{0,248},{1,249},{2,250},{3,251},{4,252},{5,253},{6,254},{7,255},{8... | collective-permute-start | bytes 245768 | tf_op jit(solution)/shard_map/ppermute | solution.py:260
  17.9 0.9 %copy.27 = bf16[2,2,40,256]{3,2,1,0:T(8,128)(2,1)S(1)} copy(bf16[2,2,40,256]{3,1,2,0:T(2,128)(2,1)} %bitcast.76) | data formatting | bytes 163840 | tf_op jit(solution)/shard_map/transpose | solution.py:258
  18.8 0.0 collective-permute-done
  18.9 2.4 %collective-permute-done.1 = bf16[2,2,40,256]{3,1,2,0:T(2,128)(2,1)S(1)} collective-permute-done((bf16[2,2,40,256]{3,1,2,0:T(2,128)(2,1)}, bf16[2,2,40,256]{3,1,2,0:T(2,128)(2,1)S(1)}, u32[]{:S(2)}, u32[]{:S(2)}) %collective-permute-start.1) | collective-permute-done | bytes 81952 | tf_op jit(solution)/shard_map/ppermute | solution.py:260
  21.3 0.1 broadcast_select_fusion.1
  21.4 0.0 copy-start
  21.4 0.9 %pad_maximum_fusion = bf16[4,2,2,2,40,256]{5,4,3,2,1,0:T(8,128)(2,1)} fusion(bf16[4,1,2,2,40,256]{5,4,3,2,1,0:T(8,128)(2,1)S(1)} %get-tuple-element.73, bf16[4,1,2,2,40,256]{5,4,3,2,1,0:T(8,128)(2,1)S(1)} %get-tuple-element.72), kind=kLoop, calls=%fused_computation.11 | loop fusion | flops 327680 | bytes 1310720 | tf_op jit(solution)/shard_map/stack | solution.py:268
  22.4 0.0 copy-start.1
  22.4 5.0 %all-to-all-start = ((bf16[4,2,2,2,40,256]{5,4,3,2,1,0:T(8,128)(2,1)}), bf16[4,2,2,2,40,256]{5,4,3,2,1,0:T(8,128)(2,1)S(1)}, u32[]{:S(2)}, u32[]{:S(2)}) async-start(bf16[4,2,2,2,40,256]{5,4,3,2,1,0:T(8,128)(2,1)} %pad_maximum_fusion), calls=%async_computation | async-start | bytes 1310720 | tf_op jit(solution)/shard_map/all_to_all | solution.py:271
  28.0 0.0 copy-done
  28.0 0.1 copy.41
  28.1 0.1 copy.42
  28.2 0.0 copy-done.1
  28.3 0.1 pad_maximum_fusion.1
  28.3 7.1 %all-to-all-done = bf16[4,2,2,2,40,256]{5,4,3,2,1,0:T(8,128)(2,1)S(1)} async-done(((bf16[4,2,2,2,40,256]{5,4,3,2,1,0:T(8,128)(2,1)}), bf16[4,2,2,2,40,256]{5,4,3,2,1,0:T(8,128)(2,1)S(1)}, u32[]{:S(2)}, u32[]{:S(2)}) %all-to-all-start) | async-done | bytes 655392 | tf_op jit(solution)/shard_map/all_to_all | solution.py:271
  35.4 0.2 fusion.2
  35.8 0.1 constant_dynamic-slice_fusion
  35.9 0.0 copy-start.2
  35.9 1.2 %conditional.3 = ((bf16[2,256,256]{2,1,0:T(8,128)(2,1)S(1)}, bf16[2,2,256,256]{3,2,1,0:T(8,128)(2,1)S(1)})) conditional(s32[]{:T(128)} %convert_element_type.65, bf16[2,256,256]{2,1,0:T(8,128)(2,1)S(1)} %bitcast.70, (bf16[2,256,256]{2,1,0:T(8,128)(2,1)S(1)}, bf16[2,2,256,256]{3,2,1,0:T(8,128)(2,1)S(1)}, bf16[4,256,256]{2,1,0:T(8,128)(2,1)S(1)}) %tuple.57), branch_computations={%region_0.1_spmd, %region_1.2_spmd} | conditional | flops 536870912 | bytes 2097160 | solution.py:320
  35.9 1.1 %branch_1_fun.3 = (bf16[2,256,256]{2,1,0:T(8,128)(2,1)S(1)}, bf16[2,2,256,256]{3,2,1,0:T(8,128)(2,1)S(1)}) custom-call(bf16[2,256,256]{2,1,0:T(8,128)(2,1)S(1)} %get-tuple-element.44.field_ref, bf16[2,2,256,256]{3,2,1,0:T(8,128)(2,1)S(1)} %get-tuple-element.45.patch_ref, bf16[4,256,256]{2,1,0:T(8,128)(2,1)S(1)} %get-tuple-element.46.mat_ref), custom_call_target="tpu_custom_call" | custom-call | flops 536870912 | bytes 2097152 | tf_op jit(solution)/shard_map/cond/branch_1_fun/pallas_call | solution.py:236
  37.1 1.3 %collective-permute-start.2 = (bf16[2,256,256]{2,1,0:T(8,128)(2,1)S(1)}, bf16[2,256,256]{2,1,0:T(8,128)(2,1)S(1)}, u32[]{:S(2)}, u32[]{:S(2)}) collective-permute-start(bf16[2,256,256]{2,1,0:T(8,128)(2,1)S(1)} %get-tuple-element.61), channel_id=1, source_target_pairs={{0,256},{1,257},{2,258},{3,259},{4,260},{5,261},{6,262},{7,263},{8... | collective-permute-start | bytes 786440 | tf_op jit(solution)/shard_map/ppermute | solution.py:20
  38.4 1.1 %multiply_convert_fusion = (bf16[1,256,256]{2,1,0:T(8,128)(2,1)S(1)}, bf16[1,256,256]{2,1,0:T(8,128)(2,1)S(1)}) fusion(), kind=kLoop, calls=%fused_computation.26 | loop fusion | flops 1245184 | bytes 262144 | tf_op jit(solution)/shard_map/convert.2
  39.5 0.0 collective-permute-done.2
  39.6 0.0 copy-done.2
  39.6 0.1 conditional.4
  39.7 1.3 %collective-permute-start.3 = (bf16[2,256,256]{2,1,0:T(8,128)(2,1)S(1)}, bf16[2,256,256]{2,1,0:T(8,128)(2,1)S(1)}, u32[]{:S(2)}, u32[]{:S(2)}) collective-permute-start(bf16[2,256,256]{2,1,0:T(8,128)(2,1)S(1)} %get-tuple-element.63), channel_id=1, source_target_pairs={{256,0},{257,1},{258,2},{259,3},{260,4},{261,5},{262,6},{263,7},{2... | collective-permute-start | bytes 786440 | tf_op jit(solution)/shard_map/ppermute | solution.py:20
  41.6 4.0 %collective-permute-done.3 = bf16[2,256,256]{2,1,0:T(8,128)(2,1)S(1)} collective-permute-done((bf16[2,256,256]{2,1,0:T(8,128)(2,1)S(1)}, bf16[2,256,256]{2,1,0:T(8,128)(2,1)S(1)}, u32[]{:S(2)}, u32[]{:S(2)}) %collective-permute-start.3) | collective-permute-done | bytes 262176 | tf_op jit(solution)/shard_map/ppermute | solution.py:20
  45.6 1.9 %conditional.5 = (bf16[2,2,256,256]{3,2,1,0:T(8,128)(2,1)S(1)}) conditional(s32[]{:T(128)} %convert_element_type.65, bf16[2,2,256,256]{3,2,1,0:T(8,128)(2,1)S(1)} %get-tuple-element.62, (bf16[2,256,256]{2,1,0:T(8,128)(2,1)S(1)}, bf16[2,2,256,256]{3,2,1,0:T(8,128)(2,1)S(1)}, bf16[2,2,256,256]{3,2,1,0:T(8,128)(2,1)S(1)}, ...), branch_computations={%region_4.5_spmd, %region_5.6_spmd} | conditional | flops 536870912 | bytes 2621448 | solution.py:337
  45.6 1.9 %branch_1_fun.5 = (bf16[2,256,256]{2,1,0:T(8,128)(2,1)}, bf16[2,2,256,256]{3,2,1,0:T(8,128)(2,1)S(1)}) custom-call(bf16[2,256,256]{2,1,0:T(8,128)(2,1)S(1)} %get-tuple-element.52.back_ref, bf16[2,2,256,256]{3,2,1,0:T(8,128)(2,1)S(1)} %get-tuple-element.53.patch_ref, bf16[2,2,256,256]{3,2,1,0:T(8,128)(2,1)S(1)} %get-tuple-element.54.incident_ref, ...), custom_call_target="tpu_custom_call" | custom-call | flops 536870912 | bytes 2621440 | tf_op jit(solution)/shard_map/cond/branch_1_fun/pallas_call | solution.py:236
  47.5 0.1 convert_multiply_fusion
  47.6 0.2 fusion
  47.8 0.3 fusion.1
  48.1 12.0 %all_to_all.10 = bf16[4,2,2,2,40,256]{5,4,1,3,2,0:T(8,128)(2,1)S(1)} all-to-all(bf16[4,2,2,2,40,256]{5,4,1,3,2,0:T(8,128)(2,1)S(1)} %copy.32), channel_id=1, replica_groups=mesh['section'=2,'lines'=64,'x'=4] {'x'}, dimensions={0} | all-to-all | bytes 1310720 | tf_op jit(solution)/shard_map/all_to_all | solution.py:353
  60.1 0.2 convert_element_type.74
  60.2 0.2 select_reduce_fusion.1
  60.4 3.6 %collective-permute-start.4 = (bf16[2,2,40,256]{3,2,1,0:T(8,128)(2,1)S(1)}, bf16[2,2,40,256]{3,2,1,0:T(8,128)(2,1)S(1)}, u32[]{:S(2)}, u32[]{:S(2)}) collective-permute-start(bf16[2,2,40,256]{3,2,1,0:T(8,128)(2,1)S(1)} %get-tuple-element.67), channel_id=1, source_target_pairs={{0,4},{1,5},{2,6},{3,7},{4,8},{5,9},{6,10},{7,11},{8,12},{9,13},{1... | collective-permute-start | bytes 245768 | tf_op jit(solution)/shard_map/ppermute | solution.py:363
  64.0 1.9 %collective-permute-start.5 = (bf16[2,2,40,256]{3,2,1,0:T(8,128)(2,1)S(1)}, bf16[2,2,40,256]{3,2,1,0:T(8,128)(2,1)S(1)}, u32[]{:S(2)}, u32[]{:S(2)}) collective-permute-start(bf16[2,2,40,256]{3,2,1,0:T(8,128)(2,1)S(1)} %get-tuple-element.68), channel_id=1, source_target_pairs={{0,8},{1,9},{2,10},{3,11},{4,12},{5,13},{6,14},{7,15},{8,16},{9,17... | collective-permute-start | bytes 245768 | tf_op jit(solution)/shard_map/ppermute | solution.py:363
  65.9 6.3 %collective-permute-done.4 = bf16[2,2,40,256]{3,2,1,0:T(8,128)(2,1)S(1)} collective-permute-done((bf16[2,2,40,256]{3,2,1,0:T(8,128)(2,1)S(1)}, bf16[2,2,40,256]{3,2,1,0:T(8,128)(2,1)S(1)}, u32[]{:S(2)}, u32[]{:S(2)}) %collective-permute-start.4) | collective-permute-done | bytes 81952 | tf_op jit(solution)/shard_map/ppermute | solution.py:363
  72.2 2.8 %collective-permute-done.5 = bf16[2,2,40,256]{3,2,1,0:T(8,128)(2,1)S(1)} collective-permute-done((bf16[2,2,40,256]{3,2,1,0:T(8,128)(2,1)S(1)}, bf16[2,2,40,256]{3,2,1,0:T(8,128)(2,1)S(1)}, u32[]{:S(2)}, u32[]{:S(2)}) %collective-permute-start.5) | collective-permute-done | bytes 81952 | tf_op jit(solution)/shard_map/ppermute | solution.py:363
  75.1 0.8 copy.37
  (18 shorter events, 0.3 us)
Async XLA Ops:
  0.0 18.8 %collective-permute-start = (bf16[2,2,40,256]{3,1,2,0:T(2,128)(2,1)}, bf16[2,2,40,256]{3,1,2,0:T(2,128)(2,1)S(1)}, u32[]{:S(2)}, u32[]{:S(2)}) collective-permute-start(bf16[2,2,40,256]{3,1,2,0:T(2,128)(2,1)} %bitcast.74), channel_id=1, source_target_pairs={{0,252},{1,253},{2,254},{3,255},{4,0},{5,1},{6,2},{7,3},{8,4},{9,5... | collective-permute-start | bytes 245768 | tf_op jit(solution)/shard_map/ppermute | solution.py:260
  13.8 7.4 %collective-permute-start.1 = (bf16[2,2,40,256]{3,1,2,0:T(2,128)(2,1)}, bf16[2,2,40,256]{3,1,2,0:T(2,128)(2,1)S(1)}, u32[]{:S(2)}, u32[]{:S(2)}) collective-permute-start(bf16[2,2,40,256]{3,1,2,0:T(2,128)(2,1)} %bitcast.75), channel_id=1, source_target_pairs={{0,248},{1,249},{2,250},{3,251},{4,252},{5,253},{6,254},{7,255},{8... | collective-permute-start | bytes 245768 | tf_op jit(solution)/shard_map/ppermute | solution.py:260
  21.4 6.5 %copy-start = (bf16[2,256,256]{2,1,0:T(8,128)(2,1)S(1)}, bf16[2,256,256]{2,1,0:T(8,128)(2,1)}, u32[]{:S(2)}) copy-start(bf16[2,256,256]{2,1,0:T(8,128)(2,1)} %param.13) | copy-start | bytes 786436
  22.4 5.9 %copy-start.1 = (bf16[256,2,256]{2,1,0:T(2,128)(2,1)S(1)}, bf16[256,2,256]{2,1,0:T(2,128)(2,1)}, u32[]{:S(2)}) copy-start(bf16[256,2,256]{2,1,0:T(2,128)(2,1)} %param.12) | copy-start | bytes 786436
  22.4 13.0 %all-to-all-start = ((bf16[4,2,2,2,40,256]{5,4,3,2,1,0:T(8,128)(2,1)}), bf16[4,2,2,2,40,256]{5,4,3,2,1,0:T(8,128)(2,1)S(1)}, u32[]{:S(2)}, u32[]{:S(2)}) async-start(bf16[4,2,2,2,40,256]{5,4,3,2,1,0:T(8,128)(2,1)} %pad_maximum_fusion), calls=%async_computation | async-start | bytes 1310720 | tf_op jit(solution)/shard_map/all_to_all | solution.py:271
  35.9 3.6 %copy-start.2 = (bf16[1,256,256]{2,1,0:T(8,128)(2,1)S(1)}, bf16[1,256,256]{2,1,0:T(8,128)(2,1)}, u32[]{:S(2)}) copy-start(bf16[1,256,256]{2,1,0:T(8,128)(2,1)} %param.17) | copy-start | bytes 393220
  37.1 2.5 %collective-permute-start.2 = (bf16[2,256,256]{2,1,0:T(8,128)(2,1)S(1)}, bf16[2,256,256]{2,1,0:T(8,128)(2,1)S(1)}, u32[]{:S(2)}, u32[]{:S(2)}) collective-permute-start(bf16[2,256,256]{2,1,0:T(8,128)(2,1)S(1)} %get-tuple-element.61), channel_id=1, source_target_pairs={{0,256},{1,257},{2,258},{3,259},{4,260},{5,261},{6,262},{7,263},{8... | collective-permute-start | bytes 786440 | tf_op jit(solution)/shard_map/ppermute | solution.py:20
  39.7 5.9 %collective-permute-start.3 = (bf16[2,256,256]{2,1,0:T(8,128)(2,1)S(1)}, bf16[2,256,256]{2,1,0:T(8,128)(2,1)S(1)}, u32[]{:S(2)}, u32[]{:S(2)}) collective-permute-start(bf16[2,256,256]{2,1,0:T(8,128)(2,1)S(1)} %get-tuple-element.63), channel_id=1, source_target_pairs={{256,0},{257,1},{258,2},{259,3},{260,4},{261,5},{262,6},{263,7},{2... | collective-permute-start | bytes 786440 | tf_op jit(solution)/shard_map/ppermute | solution.py:20
  60.4 11.8 %collective-permute-start.4 = (bf16[2,2,40,256]{3,2,1,0:T(8,128)(2,1)S(1)}, bf16[2,2,40,256]{3,2,1,0:T(8,128)(2,1)S(1)}, u32[]{:S(2)}, u32[]{:S(2)}) collective-permute-start(bf16[2,2,40,256]{3,2,1,0:T(8,128)(2,1)S(1)} %get-tuple-element.67), channel_id=1, source_target_pairs={{0,4},{1,5},{2,6},{3,7},{4,8},{5,9},{6,10},{7,11},{8,12},{9,13},{1... | collective-permute-start | bytes 245768 | tf_op jit(solution)/shard_map/ppermute | solution.py:363
  64.0 11.0 %collective-permute-start.5 = (bf16[2,2,40,256]{3,2,1,0:T(8,128)(2,1)S(1)}, bf16[2,2,40,256]{3,2,1,0:T(8,128)(2,1)S(1)}, u32[]{:S(2)}, u32[]{:S(2)}) collective-permute-start(bf16[2,2,40,256]{3,2,1,0:T(8,128)(2,1)S(1)} %get-tuple-element.68), channel_id=1, source_target_pairs={{0,8},{1,9},{2,10},{3,11},{4,12},{5,13},{6,14},{7,15},{8,16},{9,17... | collective-permute-start | bytes 245768 | tf_op jit(solution)/shard_map/ppermute | solution.py:363

commit v12 on v11

--- a/solution.py
+++ b/solution.py
@@ -178,7 +178,7 @@
     return rounded(times_right_conj(*half_back, real, imag))
 
 
-def retreat_steps(back, patch_ref, incident_ref, mats, grad_ref):
+def retreat_steps(back, patch_ref, incident_ref, mats, grad_ref, keep_back=True):
     real, imag, real_t, imag_t = mats
     for slice_at in reversed(range(patch_ref.shape[0])):
         middle = rounded(times_left_adj(real_t, imag_t, *back))
@@ -187,6 +187,8 @@
         inc_imag = incident_ref[slice_at, 1].astype(jnp.float32)
         grad_ref[slice_at, 0] = (inc_real * bar_real + inc_imag * bar_imag).astype(grad_ref.dtype)
         grad_ref[slice_at, 1] = (inc_real * bar_imag - inc_imag * bar_real).astype(grad_ref.dtype)
+        if slice_at == 0 and not keep_back:
+            break
         pat_real = patch_ref[slice_at, 0].astype(jnp.float32)
         pat_imag = patch_ref[slice_at, 1].astype(jnp.float32)
         back = rounded(
@@ -223,6 +225,12 @@
     )
     out_ref[0] = back[0]
     out_ref[1] = back[1]
+
+
+def final_retreat_kernel(back_ref, patch_ref, incident_ref, mat_ref, grad_ref):
+    retreat_steps(
+        (back_ref[0], back_ref[1]), patch_ref, incident_ref, mats_of(mat_ref), grad_ref, False
+    )
 
 
 def planes_of(matrix):
@@ -332,7 +340,14 @@
         waves,
         gradients,
     )
-    for section_step in reversed(range(sections - 1)):
+    def final_retreat(back_in, incidents):
+        outs = jax.ShapeDtypeStruct(planes.shape, jnp.bfloat16)
+        flops = planes.shape[0] * 8 * dot_flops
+        return run_kernel(
+            final_retreat_kernel, outs, flops, back_in, planes, incidents, kernel_planes
+        )
+
+    for section_step in reversed(range(1, sections - 1)):
         adjoints = passed_along(adjoints, "section", -1)
         adjoints, gradients = lax.cond(
             section_now == section_step,
@@ -341,6 +356,14 @@
             adjoints,
             gradients,
         )
+    adjoints = passed_along(adjoints, "section", -1)
+    gradients = lax.cond(
+        section_now == 0,
+        lambda field_in, kept: final_retreat(field_in, stored),
+        lambda field_in, kept: kept,
+        adjoints,
+        gradients,
+    )
     gradients = gradients * live_slots[0].astype(jnp.float32)
     span = 2 * row_size * local_rows
     margin = span - width

time: 76.2 us -> 76.2 us (level)
  Pallas kernels: 3.03 us -> 2.25 us
    pallas_call x2, Pallas kernels: 3.03 us -> 2.25 us  [run_kernel(): pl.pallas_call(body, out_shape=outs, scratch_shapes=list(scratch), cost_e...]
    all_to_all x1, blocking collectives: 12 us -> 12.7 us  [on_device(): incoming = lax.all_to_all(outgoing, row_axis, 0, 0).astype(jnp.float32)]
where the time goes in v12:
time: 76.2 us; the launch traced here: 75.8 us
  starting transfers between devices  30.9 us (41%)
  waiting for transfers between devices  22.6 us (30%)
  blocking collectives  12.7 us (17%)
  other arithmetic  3.21 us (4%)
  local copies, waits for them, and re-layouts  2.44 us (3%)
  Pallas kernels  2.25 us (3%)
  between operations  1.67 us (2%)
    ppermute x2, starting transfers between devices, on_device(): lax.ppermute(slab, tile_axes, [(s, (s - ahead * row_size) % tile_count) f...  17.9 us
    all_to_all x1, blocking collectives, on_device(): incoming = lax.all_to_all(outgoing, row_axis, 0, 0).astype(jnp.float32)  12.7 us
    ppermute x2, waiting for transfers between devices, on_device(): lax.ppermute(spill.astype(jnp.bfloat16), tile_axes, [(s, (s + ahead * row...  9.12 us
    all_to_all x1, waiting for transfers between devices, on_device(): got = lax.all_to_all(sent, row_axis, 0, 0)  7.05 us
    ppermute x2, starting transfers between devices, on_device(): lax.ppermute(spill.astype(jnp.bfloat16), tile_axes, [(s, (s + ahead * row...  5.47 us
    all_to_all x1, starting transfers between devices, on_device(): got = lax.all_to_all(sent, row_axis, 0, 0)  4.96 us
    ppermute x2, waiting for transfers between devices, passed_along(): return lax.ppermute(shard, axis, pairs)  3.96 us
    ppermute x2, starting transfers between devices, passed_along(): return lax.ppermute(shard, axis, pairs)  2.6 us
  transfers between devices with their start and end apart: 7, of which 5 were waited for; matrix products, arithmetic and copies ran while one was open for 3% of the time, Pallas kernels for 0%

profile of v12, /device:TPU:2, one launch (start us, length us, event | category | flops | bytes accessed | tf_op | source)
XLA Modules:
  0.0 75.8 jit_solution(11416244146297348325)
XLA Ops:
  0.0 13.8 %collective-permute-start = (bf16[2,2,40,256]{3,1,2,0:T(2,128)(2,1)}, bf16[2,2,40,256]{3,1,2,0:T(2,128)(2,1)S(1)}, u32[]{:S(2)}, u32[]{:S(2)}) collective-permute-start(bf16[2,2,40,256]{3,1,2,0:T(2,128)(2,1)} %bitcast.74), channel_id=1, source_target_pairs={{0,252},{1,253},{2,254},{3,255},{4,0},{5,1},{6,2},{7,3},{8,4},{9,5... | collective-permute-start | bytes 245768 | tf_op jit(solution)/shard_map/ppermute | solution.py:268
  13.8 4.0 %collective-permute-start.1 = (bf16[2,2,40,256]{3,1,2,0:T(2,128)(2,1)}, bf16[2,2,40,256]{3,1,2,0:T(2,128)(2,1)S(1)}, u32[]{:S(2)}, u32[]{:S(2)}) collective-permute-start(bf16[2,2,40,256]{3,1,2,0:T(2,128)(2,1)} %bitcast.75), channel_id=1, source_target_pairs={{0,248},{1,249},{2,250},{3,251},{4,252},{5,253},{6,254},{7,255},{8... | collective-permute-start | bytes 245768 | tf_op jit(solution)/shard_map/ppermute | solution.py:268
  17.9 0.9 %copy.27 = bf16[2,2,40,256]{3,2,1,0:T(8,128)(2,1)S(1)} copy(bf16[2,2,40,256]{3,1,2,0:T(2,128)(2,1)} %bitcast.76) | data formatting | bytes 163840 | tf_op jit(solution)/shard_map/transpose | solution.py:266
  18.8 0.0 collective-permute-done
  18.9 2.4 %collective-permute-done.1 = bf16[2,2,40,256]{3,1,2,0:T(2,128)(2,1)S(1)} collective-permute-done((bf16[2,2,40,256]{3,1,2,0:T(2,128)(2,1)}, bf16[2,2,40,256]{3,1,2,0:T(2,128)(2,1)S(1)}, u32[]{:S(2)}, u32[]{:S(2)}) %collective-permute-start.1) | collective-permute-done | bytes 81952 | tf_op jit(solution)/shard_map/ppermute | solution.py:268
  21.3 0.1 broadcast_select_fusion.1
  21.4 0.0 copy-start
  21.4 0.9 %pad_maximum_fusion = bf16[4,2,2,2,40,256]{5,4,3,2,1,0:T(8,128)(2,1)} fusion(bf16[4,1,2,2,40,256]{5,4,3,2,1,0:T(8,128)(2,1)S(1)} %get-tuple-element.72, bf16[4,1,2,2,40,256]{5,4,3,2,1,0:T(8,128)(2,1)S(1)} %get-tuple-element.71), kind=kLoop, calls=%fused_computation.11 | loop fusion | flops 327680 | bytes 1310720 | tf_op jit(solution)/shard_map/stack | solution.py:276
  22.4 0.0 copy-start.1
  22.4 5.0 %all-to-all-start = ((bf16[4,2,2,2,40,256]{5,4,3,2,1,0:T(8,128)(2,1)}), bf16[4,2,2,2,40,256]{5,4,3,2,1,0:T(8,128)(2,1)S(1)}, u32[]{:S(2)}, u32[]{:S(2)}) async-start(bf16[4,2,2,2,40,256]{5,4,3,2,1,0:T(8,128)(2,1)} %pad_maximum_fusion), calls=%async_computation | async-start | bytes 1310720 | tf_op jit(solution)/shard_map/all_to_all | solution.py:279
  28.0 0.0 copy-done
  28.0 0.1 copy.41
  28.1 0.1 copy.42
  28.2 0.0 copy-done.1
  28.3 0.1 pad_maximum_fusion.1
  28.3 7.1 %all-to-all-done = bf16[4,2,2,2,40,256]{5,4,3,2,1,0:T(8,128)(2,1)S(1)} async-done(((bf16[4,2,2,2,40,256]{5,4,3,2,1,0:T(8,128)(2,1)}), bf16[4,2,2,2,40,256]{5,4,3,2,1,0:T(8,128)(2,1)S(1)}, u32[]{:S(2)}, u32[]{:S(2)}) %all-to-all-start) | async-done | bytes 655392 | tf_op jit(solution)/shard_map/all_to_all | solution.py:279
  35.4 0.2 fusion.2
  35.8 0.1 constant_dynamic-slice_fusion
  35.9 0.0 copy-start.2
  35.9 1.2 %conditional.3 = ((bf16[2,256,256]{2,1,0:T(8,128)(2,1)S(1)}, bf16[2,2,256,256]{3,2,1,0:T(8,128)(2,1)S(1)})) conditional(s32[]{:T(128)} %convert_element_type.65, bf16[2,256,256]{2,1,0:T(8,128)(2,1)S(1)} %bitcast.70, (bf16[2,256,256]{2,1,0:T(8,128)(2,1)S(1)}, bf16[2,2,256,256]{3,2,1,0:T(8,128)(2,1)S(1)}, bf16[4,256,256]{2,1,0:T(8,128)(2,1)S(1)}) %tuple.57), branch_computations={%region_0.1_spmd, %region_1.2_spmd} | conditional | flops 536870912 | bytes 2097160 | solution.py:328
  35.9 1.1 %branch_1_fun.3 = (bf16[2,256,256]{2,1,0:T(8,128)(2,1)S(1)}, bf16[2,2,256,256]{3,2,1,0:T(8,128)(2,1)S(1)}) custom-call(bf16[2,256,256]{2,1,0:T(8,128)(2,1)S(1)} %get-tuple-element.44.field_ref, bf16[2,2,256,256]{3,2,1,0:T(8,128)(2,1)S(1)} %get-tuple-element.45.patch_ref, bf16[4,256,256]{2,1,0:T(8,128)(2,1)S(1)} %get-tuple-element.46.mat_ref), custom_call_target="tpu_custom_call" | custom-call | flops 536870912 | bytes 2097152 | tf_op jit(solution)/shard_map/cond/branch_1_fun/pallas_call | solution.py:244
  37.1 1.3 %collective-permute-start.2 = (bf16[2,256,256]{2,1,0:T(8,128)(2,1)S(1)}, bf16[2,256,256]{2,1,0:T(8,128)(2,1)S(1)}, u32[]{:S(2)}, u32[]{:S(2)}) collective-permute-start(bf16[2,256,256]{2,1,0:T(8,128)(2,1)S(1)} %get-tuple-element.60), channel_id=1, source_target_pairs={{0,256},{1,257},{2,258},{3,259},{4,260},{5,261},{6,262},{7,263},{8... | collective-permute-start | bytes 786440 | tf_op jit(solution)/shard_map/ppermute | solution.py:20
  38.4 1.1 %multiply_convert_fusion = (bf16[1,256,256]{2,1,0:T(8,128)(2,1)S(1)}, bf16[1,256,256]{2,1,0:T(8,128)(2,1)S(1)}) fusion(), kind=kLoop, calls=%fused_computation.26 | loop fusion | flops 1245184 | bytes 262144 | tf_op jit(solution)/shard_map/convert.2
  39.5 0.0 collective-permute-done.2
  39.6 0.0 copy-done.2
  39.6 0.1 conditional.4
  39.7 1.3 %collective-permute-start.3 = (bf16[2,256,256]{2,1,0:T(8,128)(2,1)S(1)}, bf16[2,256,256]{2,1,0:T(8,128)(2,1)S(1)}, u32[]{:S(2)}, u32[]{:S(2)}) collective-permute-start(bf16[2,256,256]{2,1,0:T(8,128)(2,1)S(1)} %get-tuple-element.62), channel_id=1, source_target_pairs={{256,0},{257,1},{258,2},{259,3},{260,4},{261,5},{262,6},{263,7},{2... | collective-permute-start | bytes 786440 | tf_op jit(solution)/shard_map/ppermute | solution.py:20
  41.6 4.0 %collective-permute-done.3 = bf16[2,256,256]{2,1,0:T(8,128)(2,1)S(1)} collective-permute-done((bf16[2,256,256]{2,1,0:T(8,128)(2,1)S(1)}, bf16[2,256,256]{2,1,0:T(8,128)(2,1)S(1)}, u32[]{:S(2)}, u32[]{:S(2)}) %collective-permute-start.3) | collective-permute-done | bytes 262176 | tf_op jit(solution)/shard_map/ppermute | solution.py:20
  45.6 1.1 %conditional.5 = (bf16[2,2,256,256]{3,2,1,0:T(8,128)(2,1)S(1)}) conditional(s32[]{:T(128)} %convert_element_type.65, bf16[2,2,256,256]{3,2,1,0:T(8,128)(2,1)S(1)} %get-tuple-element.61, (bf16[2,256,256]{2,1,0:T(8,128)(2,1)S(1)}, bf16[2,2,256,256]{3,2,1,0:T(8,128)(2,1)S(1)}, bf16[2,2,256,256]{3,2,1,0:T(8,128)(2,1)S(1)}, ...), branch_computations={%region_4.5_spmd, %region_5.6_spmd} | conditional | flops 536870912 | bytes 2359304 | solution.py:360
  45.6 1.1 %branch_1_fun.5 = bf16[2,2,256,256]{3,2,1,0:T(8,128)(2,1)S(1)} custom-call(bf16[2,256,256]{2,1,0:T(8,128)(2,1)S(1)} %get-tuple-element.52.back_ref, bf16[2,2,256,256]{3,2,1,0:T(8,128)(2,1)S(1)} %get-tuple-element.53.patch_ref, bf16[2,2,256,256]{3,2,1,0:T(8,128)(2,1)S(1)} %get-tuple-element.54.incident_ref, bf16[4,256,256]{2,1,0:T(8,128)(2,1)S(1)} %get-tuple-element.55.mat_ref), custom_call_target="tpu_custom_call" | custom-call | flops 536870912 | bytes 2359296 | tf_op jit(solution)/shard_map/cond/branch_1_fun/pallas_call | solution.py:244
  46.7 0.1 convert_multiply_fusion
  46.8 0.2 fusion
  47.0 0.3 fusion.1
  47.3 12.7 %all_to_all.10 = bf16[4,2,2,2,40,256]{5,4,1,3,2,0:T(8,128)(2,1)S(1)} all-to-all(bf16[4,2,2,2,40,256]{5,4,1,3,2,0:T(8,128)(2,1)S(1)} %copy.32), channel_id=1, replica_groups=mesh['section'=2,'lines'=64,'x'=4] {'x'}, dimensions={0} | all-to-all | bytes 1310720 | tf_op jit(solution)/shard_map/all_to_all | solution.py:376
  60.1 0.2 convert_element_type.74
  60.2 0.2 select_reduce_fusion.1
  60.4 3.5 %collective-permute-start.4 = (bf16[2,2,40,256]{3,2,1,0:T(8,128)(2,1)S(1)}, bf16[2,2,40,256]{3,2,1,0:T(8,128)(2,1)S(1)}, u32[]{:S(2)}, u32[]{:S(2)}) collective-permute-start(bf16[2,2,40,256]{3,2,1,0:T(8,128)(2,1)S(1)} %get-tuple-element.66), channel_id=1, source_target_pairs={{0,4},{1,5},{2,6},{3,7},{4,8},{5,9},{6,10},{7,11},{8,12},{9,13},{1... | collective-permute-start | bytes 245768 | tf_op jit(solution)/shard_map/ppermute | solution.py:386
  64.0 1.9 %collective-permute-start.5 = (bf16[2,2,40,256]{3,2,1,0:T(8,128)(2,1)S(1)}, bf16[2,2,40,256]{3,2,1,0:T(8,128)(2,1)S(1)}, u32[]{:S(2)}, u32[]{:S(2)}) collective-permute-start(bf16[2,2,40,256]{3,2,1,0:T(8,128)(2,1)S(1)} %get-tuple-element.67), channel_id=1, source_target_pairs={{0,8},{1,9},{2,10},{3,11},{4,12},{5,13},{6,14},{7,15},{8,16},{9,17... | collective-permute-start | bytes 245768 | tf_op jit(solution)/shard_map/ppermute | solution.py:386
  65.9 6.7 %collective-permute-done.4 = bf16[2,2,40,256]{3,2,1,0:T(8,128)(2,1)S(1)} collective-permute-done((bf16[2,2,40,256]{3,2,1,0:T(8,128)(2,1)S(1)}, bf16[2,2,40,256]{3,2,1,0:T(8,128)(2,1)S(1)}, u32[]{:S(2)}, u32[]{:S(2)}) %collective-permute-start.4) | collective-permute-done | bytes 81952 | tf_op jit(solution)/shard_map/ppermute | solution.py:386
  72.6 2.5 %collective-permute-done.5 = bf16[2,2,40,256]{3,2,1,0:T(8,128)(2,1)S(1)} collective-permute-done((bf16[2,2,40,256]{3,2,1,0:T(8,128)(2,1)S(1)}, bf16[2,2,40,256]{3,2,1,0:T(8,128)(2,1)S(1)}, u32[]{:S(2)}, u32[]{:S(2)}) %collective-permute-start.5) | collective-permute-done | bytes 81952 | tf_op jit(solution)/shard_map/ppermute | solution.py:386
  75.1 0.8 copy.37
  (18 shorter events, 0.3 us)
Async XLA Ops:
  0.0 18.8 %collective-permute-start = (bf16[2,2,40,256]{3,1,2,0:T(2,128)(2,1)}, bf16[2,2,40,256]{3,1,2,0:T(2,128)(2,1)S(1)}, u32[]{:S(2)}, u32[]{:S(2)}) collective-permute-start(bf16[2,2,40,256]{3,1,2,0:T(2,128)(2,1)} %bitcast.74), channel_id=1, source_target_pairs={{0,252},{1,253},{2,254},{3,255},{4,0},{5,1},{6,2},{7,3},{8,4},{9,5... | collective-permute-start | bytes 245768 | tf_op jit(solution)/shard_map/ppermute | solution.py:268
  13.8 7.4 %collective-permute-start.1 = (bf16[2,2,40,256]{3,1,2,0:T(2,128)(2,1)}, bf16[2,2,40,256]{3,1,2,0:T(2,128)(2,1)S(1)}, u32[]{:S(2)}, u32[]{:S(2)}) collective-permute-start(bf16[2,2,40,256]{3,1,2,0:T(2,128)(2,1)} %bitcast.75), channel_id=1, source_target_pairs={{0,248},{1,249},{2,250},{3,251},{4,252},{5,253},{6,254},{7,255},{8... | collective-permute-start | bytes 245768 | tf_op jit(solution)/shard_map/ppermute | solution.py:268
  21.4 6.5 %copy-start = (bf16[2,256,256]{2,1,0:T(8,128)(2,1)S(1)}, bf16[2,256,256]{2,1,0:T(8,128)(2,1)}, u32[]{:S(2)}) copy-start(bf16[2,256,256]{2,1,0:T(8,128)(2,1)} %param.13) | copy-start | bytes 786436
  22.4 5.9 %copy-start.1 = (bf16[256,2,256]{2,1,0:T(2,128)(2,1)S(1)}, bf16[256,2,256]{2,1,0:T(2,128)(2,1)}, u32[]{:S(2)}) copy-start(bf16[256,2,256]{2,1,0:T(2,128)(2,1)} %param.12) | copy-start | bytes 786436
  22.4 13.0 %all-to-all-start = ((bf16[4,2,2,2,40,256]{5,4,3,2,1,0:T(8,128)(2,1)}), bf16[4,2,2,2,40,256]{5,4,3,2,1,0:T(8,128)(2,1)S(1)}, u32[]{:S(2)}, u32[]{:S(2)}) async-start(bf16[4,2,2,2,40,256]{5,4,3,2,1,0:T(8,128)(2,1)} %pad_maximum_fusion), calls=%async_computation | async-start | bytes 1310720 | tf_op jit(solution)/shard_map/all_to_all | solution.py:279
  35.9 3.6 %copy-start.2 = (bf16[1,256,256]{2,1,0:T(8,128)(2,1)S(1)}, bf16[1,256,256]{2,1,0:T(8,128)(2,1)}, u32[]{:S(2)}) copy-start(bf16[1,256,256]{2,1,0:T(8,128)(2,1)} %param.17) | copy-start | bytes 393220
  37.1 2.5 %collective-permute-start.2 = (bf16[2,256,256]{2,1,0:T(8,128)(2,1)S(1)}, bf16[2,256,256]{2,1,0:T(8,128)(2,1)S(1)}, u32[]{:S(2)}, u32[]{:S(2)}) collective-permute-start(bf16[2,256,256]{2,1,0:T(8,128)(2,1)S(1)} %get-tuple-element.60), channel_id=1, source_target_pairs={{0,256},{1,257},{2,258},{3,259},{4,260},{5,261},{6,262},{7,263},{8... | collective-permute-start | bytes 786440 | tf_op jit(solution)/shard_map/ppermute | solution.py:20
  39.7 5.9 %collective-permute-start.3 = (bf16[2,256,256]{2,1,0:T(8,128)(2,1)S(1)}, bf16[2,256,256]{2,1,0:T(8,128)(2,1)S(1)}, u32[]{:S(2)}, u32[]{:S(2)}) collective-permute-start(bf16[2,256,256]{2,1,0:T(8,128)(2,1)S(1)} %get-tuple-element.62), channel_id=1, source_target_pairs={{256,0},{257,1},{258,2},{259,3},{260,4},{261,5},{262,6},{263,7},{2... | collective-permute-start | bytes 786440 | tf_op jit(solution)/shard_map/ppermute | solution.py:20
  60.4 12.1 %collective-permute-start.4 = (bf16[2,2,40,256]{3,2,1,0:T(8,128)(2,1)S(1)}, bf16[2,2,40,256]{3,2,1,0:T(8,128)(2,1)S(1)}, u32[]{:S(2)}, u32[]{:S(2)}) collective-permute-start(bf16[2,2,40,256]{3,2,1,0:T(8,128)(2,1)S(1)} %get-tuple-element.66), channel_id=1, source_target_pairs={{0,4},{1,5},{2,6},{3,7},{4,8},{5,9},{6,10},{7,11},{8,12},{9,13},{1... | collective-permute-start | bytes 245768 | tf_op jit(solution)/shard_map/ppermute | solution.py:386
  64.0 11.0 %collective-permute-start.5 = (bf16[2,2,40,256]{3,2,1,0:T(8,128)(2,1)S(1)}, bf16[2,2,40,256]{3,2,1,0:T(8,128)(2,1)S(1)}, u32[]{:S(2)}, u32[]{:S(2)}) collective-permute-start(bf16[2,2,40,256]{3,2,1,0:T(8,128)(2,1)S(1)} %get-tuple-element.67), channel_id=1, source_target_pairs={{0,8},{1,9},{2,10},{3,11},{4,12},{5,13},{6,14},{7,15},{8,16},{9,17... | collective-permute-start | bytes 245768 | tf_op jit(solution)/shard_map/ppermute | solution.py:386

commit v13 on v12

--- a/solution.py
+++ b/solution.py
@@ -147,12 +147,13 @@
     return (pair[0].astype(jnp.bfloat16), pair[1].astype(jnp.bfloat16))
 
 
-def march_steps(field, patch_ref, mats, incident_ref):
+def march_steps(field, patch_ref, mats, incident_ref, skip=0):
     real, imag, real_t, imag_t = mats
     field_real, field_imag = field
     for slice_at in range(patch_ref.shape[0]):
-        incident_ref[slice_at, 0] = field_real
-        incident_ref[slice_at, 1] = field_imag
+        if slice_at >= skip:
+            incident_ref[slice_at - skip, 0] = field_real
+            incident_ref[slice_at - skip, 1] = field_imag
         first_real = field_real.astype(jnp.float32)
         first_imag = field_imag.astype(jnp.float32)
         second_real = patch_ref[slice_at, 0].astype(jnp.float32)
@@ -178,13 +179,20 @@
     return rounded(times_right_conj(*half_back, real, imag))
 
 
-def retreat_steps(back, patch_ref, incident_ref, mats, grad_ref, keep_back=True):
+def retreat_steps(back, patch_ref, incident_ref, mats, grad_ref, keep_back=True, first=None):
     real, imag, real_t, imag_t = mats
     for slice_at in reversed(range(patch_ref.shape[0])):
         middle = rounded(times_left_adj(real_t, imag_t, *back))
         bar_real, bar_imag = times_right_conj(*middle, real, imag)
-        inc_real = incident_ref[slice_at, 0].astype(jnp.float32)
-        inc_imag = incident_ref[slice_at, 1].astype(jnp.float32)
+        if first is None:
+            inc_real = incident_ref[slice_at, 0].astype(jnp.float32)
+            inc_imag = incident_ref[slice_at, 1].astype(jnp.float32)
+        elif slice_at == 0:
+            inc_real = first[0].astype(jnp.float32)
+            inc_imag = first[1].astype(jnp.float32)
+        else:
+            inc_real = incident_ref[slice_at - 1, 0].astype(jnp.float32)
+            inc_imag = incident_ref[slice_at - 1, 1].astype(jnp.float32)
         grad_ref[slice_at, 0] = (inc_real * bar_real + inc_imag * bar_imag).astype(grad_ref.dtype)
         grad_ref[slice_at, 1] = (inc_real * bar_imag - inc_imag * bar_real).astype(grad_ref.dtype)
         if slice_at == 0 and not keep_back:
@@ -202,7 +210,9 @@
 
 
 def march_kernel(field_ref, patch_ref, mat_ref, out_ref, incident_ref):
-    field = march_steps((field_ref[0], field_ref[1]), patch_ref, mats_of(mat_ref), incident_ref)
+    field = march_steps(
+        (field_ref[0], field_ref[1]), patch_ref, mats_of(mat_ref), incident_ref, skip=1
+    )
     out_ref[0] = field[0]
     out_ref[1] = field[1]
 
@@ -219,17 +229,19 @@
     out_ref[1] = back[1]
 
 
-def retreat_kernel(back_ref, patch_ref, incident_ref, mat_ref, out_ref, grad_ref):
+def retreat_kernel(back_ref, patch_ref, incident_ref, first_ref, mat_ref, out_ref, grad_ref):
+    first = (first_ref[0], first_ref[1])
     back = retreat_steps(
-        (back_ref[0], back_ref[1]), patch_ref, incident_ref, mats_of(mat_ref), grad_ref
+        (back_ref[0], back_ref[1]), patch_ref, incident_ref, mats_of(mat_ref), grad_ref, True, first
     )
     out_ref[0] = back[0]
     out_ref[1] = back[1]
 
 
-def final_retreat_kernel(back_ref, patch_ref, incident_ref, mat_ref, grad_ref):
+def final_retreat_kernel(back_ref, patch_ref, incident_ref, first_ref, mat_ref, grad_ref):
+    first = (first_ref[0], first_ref[1])
     retreat_steps(
-        (back_ref[0], back_ref[1]), patch_ref, incident_ref, mats_of(mat_ref), grad_ref, False
+        (back_ref[0], back_ref[1]), patch_ref, incident_ref, mats_of(mat_ref), grad_ref, False, first
     )
 
 
@@ -290,16 +302,20 @@
     field_shape = jax.ShapeDtypeStruct((2, width, width), jnp.bfloat16)
     dot_flops = 2 * width**3
 
+    kept_shape = (planes.shape[0] - 1,) + planes.shape[1:]
+
     def march(field_in):
-        outs = (field_shape, jax.ShapeDtypeStruct(planes.shape, jnp.bfloat16))
+        outs = (field_shape, jax.ShapeDtypeStruct(kept_shape, jnp.bfloat16))
         flops = slice_count * 8 * dot_flops
         return tuple(run_kernel(march_kernel, outs, flops, field_in, planes, kernel_planes))
 
-    def retreat(back_in, incidents):
+    def retreat(back_in, incidents, first):
         outs = (field_shape, jax.ShapeDtypeStruct(planes.shape, jnp.bfloat16))
         flops = slice_count * 8 * dot_flops
         return tuple(
-            run_kernel(retreat_kernel, outs, flops, back_in, planes, incidents, kernel_planes)
+            run_kernel(
+                retreat_kernel, outs, flops, back_in, planes, incidents, first, kernel_planes
+            )
         )
 
     def whole(field_in):
@@ -319,18 +335,20 @@
         )
         return (back, grads)
 
-    stored = jnp.zeros(planes.shape, jnp.bfloat16)
+    stored = jnp.zeros(kept_shape, jnp.bfloat16)
     gradients = jnp.zeros(planes.shape, jnp.bfloat16)
     waves = jnp.transpose(probe, (1, 0, 2))
+    entering = waves
     for section_step in range(sections - 1):
         if section_step > 0:
             waves = passed_along(waves, "section", 1)
-        waves, stored = lax.cond(
+        waves, stored, entering = lax.cond(
             section_now == section_step,
-            lambda field_in, kept: march(field_in),
-            lambda field_in, kept: (field_in, kept),
+            lambda field_in, kept, first: march(field_in) + (field_in,),
+            lambda field_in, kept, first: (field_in, kept, first),
             waves,
             stored,
+            entering,
         )
     waves = passed_along(waves, "section", 1)
     adjoints, gradients = lax.cond(
@@ -340,18 +358,18 @@
         waves,
         gradients,
     )
-    def final_retreat(back_in, incidents):
+    def final_retreat(back_in, incidents, first):
         outs = jax.ShapeDtypeStruct(planes.shape, jnp.bfloat16)
         flops = planes.shape[0] * 8 * dot_flops
         return run_kernel(
-            final_retreat_kernel, outs, flops, back_in, planes, incidents, kernel_planes
+            final_retreat_kernel, outs, flops, back_in, planes, incidents, first, kernel_planes
         )
 
     for section_step in reversed(range(1, sections - 1)):
         adjoints = passed_along(adjoints, "section", -1)
         adjoints, gradients = lax.cond(
             section_now == section_step,
-            lambda field_in, kept: retreat(field_in, stored),
+            lambda field_in, kept: retreat(field_in, stored, entering),
             lambda field_in, kept: (field_in, kept),
             adjoints,
             gradients,
@@ -359,7 +377,7 @@
     adjoints = passed_along(adjoints, "section", -1)
     gradients = lax.cond(
         section_now == 0,
-        lambda field_in, kept: final_retreat(field_in, stored),
+        lambda field_in, kept: final_retreat(field_in, stored, entering),
         lambda field_in, kept: kept,
         adjoints,
         gradients,

time: 76.2 us -> 76.2 us (level)
  no operation moved by 1% of the time
where the time goes in v13:
time: 76.2 us; the launch traced here: 75.8 us
  starting transfers between devices  30.9 us (41%)
  waiting for transfers between devices  22.6 us (30%)
  blocking collectives  12.7 us (17%)
  other arithmetic  3.21 us (4%)
  local copies, waits for them, and re-layouts  2.44 us (3%)
  Pallas kernels  2.22 us (3%)
  between operations  1.67 us (2%)
    ppermute x2, starting transfers between devices, on_device(): lax.ppermute(slab, tile_axes, [(s, (s - ahead * row_size) % tile_count) f...  17.9 us
    all_to_all x1, blocking collectives, on_device(): incoming = lax.all_to_all(outgoing, row_axis, 0, 0).astype(jnp.float32)  12.7 us
    ppermute x2, waiting for transfers between devices, on_device(): lax.ppermute(spill.astype(jnp.bfloat16), tile_axes, [(s, (s + ahead * row...  9.13 us
    all_to_all x1, waiting for transfers between devices, on_device(): got = lax.all_to_all(sent, row_axis, 0, 0)  7.05 us
    ppermute x2, starting transfers between devices, on_device(): lax.ppermute(spill.astype(jnp.bfloat16), tile_axes, [(s, (s + ahead * row...  5.46 us
    all_to_all x1, starting transfers between devices, on_device(): got = lax.all_to_all(sent, row_axis, 0, 0)  4.96 us
    ppermute x2, waiting for transfers between devices, passed_along(): return lax.ppermute(shard, axis, pairs)  3.96 us
    ppermute x2, starting transfers between devices, passed_along(): return lax.ppermute(shard, axis, pairs)  2.6 us
  transfers between devices with their start and end apart: 7, of which 5 were waited for; matrix products, arithmetic and copies ran while one was open for 3% of the time, Pallas kernels for 0%

profile of v13, /device:TPU:2, one launch (start us, length us, event | category | flops | bytes accessed | tf_op | source)
XLA Modules:
  0.0 75.8 jit_solution(12171003455312561746)
XLA Ops:
  0.0 13.8 %collective-permute-start = (bf16[2,2,40,256]{3,1,2,0:T(2,128)(2,1)}, bf16[2,2,40,256]{3,1,2,0:T(2,128)(2,1)S(1)}, u32[]{:S(2)}, u32[]{:S(2)}) collective-permute-start(bf16[2,2,40,256]{3,1,2,0:T(2,128)(2,1)} %bitcast.74), channel_id=1, source_target_pairs={{0,252},{1,253},{2,254},{3,255},{4,0},{5,1},{6,2},{7,3},{8,4},{9,5... | collective-permute-start | bytes 245768 | tf_op jit(solution)/shard_map/ppermute | solution.py:280
  13.8 4.0 %collective-permute-start.1 = (bf16[2,2,40,256]{3,1,2,0:T(2,128)(2,1)}, bf16[2,2,40,256]{3,1,2,0:T(2,128)(2,1)S(1)}, u32[]{:S(2)}, u32[]{:S(2)}) collective-permute-start(bf16[2,2,40,256]{3,1,2,0:T(2,128)(2,1)} %bitcast.75), channel_id=1, source_target_pairs={{0,248},{1,249},{2,250},{3,251},{4,252},{5,253},{6,254},{7,255},{8... | collective-permute-start | bytes 245768 | tf_op jit(solution)/shard_map/ppermute | solution.py:280
  17.9 0.9 %copy.27 = bf16[2,2,40,256]{3,2,1,0:T(8,128)(2,1)S(1)} copy(bf16[2,2,40,256]{3,1,2,0:T(2,128)(2,1)} %bitcast.76) | data formatting | bytes 163840 | tf_op jit(solution)/shard_map/transpose | solution.py:278
  18.8 0.0 collective-permute-done
  18.9 2.4 %collective-permute-done.1 = bf16[2,2,40,256]{3,1,2,0:T(2,128)(2,1)S(1)} collective-permute-done((bf16[2,2,40,256]{3,1,2,0:T(2,128)(2,1)}, bf16[2,2,40,256]{3,1,2,0:T(2,128)(2,1)S(1)}, u32[]{:S(2)}, u32[]{:S(2)}) %collective-permute-start.1) | collective-permute-done | bytes 81952 | tf_op jit(solution)/shard_map/ppermute | solution.py:280
  21.3 0.1 broadcast_select_fusion.1
  21.4 0.0 copy-start
  21.4 0.9 %pad_maximum_fusion = bf16[4,2,2,2,40,256]{5,4,3,2,1,0:T(8,128)(2,1)} fusion(bf16[4,1,2,2,40,256]{5,4,3,2,1,0:T(8,128)(2,1)S(1)} %get-tuple-element.79, bf16[4,1,2,2,40,256]{5,4,3,2,1,0:T(8,128)(2,1)S(1)} %get-tuple-element.78), kind=kLoop, calls=%fused_computation.11 | loop fusion | flops 327680 | bytes 1310720 | tf_op jit(solution)/shard_map/stack | solution.py:288
  22.4 0.0 copy-start.1
  22.4 5.0 %all-to-all-start = ((bf16[4,2,2,2,40,256]{5,4,3,2,1,0:T(8,128)(2,1)}), bf16[4,2,2,2,40,256]{5,4,3,2,1,0:T(8,128)(2,1)S(1)}, u32[]{:S(2)}, u32[]{:S(2)}) async-start(bf16[4,2,2,2,40,256]{5,4,3,2,1,0:T(8,128)(2,1)} %pad_maximum_fusion), calls=%async_computation | async-start | bytes 1310720 | tf_op jit(solution)/shard_map/all_to_all | solution.py:291
  28.0 0.0 copy-done
  28.0 0.1 copy.41
  28.1 0.1 copy.42
  28.2 0.0 copy-done.1
  28.3 0.1 pad_maximum_fusion.1
  28.3 7.1 %all-to-all-done = bf16[4,2,2,2,40,256]{5,4,3,2,1,0:T(8,128)(2,1)S(1)} async-done(((bf16[4,2,2,2,40,256]{5,4,3,2,1,0:T(8,128)(2,1)}), bf16[4,2,2,2,40,256]{5,4,3,2,1,0:T(8,128)(2,1)S(1)}, u32[]{:S(2)}, u32[]{:S(2)}) %all-to-all-start) | async-done | bytes 655392 | tf_op jit(solution)/shard_map/all_to_all | solution.py:291
  35.4 0.2 fusion.2
  35.8 0.1 constant_dynamic-slice_fusion
  35.9 0.0 copy-start.2
  35.9 1.1 %conditional.3 = (bf16[2,256,256]{2,1,0:T(8,128)(2,1)S(1)}, bf16[1,2,256,256]{3,2,1,0:T(8,128)(2,1)S(1)}, bf16[2,256,256]{2,1,0:T(8,128)(2,1)S(1)}) conditional(s32[]{:T(128)} %convert_element_type.65, bf16[2,256,256]{2,1,0:T(8,128)(2,1)S(1)} %bitcast.70, (bf16[2,256,256]{2,1,0:T(8,128)(2,1)S(1)}, bf16[2,2,256,256]{3,2,1,0:T(8,128)(2,1)S(1)}, ...), branch_computations={%region_0.1_spmd, %region_1.2_spmd} | conditional | flops 536870912 | bytes 1835032 | solution.py:345
  35.9 1.1 %branch_1_fun.3 = (bf16[2,256,256]{2,1,0:T(8,128)(2,1)S(1)}, bf16[1,2,256,256]{3,2,1,0:T(8,128)(2,1)S(1)}) custom-call(bf16[2,256,256]{2,1,0:T(8,128)(2,1)S(1)} %get-tuple-element.87.field_ref, bf16[2,2,256,256]{3,2,1,0:T(8,128)(2,1)S(1)} %get-tuple-element.47.patch_ref, bf16[4,256,256]{2,1,0:T(8,128)(2,1)S(1)} %get-tuple-element.48.mat_ref), custom_call_target="tpu_custom_call" | custom-call | flops 536870912 | bytes 1835008 | tf_op jit(solution)/shard_map/cond/branch_1_fun/pallas_call | solution.py:256
  37.1 1.3 %collective-permute-start.2 = (bf16[2,256,256]{2,1,0:T(8,128)(2,1)S(1)}, bf16[2,256,256]{2,1,0:T(8,128)(2,1)S(1)}, u32[]{:S(2)}, u32[]{:S(2)}) collective-permute-start(bf16[2,256,256]{2,1,0:T(8,128)(2,1)S(1)} %get-tuple-element.66), channel_id=1, source_target_pairs={{0,256},{1,257},{2,258},{3,259},{4,260},{5,261},{6,262},{7,263},{8... | collective-permute-start | bytes 786440 | tf_op jit(solution)/shard_map/ppermute | solution.py:20
  38.4 1.1 %multiply_convert_fusion = (bf16[1,256,256]{2,1,0:T(8,128)(2,1)S(1)}, bf16[1,256,256]{2,1,0:T(8,128)(2,1)S(1)}) fusion(), kind=kLoop, calls=%fused_computation.26 | loop fusion | flops 1245184 | bytes 262144 | tf_op jit(solution)/shard_map/convert.2
  39.5 0.0 collective-permute-done.2
  39.5 0.0 copy-done.2
  39.5 0.1 conditional.4
  39.6 1.3 %collective-permute-start.3 = (bf16[2,256,256]{2,1,0:T(8,128)(2,1)S(1)}, bf16[2,256,256]{2,1,0:T(8,128)(2,1)S(1)}, u32[]{:S(2)}, u32[]{:S(2)}) collective-permute-start(bf16[2,256,256]{2,1,0:T(8,128)(2,1)S(1)} %get-tuple-element.68), channel_id=1, source_target_pairs={{256,0},{257,1},{258,2},{259,3},{260,4},{261,5},{262,6},{263,7},{2... | collective-permute-start | bytes 786440 | tf_op jit(solution)/shard_map/ppermute | solution.py:20
  41.6 4.0 %collective-permute-done.3 = bf16[2,256,256]{2,1,0:T(8,128)(2,1)S(1)} collective-permute-done((bf16[2,256,256]{2,1,0:T(8,128)(2,1)S(1)}, bf16[2,256,256]{2,1,0:T(8,128)(2,1)S(1)}, u32[]{:S(2)}, u32[]{:S(2)}) %collective-permute-start.3) | collective-permute-done | bytes 262176 | tf_op jit(solution)/shard_map/ppermute | solution.py:20
  45.6 1.1 %conditional.5 = (bf16[2,2,256,256]{3,2,1,0:T(8,128)(2,1)S(1)}) conditional(s32[]{:T(128)} %convert_element_type.65, bf16[2,2,256,256]{3,2,1,0:T(8,128)(2,1)S(1)} %get-tuple-element.67, (bf16[2,256,256]{2,1,0:T(8,128)(2,1)S(1)}, bf16[2,2,256,256]{3,2,1,0:T(8,128)(2,1)S(1)}, bf16[1,2,256,256]{3,2,1,0:T(8,128)(2,1)S(1)}, ...), branch_computations={%region_4.5_spmd, %region_5.6_spmd} | conditional | flops 536870912 | bytes 2359304 | solution.py:378
  45.6 1.1 %branch_1_fun.5 = bf16[2,2,256,256]{3,2,1,0:T(8,128)(2,1)S(1)} custom-call(bf16[2,256,256]{2,1,0:T(8,128)(2,1)S(1)} %get-tuple-element.56.back_ref, bf16[2,2,256,256]{3,2,1,0:T(8,128)(2,1)S(1)} %get-tuple-element.57.patch_ref, bf16[1,2,256,256]{3,2,1,0:T(8,128)(2,1)S(1)} %get-tuple-element.58.incident_ref, ...), custom_call_target="tpu_custom_call" | custom-call | flops 536870912 | bytes 2359296 | tf_op jit(solution)/shard_map/cond/branch_1_fun/pallas_call | solution.py:256
  46.7 0.1 convert_multiply_fusion
  46.8 0.2 fusion
  47.0 0.3 fusion.1
  47.3 12.7 %all_to_all.10 = bf16[4,2,2,2,40,256]{5,4,1,3,2,0:T(8,128)(2,1)S(1)} all-to-all(bf16[4,2,2,2,40,256]{5,4,1,3,2,0:T(8,128)(2,1)S(1)} %copy.32), channel_id=1, replica_groups=mesh['section'=2,'lines'=64,'x'=4] {'x'}, dimensions={0} | all-to-all | bytes 1310720 | tf_op jit(solution)/shard_map/all_to_all | solution.py:394
  60.1 0.2 convert_element_type.74
  60.2 0.2 select_reduce_fusion.1
  60.4 3.5 %collective-permute-start.4 = (bf16[2,2,40,256]{3,2,1,0:T(8,128)(2,1)S(1)}, bf16[2,2,40,256]{3,2,1,0:T(8,128)(2,1)S(1)}, u32[]{:S(2)}, u32[]{:S(2)}) collective-permute-start(bf16[2,2,40,256]{3,2,1,0:T(8,128)(2,1)S(1)} %get-tuple-element.73), channel_id=1, source_target_pairs={{0,4},{1,5},{2,6},{3,7},{4,8},{5,9},{6,10},{7,11},{8,12},{9,13},{1... | collective-permute-start | bytes 245768 | tf_op jit(solution)/shard_map/ppermute | solution.py:404
  64.0 1.9 %collective-permute-start.5 = (bf16[2,2,40,256]{3,2,1,0:T(8,128)(2,1)S(1)}, bf16[2,2,40,256]{3,2,1,0:T(8,128)(2,1)S(1)}, u32[]{:S(2)}, u32[]{:S(2)}) collective-permute-start(bf16[2,2,40,256]{3,2,1,0:T(8,128)(2,1)S(1)} %get-tuple-element.74), channel_id=1, source_target_pairs={{0,8},{1,9},{2,10},{3,11},{4,12},{5,13},{6,14},{7,15},{8,16},{9,17... | collective-permute-start | bytes 245768 | tf_op jit(solution)/shard_map/ppermute | solution.py:404
  65.9 6.7 %collective-permute-done.4 = bf16[2,2,40,256]{3,2,1,0:T(8,128)(2,1)S(1)} collective-permute-done((bf16[2,2,40,256]{3,2,1,0:T(8,128)(2,1)S(1)}, bf16[2,2,40,256]{3,2,1,0:T(8,128)(2,1)S(1)}, u32[]{:S(2)}, u32[]{:S(2)}) %collective-permute-start.4) | collective-permute-done | bytes 81952 | tf_op jit(solution)/shard_map/ppermute | solution.py:404
  72.6 2.5 %collective-permute-done.5 = bf16[2,2,40,256]{3,2,1,0:T(8,128)(2,1)S(1)} collective-permute-done((bf16[2,2,40,256]{3,2,1,0:T(8,128)(2,1)S(1)}, bf16[2,2,40,256]{3,2,1,0:T(8,128)(2,1)S(1)}, u32[]{:S(2)}, u32[]{:S(2)}) %collective-permute-start.5) | collective-permute-done | bytes 81952 | tf_op jit(solution)/shard_map/ppermute | solution.py:404
  75.1 0.8 copy.37
  (18 shorter events, 0.3 us)
Async XLA Ops:
  0.0 18.8 %collective-permute-start = (bf16[2,2,40,256]{3,1,2,0:T(2,128)(2,1)}, bf16[2,2,40,256]{3,1,2,0:T(2,128)(2,1)S(1)}, u32[]{:S(2)}, u32[]{:S(2)}) collective-permute-start(bf16[2,2,40,256]{3,1,2,0:T(2,128)(2,1)} %bitcast.74), channel_id=1, source_target_pairs={{0,252},{1,253},{2,254},{3,255},{4,0},{5,1},{6,2},{7,3},{8,4},{9,5... | collective-permute-start | bytes 245768 | tf_op jit(solution)/shard_map/ppermute | solution.py:280
  13.8 7.4 %collective-permute-start.1 = (bf16[2,2,40,256]{3,1,2,0:T(2,128)(2,1)}, bf16[2,2,40,256]{3,1,2,0:T(2,128)(2,1)S(1)}, u32[]{:S(2)}, u32[]{:S(2)}) collective-permute-start(bf16[2,2,40,256]{3,1,2,0:T(2,128)(2,1)} %bitcast.75), channel_id=1, source_target_pairs={{0,248},{1,249},{2,250},{3,251},{4,252},{5,253},{6,254},{7,255},{8... | collective-permute-start | bytes 245768 | tf_op jit(solution)/shard_map/ppermute | solution.py:280
  21.4 6.5 %copy-start = (bf16[2,256,256]{2,1,0:T(8,128)(2,1)S(1)}, bf16[2,256,256]{2,1,0:T(8,128)(2,1)}, u32[]{:S(2)}) copy-start(bf16[2,256,256]{2,1,0:T(8,128)(2,1)} %param.13) | copy-start | bytes 786436
  22.4 5.9 %copy-start.1 = (bf16[256,2,256]{2,1,0:T(2,128)(2,1)S(1)}, bf16[256,2,256]{2,1,0:T(2,128)(2,1)}, u32[]{:S(2)}) copy-start(bf16[256,2,256]{2,1,0:T(2,128)(2,1)} %param.12) | copy-start | bytes 786436
  22.4 13.0 %all-to-all-start = ((bf16[4,2,2,2,40,256]{5,4,3,2,1,0:T(8,128)(2,1)}), bf16[4,2,2,2,40,256]{5,4,3,2,1,0:T(8,128)(2,1)S(1)}, u32[]{:S(2)}, u32[]{:S(2)}) async-start(bf16[4,2,2,2,40,256]{5,4,3,2,1,0:T(8,128)(2,1)} %pad_maximum_fusion), calls=%async_computation | async-start | bytes 1310720 | tf_op jit(solution)/shard_map/all_to_all | solution.py:291
  35.9 3.6 %copy-start.2 = (bf16[1,256,256]{2,1,0:T(8,128)(2,1)S(1)}, bf16[1,256,256]{2,1,0:T(8,128)(2,1)}, u32[]{:S(2)}) copy-start(bf16[1,256,256]{2,1,0:T(8,128)(2,1)} %param.17) | copy-start | bytes 393220
  37.1 2.5 %collective-permute-start.2 = (bf16[2,256,256]{2,1,0:T(8,128)(2,1)S(1)}, bf16[2,256,256]{2,1,0:T(8,128)(2,1)S(1)}, u32[]{:S(2)}, u32[]{:S(2)}) collective-permute-start(bf16[2,256,256]{2,1,0:T(8,128)(2,1)S(1)} %get-tuple-element.66), channel_id=1, source_target_pairs={{0,256},{1,257},{2,258},{3,259},{4,260},{5,261},{6,262},{7,263},{8... | collective-permute-start | bytes 786440 | tf_op jit(solution)/shard_map/ppermute | solution.py:20
  39.6 5.9 %collective-permute-start.3 = (bf16[2,256,256]{2,1,0:T(8,128)(2,1)S(1)}, bf16[2,256,256]{2,1,0:T(8,128)(2,1)S(1)}, u32[]{:S(2)}, u32[]{:S(2)}) collective-permute-start(bf16[2,256,256]{2,1,0:T(8,128)(2,1)S(1)} %get-tuple-element.68), channel_id=1, source_target_pairs={{256,0},{257,1},{258,2},{259,3},{260,4},{261,5},{262,6},{263,7},{2... | collective-permute-start | bytes 786440 | tf_op jit(solution)/shard_map/ppermute | solution.py:20
  60.4 12.2 %collective-permute-start.4 = (bf16[2,2,40,256]{3,2,1,0:T(8,128)(2,1)S(1)}, bf16[2,2,40,256]{3,2,1,0:T(8,128)(2,1)S(1)}, u32[]{:S(2)}, u32[]{:S(2)}) collective-permute-start(bf16[2,2,40,256]{3,2,1,0:T(8,128)(2,1)S(1)} %get-tuple-element.73), channel_id=1, source_target_pairs={{0,4},{1,5},{2,6},{3,7},{4,8},{5,9},{6,10},{7,11},{8,12},{9,13},{1... | collective-permute-start | bytes 245768 | tf_op jit(solution)/shard_map/ppermute | solution.py:404
  64.0 11.1 %collective-permute-start.5 = (bf16[2,2,40,256]{3,2,1,0:T(8,128)(2,1)S(1)}, bf16[2,2,40,256]{3,2,1,0:T(8,128)(2,1)S(1)}, u32[]{:S(2)}, u32[]{:S(2)}) collective-permute-start(bf16[2,2,40,256]{3,2,1,0:T(8,128)(2,1)S(1)} %get-tuple-element.74), channel_id=1, source_target_pairs={{0,8},{1,9},{2,10},{3,11},{4,12},{5,13},{6,14},{7,15},{8,16},{9,17... | collective-permute-start | bytes 245768 | tf_op jit(solution)/shard_map/ppermute | solution.py:404
